TPU v7x, 256 devices: a whole 4x4x8 slice. The times are simulated.
256 devices in a mesh: group: 16 (over x_lo, y, core), tensor: 16 (over z, x_hi).
Axes of the slice: x: 4 (x_hi: 2, x_lo: 2; x = x_hi * 2 + x_lo), y: 4, z: 8, core: 2. Of those that a mesh axis runs over, the one named last changes fastest.
Arguments:
- attention: bfloat16 [6144, 8192], P('group', 'tensor'), may hold values from -6 to 6
- out_weight: bfloat16 [8192, 8192], P('tensor', 'group'), may hold values from -0.0625 to 0.0625
- residual: bfloat16 [6144, 8192], P('group', 'tensor')
- gain: float32 [8192], P('tensor'), may hold values from 0.25 to 1.75
- token_tr: int32 [16, 384], P('group'), may hold values from 0 to 95, never falling along the last dimension, each value on 1 to 8 neighbouring positions
- lag_offsets: int32 [4], replicated, may hold values from 1 to 4, as said below
- responses: bfloat16 [1536, 10240], P(None, 'group'), may hold values from -6 to 6
Outputs:
- cross: float32 [4, 8192, 10240], P(None, 'tensor', 'group')
Inputs may be any that keep to these rules, and one draw needn't show every extreme that they name: `token_tr`: within each group the TR numbers never fall, and every TR of the group holds 1 to 8 tokens. `lag_offsets`: the lags are the numbers 1 to 4 in some order.
All inputs are finite; a program needn't handle non-finite values.
Results may differ from a plain program's by a relative error of at most 0.0038.
Values may be sent and summed in bfloat16 or wider, within the bound.
No kernel may reach another device: no remote copies, remote signals or barrier semaphores. Data moves between devices by JAX's collectives and lax.ppermute only.
A program may use at most 128 MiB of HBM per device.

v0:
```python
import jax
import jax.numpy as jnp
from jax import lax
from jax.sharding import PartitionSpec as P

D = 8192
LAGS = 4
R_DEV = 96


def from_behind(block, axis, distance):
    devices = range(lax.axis_size(axis))
    route = [(i - distance, i) for i in devices if i - distance in devices]
    return lax.ppermute(block, axis, route)


def delayed(extended, lag_offsets, count):
    pieces = []
    for step in range(LAGS):
        start = LAGS - lag_offsets[step]
        pieces.append(lax.dynamic_slice_in_dim(extended, start, count, 0))
    return jnp.concatenate(pieces, axis=1)


def on_device(attention, out_weight, residual, gain, token_tr, lag_offsets, responses):
    partial_sums = jnp.dot(
        attention,
        lax.all_gather(out_weight, "group", axis=1, tiled=True),
        preferred_element_type=jnp.float32,
    )
    summed = lax.psum_scatter(partial_sums, "tensor", scatter_dimension=1, tiled=True)
    hidden = residual.astype(jnp.float32) + summed
    squares = lax.psum(jnp.sum(hidden * hidden, axis=1), "tensor")
    normed = (hidden * lax.rsqrt(squares[:, None] / D + 1e-05) * gain[None, :]).astype(jnp.bfloat16)
    member = jnp.arange(R_DEV, dtype=jnp.int32)[:, None] == token_tr[0][None, :]
    counts = jnp.sum(member.astype(jnp.float32), axis=1, keepdims=True)
    binned = (
        jnp.dot(member.astype(jnp.bfloat16), normed, preferred_element_type=jnp.float32) / counts
    ).astype(jnp.bfloat16)
    width = binned.shape[1]
    total_trs = responses.shape[0]
    contract = (((0,), (0,)), ((), ()))
    tail_rows = binned[R_DEV - LAGS :]
    prior = from_behind(tail_rows, "group", 1)
    lagged = delayed(jnp.concatenate([prior, binned], axis=0), lag_offsets, R_DEV)
    accumulated = lax.dot_general(
        lax.all_gather(lagged, "group", axis=0, tiled=True),
        responses,
        contract,
        preferred_element_type=jnp.float32,
    )
    scaled = accumulated * (1.0 / jnp.sqrt(jnp.float32(total_trs)))
    return scaled.reshape(LAGS, width, responses.shape[1])


def solution(mesh):
    return jax.shard_map(
        on_device,
        mesh=mesh,
        in_specs=(
            P("group", "tensor"),
            P("tensor", "group"),
            P("group", "tensor"),
            P("tensor"),
            P("group", None),
            P(),
            P(None, "group"),
        ),
        out_specs=P(None, "tensor", "group"),
        check_vma=False,
    )
```

profile of v0, /device:TPU:1, one launch (start us, length us, event | category | flops | bytes accessed | tf_op | source)
XLA Modules:
  0.0 438.3 jit_solution(9444380534327662025)
XLA Ops:
  6.5 0.0 copy-start
  6.5 0.0 all-gather.3.cloned.1.call-start
  6.5 0.7 all-gather.3.cloned.1.call-update
  7.3 0.0 reduce-scatter.2.cloned.1.call-start
  7.3 60.7 %all-gather.3.cloned.1.call-done = bf16[512,8192]{1,0:T(8,128)(2,1)} async-done(((bf16[512,512]{1,0:T(8,128)(2,1)}), bf16[512,8192]{1,0:T(8,128)(2,1)}) %all-gather.3.cloned.1.call-update) | async-done | bytes 8388624 | tf_op jit(solution)/shard_map/all_gather | solution.py:28
  68.0 11.5 %fusion.9 = f32[384,8192]{1,0:T(8,128)} fusion(bf16[384,512]{1,0:T(8,128)(2,1)} %param.7, bf16[512,8192]{1,0:T(8,128)(2,1)} %all-gather.3.cloned.1.call-done), kind=kOutput, calls=%fused_computation.22 | convolution fusion | flops 3221225472 | bytes 21364736 | tf_op jit(solution)/shard_map/dot_general | solution.py:26
  79.5 0.0 reduce-scatter.2.cloned.1.call-update
  79.5 0.0 all-gather.5.cloned.1.call-start
  79.6 0.6 copy-done.3
  80.2 0.1 convert_reduce_fusion
  80.3 245.0 %reduce-scatter.2.cloned.1.call-done = f32[384,512]{1,0:T(8,128)} async-done(((f32[384,8192]{1,0:T(8,128)}), f32[384,512]{1,0:T(8,128)}) %reduce-scatter.2.cloned.1.call-update) | async-done | bytes 786448 | tf_op jit(solution)/shard_map/reduce_scatter | solution.py:31
  325.3 0.0 copy-done.1
  325.3 1.3 multiply_reduce_fusion
  326.6 31.3 %psum.7 = f32[384]{0:T(512)S(1)} all-reduce(f32[384]{0:T(512)S(1)} %multiply_reduce_fusion), channel_id=1, replica_groups=mesh['group'=16,'tensor'=16] {'tensor'}, use_global_device_ids=true, to_apply=%region_2.0 | all-reduce | flops 384 | bytes 3072 | tf_op jit(solution)/shard_map/psum | solution.py:33
  357.9 1.5 fusion
  359.3 14.5 %collective-permute-start = (bf16[4,512]{1,0:T(4,128)(2,1)S(1)}, bf16[4,512]{1,0:T(4,128)(2,1)S(1)}, u32[]{:S(2)}, u32[]{:S(2)}) collective-permute-start(bf16[4,512]{1,0:T(4,128)(2,1)S(1)} %slice.20), channel_id=1, source_target_pairs={{0,16},{16,32},{32,48},{48,64},{64,80},{80,96},{96,112},{112,128},... | collective-permute-start | bytes 12296 | tf_op jit(solution)/shard_map/ppermute | solution.py:14
  373.8 0.0 copy-done.2
  373.8 0.6 fusion.8
  379.2 0.0 collective-permute-done
  379.2 0.1 fusion.4
  379.4 0.8 pad_maximum_fusion
  380.2 0.0 all-gather.5.cloned.1.call-update
  380.2 42.8 %all-gather.5.cloned.1.call-done = bf16[1536,2048]{1,0:T(8,128)(2,1)} async-done(((bf16[96,2048]{1,0:T(8,128)(2,1)}), bf16[1536,2048]{1,0:T(8,128)(2,1)}) %all-gather.5.cloned.1.call-update) | async-done | bytes 6291472 | tf_op jit(solution)/shard_map/all_gather | solution.py:47
  423.0 8.7 %convolution_multiply_fusion = f32[2048,640]{1,0:T(8,128)} fusion(bf16[1536,2048]{1,0:T(8,128)(2,1)} %all-gather.5.cloned.1.call-done, bf16[1536,640]{1,0:T(8,128)(2,1)S(1)} %copy-done), kind=kOutput, calls=%fused_computation | convolution fusion | flops 4027842560 | bytes 13500416 | tf_op jit(solution)/shard_map/dot_general | solution.py:46
  (9 shorter events, 0.0 us)
Async XLA Ops:
  6.5 416.5 %copy-start = (bf16[1536,640]{1,0:T(8,128)(2,1)S(1)}, bf16[1536,640]{1,0:T(8,128)(2,1)}, u32[]{:S(2)}) copy-start(bf16[1536,640]{1,0:T(8,128)(2,1)} %param.13) | copy-start | bytes 5898244
  6.5 61.4 %all-gather.3.cloned.1.call-start = ((), (), s32[]{:S(2)}) async-start(), calls=%async_computation.1 | async-start | bytes 8912896 | tf_op jit(solution)/shard_map/all_gather | solution.py:28
  7.3 318.0 %reduce-scatter.2.cloned.1.call-start = ((), (), s32[]{:S(2)}) async-start(), calls=%async_computation.2 | async-start | bytes 13369344 | tf_op jit(solution)/shard_map/reduce_scatter | solution.py:31
  79.5 0.7 copy-start.3
  79.5 245.8 %copy-start.1 = (bf16[384,512]{1,0:T(8,128)(2,1)S(1)}, bf16[384,512]{1,0:T(8,128)(2,1)}, u32[]{:S(2)}) copy-start(bf16[384,512]{1,0:T(8,128)(2,1)} %param.9) | copy-start | bytes 1179652
  79.5 278.4 %copy-start.4 = (f32[512]{0:T(512)S(1)}, f32[512]{0:T(512)}, u32[]{:S(2)}) copy-start(f32[512]{0:T(512)} %param.10) | copy-start | bytes 6148
  79.5 294.4 %copy-start.2 = (s32[4]{0:T(128)S(1)}, s32[4]{0:T(128)}, u32[]{:S(2)}) copy-start(s32[4]{0:T(128)} %param.12) | copy-start | bytes 52
  79.5 343.5 %all-gather.5.cloned.1.call-start = ((), (), s32[]{:S(2)}) async-start(), calls=%async_computation.3 | async-start | bytes 6684672 | tf_op jit(solution)/shard_map/all_gather | solution.py:47
  359.3 19.9 %collective-permute-start = (bf16[4,512]{1,0:T(4,128)(2,1)S(1)}, bf16[4,512]{1,0:T(4,128)(2,1)S(1)}, u32[]{:S(2)}, u32[]{:S(2)}) collective-permute-start(bf16[4,512]{1,0:T(4,128)(2,1)S(1)} %slice.20), channel_id=1, source_target_pairs={{0,16},{16,32},{32,48},{48,64},{64,80},{80,96},{96,112},{112,128},... | collective-permute-start | bytes 12296 | tf_op jit(solution)/shard_map/ppermute | solution.py:14
Sparse Core Ops, SparseCore 0:
  9.1 58.7 all-gather.2
  79.6 245.5 reduce-scatter.1
  380.3 42.6 all-gather.4
where the time goes:
time: 439 us; the launch traced here: 438 us
  waiting for transfers between devices  349 us (79%)
  blocking collectives  31.3 us (7%)
  matrix products  21.7 us (5%)
  between operations  17.9 us (4%)
  starting transfers between devices  14.6 us (3%)
    reduce_scatter x1, waiting for transfers between devices, on_device(): lax.psum_scatter(partial_sums, 'tensor', scatter_dimension=1, tiled=True)  245 us
    all_gather x1, waiting for transfers between devices, on_device(): lax.all_gather(out_weight, 'group', axis=1, tiled=True)  60.7 us
    all_gather x1, waiting for transfers between devices, on_device(): lax.all_gather(lagged, 'group', axis=0, tiled=True)  42.8 us
    psum x1, blocking collectives, on_device(): squares = lax.psum(jnp.sum(hidden * hidden, axis=1), 'tensor')  31.3 us
    ppermute x1, starting transfers between devices, from_behind(): return lax.ppermute(block, axis, route)  14.5 us
    dot_general x1, matrix products, on_device(): jnp.dot(attention, lax.all_gather(out_weight, 'group', axis=1, tiled=True...  11.5 us
  transfers between devices with their start and end apart: 4, of which 3 were waited for; matrix products, arithmetic and copies ran while one was open for 0% of the time, Pallas kernels for 0%

commit v1 on v0

v1 whole, which is shorter than its diff:
```python
import jax
import jax.numpy as jnp
from jax import lax
from jax.sharding import PartitionSpec as P

D = 8192
LAGS = 4
R_DEV = 96


def transposed_block(block):
    groups = lax.axis_size("group")
    tensors = lax.axis_size("tensor")
    route = [(t * tensors + g, g * tensors + t) for g in range(groups) for t in range(tensors)]
    return lax.ppermute(block, ("group", "tensor"), route)


def on_device(attention, out_weight, residual, gain, token_tr, lag_offsets, responses):
    weight_cols = lax.all_gather(transposed_block(out_weight), "group", axis=0, tiled=True)
    rows = lax.all_gather(attention, "tensor", axis=1, tiled=True)
    summed = jnp.dot(rows, weight_cols, preferred_element_type=jnp.float32)
    hidden = residual.astype(jnp.float32) + summed
    squares = lax.psum(jnp.sum(hidden * hidden, axis=1), "tensor")
    normed = (hidden * lax.rsqrt(squares[:, None] / D + 1e-05) * gain[None, :]).astype(jnp.bfloat16)
    member = jnp.arange(R_DEV, dtype=jnp.int32)[:, None] == token_tr[0][None, :]
    counts = jnp.sum(member.astype(jnp.float32), axis=1, keepdims=True)
    binned = (
        jnp.dot(member.astype(jnp.bfloat16), normed, preferred_element_type=jnp.float32) / counts
    ).astype(jnp.bfloat16)
    width = binned.shape[1]
    total_trs = responses.shape[0]
    story = lax.all_gather(binned, "group", axis=0, tiled=True)
    extended = jnp.concatenate([jnp.zeros((LAGS, width), story.dtype), story], axis=0)
    pieces = []
    for step in range(LAGS):
        start = LAGS - lag_offsets[step]
        pieces.append(lax.dynamic_slice_in_dim(extended, start, total_trs, 0))
    lagged = jnp.concatenate(pieces, axis=1)
    contract = (((0,), (0,)), ((), ()))
    accumulated = lax.dot_general(lagged, responses, contract, preferred_element_type=jnp.float32)
    scaled = accumulated * (1.0 / jnp.sqrt(jnp.float32(total_trs)))
    return scaled.reshape(LAGS, width, responses.shape[1])


def solution(mesh):
    return jax.shard_map(
        on_device,
        mesh=mesh,
        in_specs=(
            P("group", "tensor"),
            P("tensor", "group"),
            P("group", "tensor"),
            P("tensor"),
            P("group", None),
            P(),
            P(None, "group"),
        ),
        out_specs=P(None, "tensor", "group"),
        check_vma=False,
    )
```

time: 439 us -> 327 us (0.74)
  waiting for transfers between devices: 349 us -> 243 us
  starting transfers between devices: 14.6 us -> 6.11 us
  local copies, waits for them, and re-layouts: 1.22 us -> 6.39 us
    reduce_scatter x1 -> x0, waiting for transfers between devices: 245 us -> none  [on_device(): lax.psum_scatter(partial_sums, 'tensor', scatter_dimension=1, tiled=True)]
    all_gather x2 -> x3, waiting for transfers between devices: 103 us -> 195 us  [the longest x1 104 us: on_device(): rows = lax.all_gather(attention, 'tensor', axis=1, tiled=True)]
    ppermute x1, waiting for transfers between devices: 0.01 us -> 46.8 us  [transposed_block(): return lax.ppermute(block, ('group', 'tensor'), route)]
    ppermute x1, starting transfers between devices: 14.5 us -> 6.03 us  [transposed_block(): return lax.ppermute(block, ('group', 'tensor'), route)]
    dynamic_slice x0 -> x1, local copies, waits for them, and re-layouts: none -> 4.93 us  [on_device(): pieces.append(lax.dynamic_slice_in_dim(extended, start, total_trs, 0))]
  transfers between devices with their start and end apart: 4 -> 4, of which waited for: 3 -> 4; matrix products, arithmetic and copies ran while one was open for 0% -> 0% of each run, Pallas kernels for 0% -> 0%
where the time goes in v1:
time: 327 us
  waiting for transfers between devices  243 us (74%)
  blocking collectives  35.1 us (11%)
  between operations  18.1 us (6%)
  matrix products  17.5 us (5%)
  local copies, waits for them, and re-layouts  6.39 us (2%)
  starting transfers between devices  6.11 us (2%)
    all_gather x1, waiting for transfers between devices, on_device(): rows = lax.all_gather(attention, 'tensor', axis=1, tiled=True)  104 us
    all_gather x1, waiting for transfers between devices, on_device(): lax.all_gather(transposed_block(out_weight), 'group', axis=0, tiled=True)  57.3 us
    ppermute x1, waiting for transfers between devices, transposed_block(): return lax.ppermute(block, ('group', 'tensor'), route)  46.8 us
    psum x1, blocking collectives, on_device(): squares = lax.psum(jnp.sum(hidden * hidden, axis=1), 'tensor')  35.1 us
    all_gather x1, waiting for transfers between devices, on_device(): story = lax.all_gather(binned, 'group', axis=0, tiled=True)  33.8 us
    dot_general x1, matrix products, on_device(): summed = jnp.dot(rows, weight_cols, preferred_element_type=jnp.float32)  8.66 us
    dot_general x1, matrix products, on_device(): lax.dot_general(lagged, responses, contract, preferred_element_type=jnp.f...  7.88 us
  transfers between devices with their start and end apart: 4, of which 4 were waited for; matrix products, arithmetic and copies ran while one was open for 0% of the time, Pallas kernels for 0%

profile of v1, /device:TPU:1, one launch (start us, length us, event | category | flops | bytes accessed | tf_op | source)
XLA Modules:
  0.0 327.0 jit_solution(6463654039219583115)
XLA Ops:
  6.5 0.0 copy-start
  6.5 0.0 all-gather.4.cloned.1.call-start
  6.5 0.7 all-gather.4.cloned.1.call-update
  7.3 0.0 all-gather.6.cloned.1.call-start
  7.3 6.0 %collective-permute-start = (bf16[512,512]{1,0:T(8,128)(2,1)}, bf16[512,512]{1,0:T(8,128)(2,1)S(1)}, u32[]{:S(2)}, u32[]{:S(2)}) collective-permute-start(bf16[512,512]{1,0:T(8,128)(2,1)} %param.8), channel_id=1, source_target_pairs={{0,0},{16,1},{32,2},{48,3},{64,4},{80,5},{96,6},{112,7},{128,8},{1... | collective-permute-start | bytes 1572872 | tf_op jit(solution)/shard_map/ppermute | solution.py:15
  13.3 46.8 %collective-permute-done = bf16[512,512]{1,0:T(8,128)(2,1)S(1)} collective-permute-done((bf16[512,512]{1,0:T(8,128)(2,1)}, bf16[512,512]{1,0:T(8,128)(2,1)S(1)}, u32[]{:S(2)}, u32[]{:S(2)}) %collective-permute-start) | collective-permute-done | bytes 524320 | tf_op jit(solution)/shard_map/ppermute | solution.py:15
  60.1 0.8 copy-done.1
  60.9 0.0 all-gather.6.cloned.1.call-update
  60.9 0.0 all-gather.8.cloned.1.call-start
  61.0 0.7 reduce
  61.7 0.1 convert_reduce_fusion
  61.8 0.0 copy-start.3
  61.8 0.0 copy-start.2
  61.8 104.3 %all-gather.4.cloned.1.call-done = bf16[384,8192]{1,0:T(8,128)(2,1)} async-done(((bf16[384,512]{1,0:T(8,128)(2,1)}), bf16[384,8192]{1,0:T(8,128)(2,1)}) %all-gather.4.cloned.1.call-update) | async-done | bytes 6291472 | tf_op jit(solution)/shard_map/all_gather | solution.py:20
  166.1 57.3 %all-gather.6.cloned.1.call-done = bf16[8192,512]{1,0:T(8,128)(2,1)} async-done(((bf16[512,512]{1,0:T(8,128)(2,1)}), bf16[8192,512]{1,0:T(8,128)(2,1)}) %all-gather.6.cloned.1.call-update) | async-done | bytes 8388624 | tf_op jit(solution)/shard_map/all_gather | solution.py:19
  223.5 8.7 %multiply_reduce_fusion = (f32[384]{0:T(512)S(1)}, f32[384,512]{1,0:T(8,128)S(1)}) fusion(bf16[384,8192]{1,0:T(8,128)(2,1)} %all-gather.4.cloned.1.call-done, bf16[8192,512]{1,0:T(8,128)(2,1)} %all-gather.6.cloned.1.call-done, bf16[384,512]{1,0:T(8,128)(2,1)} %param.9), kind=kOutput, calls=%fused_computation.17 | convolution fusion | flops 3222011392 | bytes 15861248 | tf_op jit(solution)/shard_map/dot_general | solution.py:21
  232.1 35.1 %psum.7 = f32[384]{0:T(512)S(1)} all-reduce(f32[384]{0:T(512)S(1)} %get-tuple-element.13), channel_id=1, replica_groups=mesh['group'=16,'tensor'=16] {'tensor'}, use_global_device_ids=true, to_apply=%region_1.0 | all-reduce | flops 384 | bytes 3072 | tf_op jit(solution)/shard_map/psum | solution.py:23
  267.2 0.0 copy-done.3
  267.2 0.9 fusion.11
  268.2 0.0 all-gather.8.cloned.1.call-update
  268.2 0.7 fusion.16
  273.9 33.8 %all-gather.8.cloned.1.call-done = bf16[1536,512]{1,0:T(8,128)(2,1)} async-done(((bf16[96,512]{1,0:T(8,128)(2,1)}), bf16[1536,512]{1,0:T(8,128)(2,1)}) %all-gather.8.cloned.1.call-update) | async-done | bytes 1572880 | tf_op jit(solution)/shard_map/all_gather | solution.py:32
  307.6 4.9 %pad_dynamic-slice_fusion.3 = (bf16[1536,512]{1,0:T(8,128)(2,1)S(1)}, bf16[1536,512]{1,0:T(8,128)(2,1)S(1)}, bf16[1536,512]{1,0:T(8,128)(2,1)S(1)}, bf16[1536,512]{1,0:T(8,128)(2,1)S(1)}) fusion(s32[]{:T(128)S(6)} %select_n.12, bf16[1536,512]{1,0:T(8,128)(2,1)} %all-gather.8.cloned.1.call-done, s32[]{:T(128)S(6)} %select_n.13, s32[]{:T(128)S(6)} %select_n.14, ...), kind=kLoop, calls=%fused_computation.15 | loop fusion | bytes 7864336 | tf_op jit(solution)/shard_map/dynamic_slice | solution.py:37
  312.6 7.9 %fusion.8 = f32[2048,640]{1,0:T(8,128)} fusion(bf16[1536,640]{1,0:T(8,128)(2,1)S(1)} %copy-done, bf16[1536,512]{1,0:T(8,128)(2,1)S(1)} %get-tuple-element.8, bf16[1536,512]{1,0:T(8,128)(2,1)S(1)} %get-tuple-element.7, bf16[1536,512]{1,0:T(8,128)(2,1)S(1)} %get-tuple-element.6, bf16[1536,512]{1,0:T(8,128)(2,1)S(1)} %get-tuple-element.5), kind=kOutput, calls=%fused_computation.8 | convolution fusion | flops 4053008384 | bytes 13500416 | tf_op jit(solution)/shard_map/dot_general | solution.py:40
  (4 shorter events, 0.0 us)
Async XLA Ops:
  6.5 306.0 %copy-start = (bf16[1536,640]{1,0:T(8,128)(2,1)S(1)}, bf16[1536,640]{1,0:T(8,128)(2,1)}, u32[]{:S(2)}) copy-start(bf16[1536,640]{1,0:T(8,128)(2,1)} %param.13) | copy-start | bytes 5898244
  6.5 159.6 %all-gather.4.cloned.1.call-start = ((), (), s32[]{:S(2)}) async-start(), calls=%async_computation | async-start | bytes 6684672 | tf_op jit(solution)/shard_map/all_gather | solution.py:20
  7.3 216.2 %all-gather.6.cloned.1.call-start = ((), (), s32[]{:S(2)}) async-start(), calls=%async_computation.1 | async-start | bytes 8912896 | tf_op jit(solution)/shard_map/all_gather | solution.py:19
  7.3 52.8 %collective-permute-start = (bf16[512,512]{1,0:T(8,128)(2,1)}, bf16[512,512]{1,0:T(8,128)(2,1)S(1)}, u32[]{:S(2)}, u32[]{:S(2)}) collective-permute-start(bf16[512,512]{1,0:T(8,128)(2,1)} %param.8), channel_id=1, source_target_pairs={{0,0},{16,1},{32,2},{48,3},{64,4},{80,5},{96,6},{112,7},{128,8},{1... | collective-permute-start | bytes 1572872 | tf_op jit(solution)/shard_map/ppermute | solution.py:15
  60.1 0.8 copy-start.1
  60.9 246.7 %all-gather.8.cloned.1.call-start = ((), (), s32[]{:S(2)}) async-start(), calls=%async_computation.2 | async-start | bytes 1671168 | tf_op jit(solution)/shard_map/all_gather | solution.py:32
  61.8 205.4 %copy-start.3 = (f32[512]{0:T(512)S(1)}, f32[512]{0:T(512)}, u32[]{:S(2)}) copy-start(f32[512]{0:T(512)} %param.10) | copy-start | bytes 6148
  61.8 206.4 %copy-start.2 = (s32[4]{0:T(128)S(1)}, s32[4]{0:T(128)}, u32[]{:S(2)}) copy-start(s32[4]{0:T(128)} %param.12) | copy-start | bytes 52
Sparse Core Ops, SparseCore 0:
  9.8 156.2 all-gather.3
  168.0 55.4 all-gather.5
  268.3 39.2 all-gather.7

commit v2 on v1

--- a/solution.py
+++ b/solution.py
@@ -15,12 +15,29 @@
     return lax.ppermute(block, ("group", "tensor"), route)
 
 
+def shifted(block, axis, shift):
+    n = lax.axis_size(axis)
+    return lax.ppermute(block, axis, [(i, (i + shift) % n) for i in range(n)])
+
+
+def gathered_by_shift(block, axis):
+    n = lax.axis_size(axis)
+    return [block] + [shifted(block, axis, k) for k in range(1, n)]
+
+
 def on_device(attention, out_weight, residual, gain, token_tr, lag_offsets, responses):
+    tensors = lax.axis_size("tensor")
+    own = lax.axis_index("tensor")
+    heads = attention.shape[1]
     weight_cols = lax.all_gather(transposed_block(out_weight), "group", axis=0, tiled=True)
-    rows = lax.all_gather(attention, "tensor", axis=1, tiled=True)
-    summed = jnp.dot(rows, weight_cols, preferred_element_type=jnp.float32)
+    rows = jnp.concatenate(gathered_by_shift(attention, "tensor"), axis=1)
+    flipped = weight_cols.reshape(tensors, heads, -1)[::-1]
+    doubled = jnp.concatenate([flipped, flipped], axis=0)
+    reordered = lax.dynamic_slice_in_dim(doubled, tensors - 1 - own, tensors, 0)
+    summed = jnp.dot(rows, reordered.reshape(tensors * heads, -1), preferred_element_type=jnp.float32)
     hidden = residual.astype(jnp.float32) + summed
-    squares = lax.psum(jnp.sum(hidden * hidden, axis=1), "tensor")
+    partial = jnp.sum(hidden * hidden, axis=1)
+    squares = sum(gathered_by_shift(partial, "tensor"))
     normed = (hidden * lax.rsqrt(squares[:, None] / D + 1e-05) * gain[None, :]).astype(jnp.bfloat16)
     member = jnp.arange(R_DEV, dtype=jnp.int32)[:, None] == token_tr[0][None, :]
     counts = jnp.sum(member.astype(jnp.float32), axis=1, keepdims=True)

time: 327 us -> 395 us (1.21)
  starting transfers between devices: 6.11 us -> 142 us
  waiting for transfers between devices: 243 us -> 184 us
  blocking collectives: 35.1 us -> 0 us
  local copies, waits for them, and re-layouts: 6.39 us -> 31 us
  other arithmetic: 0.82 us -> 6.45 us
  matrix products: 17.5 us -> 12.3 us
    ppermute x0 -> x30, starting transfers between devices: none -> 136 us  [shifted(): return lax.ppermute(block, axis, [(i, (i + shift) % n) for i in range(n)])]
    all_gather x1 -> x0, waiting for transfers between devices: 104 us -> none  [on_device(): rows = lax.all_gather(attention, 'tensor', axis=1, tiled=True)]
    ppermute x0 -> x30, waiting for transfers between devices: none -> 96.5 us  [shifted(): return lax.ppermute(block, axis, [(i, (i + shift) % n) for i in range(n)])]
    all_gather x1, waiting for transfers between devices: 57.3 us -> 0.01 us  [on_device(): lax.all_gather(transposed_block(out_weight), 'group', axis=0, tiled=True)]
    psum x1 -> x0, blocking collectives: 35.1 us -> none  [on_device(): squares = lax.psum(jnp.sum(hidden * hidden, axis=1), 'tensor')]
    unnamed x8 -> x31, local copies, waits for them, and re-layouts: 0.81 us -> 17.4 us
    all_gather x1, waiting for transfers between devices: 33.8 us -> 45.2 us  [on_device(): story = lax.all_gather(binned, 'group', axis=0, tiled=True)]
    rev x0 -> x1, local copies, waits for them, and re-layouts: none -> 7.37 us  [on_device(): flipped = weight_cols.reshape(tensors, heads, -1)[::-1]]
  transfers between devices with their start and end apart: 4 -> 33, of which waited for: 4 -> 11; matrix products, arithmetic and copies ran while one was open for 0% -> 5% of each run, Pallas kernels for 0% -> 0%
where the time goes in v2:
time: 395 us
  waiting for transfers between devices  184 us (47%)
  starting transfers between devices  142 us (36%)
  local copies, waits for them, and re-layouts  31 us (8%)
  between operations  18.6 us (5%)
  matrix products  12.3 us (3%)
  other arithmetic  6.45 us (2%)
    ppermute x30, starting transfers between devices, shifted(): return lax.ppermute(block, axis, [(i, (i + shift) % n) for i in range(n)])  136 us
    ppermute x30, waiting for transfers between devices, shifted(): return lax.ppermute(block, axis, [(i, (i + shift) % n) for i in range(n)])  96.5 us
    all_gather x1, waiting for transfers between devices, on_device(): story = lax.all_gather(binned, 'group', axis=0, tiled=True)  45.2 us
    ppermute x1, waiting for transfers between devices, transposed_block(): return lax.ppermute(block, ('group', 'tensor'), route)  42.5 us
    unnamed x31, local copies, waits for them, and re-layouts  17.4 us
  transfers between devices with their start and end apart: 33, of which 11 were waited for; matrix products, arithmetic and copies ran while one was open for 5% of the time, Pallas kernels for 0%

profile of v2, /device:TPU:1, one launch (start us, length us, event | category | flops | bytes accessed | tf_op | source)
XLA Modules:
  0.0 394.7 jit_solution(8770877382894269355)
XLA Ops:
  6.5 6.1 %collective-permute-start.15 = (bf16[512,512]{1,0:T(8,128)(2,1)}, bf16[512,512]{1,0:T(8,128)(2,1)S(1)}, u32[]{:S(2)}, u32[]{:S(2)}) collective-permute-start(bf16[512,512]{1,0:T(8,128)(2,1)} %param.8), channel_id=1, source_target_pairs={{0,0},{16,1},{32,2},{48,3},{64,4},{80,5},{96,6},{112,7},{128,8},{1... | collective-permute-start | bytes 1572872 | tf_op jit(solution)/shard_map/ppermute | solution.py:15
  12.7 42.5 %collective-permute-done.15 = bf16[512,512]{1,0:T(8,128)(2,1)S(1)} collective-permute-done((bf16[512,512]{1,0:T(8,128)(2,1)}, bf16[512,512]{1,0:T(8,128)(2,1)S(1)}, u32[]{:S(2)}, u32[]{:S(2)}) %collective-permute-start.15) | collective-permute-done | bytes 524320 | tf_op jit(solution)/shard_map/ppermute | solution.py:15
  56.1 7.0 %collective-permute-start.1 = (bf16[384,512]{1,0:T(8,128)(2,1)}, bf16[384,512]{1,0:T(8,128)(2,1)}, u32[]{:S(2)}, u32[]{:S(2)}) collective-permute-start(bf16[384,512]{1,0:T(8,128)(2,1)} %param.7), channel_id=1, source_target_pairs={{0,2},{1,3},{2,4},{3,5},{4,6},{5,7},{6,8},{7,9},{8,10},{9,11},{10,... | collective-permute-start | bytes 1179656 | tf_op jit(solution)/shard_map/ppermute | solution.py:20
  63.1 7.9 %collective-permute-start.2 = (bf16[384,512]{1,0:T(8,128)(2,1)}, bf16[384,512]{1,0:T(8,128)(2,1)}, u32[]{:S(2)}, u32[]{:S(2)}) collective-permute-start(bf16[384,512]{1,0:T(8,128)(2,1)} %param.7), channel_id=1, source_target_pairs={{0,3},{1,4},{2,5},{3,6},{4,7},{5,8},{6,9},{7,10},{8,11},{9,12},{10... | collective-permute-start | bytes 1179656 | tf_op jit(solution)/shard_map/ppermute | solution.py:20
  71.0 5.8 %collective-permute-start.4 = (bf16[384,512]{1,0:T(8,128)(2,1)}, bf16[384,512]{1,0:T(8,128)(2,1)S(1)}, u32[]{:S(2)}, u32[]{:S(2)}) collective-permute-start(bf16[384,512]{1,0:T(8,128)(2,1)} %param.7), channel_id=1, source_target_pairs={{0,5},{1,6},{2,7},{3,8},{4,9},{5,10},{6,11},{7,12},{8,13},{9,14},{... | collective-permute-start | bytes 1179656 | tf_op jit(solution)/shard_map/ppermute | solution.py:20
  81.0 6.5 %collective-permute-start.6 = (bf16[384,512]{1,0:T(8,128)(2,1)}, bf16[384,512]{1,0:T(8,128)(2,1)S(1)}, u32[]{:S(2)}, u32[]{:S(2)}) collective-permute-start(bf16[384,512]{1,0:T(8,128)(2,1)} %param.7), channel_id=1, source_target_pairs={{0,7},{1,8},{2,9},{3,10},{4,11},{5,12},{6,13},{7,14},{8,15},{9,0},... | collective-permute-start | bytes 1179656 | tf_op jit(solution)/shard_map/ppermute | solution.py:20
  89.4 26.2 %collective-permute-done.2 = bf16[384,512]{1,0:T(8,128)(2,1)} collective-permute-done((bf16[384,512]{1,0:T(8,128)(2,1)}, bf16[384,512]{1,0:T(8,128)(2,1)}, u32[]{:S(2)}, u32[]{:S(2)}) %collective-permute-start.2) | collective-permute-done | bytes 393248 | tf_op jit(solution)/shard_map/ppermute | solution.py:20
  117.5 15.7 %collective-permute-start.8 = (bf16[384,512]{1,0:T(8,128)(2,1)}, bf16[384,512]{1,0:T(8,128)(2,1)S(1)}, u32[]{:S(2)}, u32[]{:S(2)}) collective-permute-start(bf16[384,512]{1,0:T(8,128)(2,1)} %param.7), channel_id=1, source_target_pairs={{0,9},{1,10},{2,11},{3,12},{4,13},{5,14},{6,15},{7,0},{8,1},{9,2},... | collective-permute-start | bytes 1179656 | tf_op jit(solution)/shard_map/ppermute | solution.py:20
  134.0 27.5 %collective-permute-done.4 = bf16[384,512]{1,0:T(8,128)(2,1)S(1)} collective-permute-done((bf16[384,512]{1,0:T(8,128)(2,1)}, bf16[384,512]{1,0:T(8,128)(2,1)S(1)}, u32[]{:S(2)}, u32[]{:S(2)}) %collective-permute-start.4) | collective-permute-done | bytes 393248 | tf_op jit(solution)/shard_map/ppermute | solution.py:20
  162.4 28.4 %collective-permute-start.10 = (bf16[384,512]{1,0:T(8,128)(2,1)}, bf16[384,512]{1,0:T(8,128)(2,1)S(1)}, u32[]{:S(2)}, u32[]{:S(2)}) collective-permute-start(bf16[384,512]{1,0:T(8,128)(2,1)} %param.7), channel_id=1, source_target_pairs={{0,11},{1,12},{2,13},{3,14},{4,15},{5,0},{6,1},{7,2},{8,3},{9,4},{... | collective-permute-start | bytes 1179656 | tf_op jit(solution)/shard_map/ppermute | solution.py:20
  192.5 18.9 %collective-permute-start.12 = (bf16[384,512]{1,0:T(8,128)(2,1)S(1)}, bf16[384,512]{1,0:T(8,128)(2,1)S(1)}, u32[]{:S(2)}, u32[]{:S(2)}) collective-permute-start(bf16[384,512]{1,0:T(8,128)(2,1)S(1)} %copy-done.2), channel_id=1, source_target_pairs={{0,13},{1,14},{2,15},{3,0},{4,1},{5,2},{6,3},{7,4},{8,5},{9,6},{10... | collective-permute-start | bytes 1179656 | tf_op jit(solution)/shard_map/ppermute | solution.py:20
  214.9 10.6 %collective-permute-done.11 = bf16[384,512]{1,0:T(8,128)(2,1)S(1)} collective-permute-done((bf16[384,512]{1,0:T(8,128)(2,1)}, bf16[384,512]{1,0:T(8,128)(2,1)S(1)}, u32[]{:S(2)}, u32[]{:S(2)}) %collective-permute-start.11) | collective-permute-done | bytes 393248 | tf_op jit(solution)/shard_map/ppermute | solution.py:20
  226.3 6.5 %collective-permute-done.12 = bf16[384,512]{1,0:T(8,128)(2,1)S(1)} collective-permute-done((bf16[384,512]{1,0:T(8,128)(2,1)S(1)}, bf16[384,512]{1,0:T(8,128)(2,1)S(1)}, u32[]{:S(2)}, u32[]{:S(2)}) %collective-permute-start.12) | collective-permute-done | bytes 393248 | tf_op jit(solution)/shard_map/ppermute | solution.py:20
  233.7 21.8 %collective-permute-done.13 = bf16[384,512]{1,0:T(8,128)(2,1)S(1)} collective-permute-done((bf16[384,512]{1,0:T(8,128)(2,1)S(1)}, bf16[384,512]{1,0:T(8,128)(2,1)S(1)}, u32[]{:S(2)}, u32[]{:S(2)}) %collective-permute-start.13) | collective-permute-done | bytes 393248 | tf_op jit(solution)/shard_map/ppermute | solution.py:20
  257.1 7.4 %rev.3 = bf16[16,512,512]{2,1,0:T(8,128)(2,1)} reverse(bf16[16,512,512]{2,1,0:T(8,128)(2,1)} %bitcast.15), dimensions={0} | reverse | bytes 16777216 | tf_op jit(solution)/shard_map/rev | solution.py:34
  264.5 6.3 %fusion = bf16[16,512,512]{2,1,0:T(8,128)(2,1)S(1)} fusion(s32[]{:T(128)S(6)} %select_n.15, bf16[16,512,512]{2,1,0:T(8,128)(2,1)} %rev.3), kind=kLoop, calls=%fused_computation.2 | loop fusion | flops 4194304 | bytes 16777220 | tf_op jit(solution)/shard_map/concatenate | solution.py:35
  274.4 9.5 %collective-permute-start.16 = (f32[384]{0:T(512)S(1)}, f32[384]{0:T(512)S(1)}, u32[]{:S(2)}, u32[]{:S(2)}) collective-permute-start(f32[384]{0:T(512)S(1)} %get-tuple-element.13), channel_id=1, source_target_pairs={{0,1},{1,2},{2,3},{3,4},{4,5},{5,6},{6,7},{7,8},{8,9},{9,10},{10,1... | collective-permute-start | bytes 4616 | tf_op jit(solution)/shard_map/ppermute | solution.py:20
  283.9 4.9 %collective-permute-start.17 = (f32[384]{0:T(512)S(1)}, f32[384]{0:T(512)S(1)}, u32[]{:S(2)}, u32[]{:S(2)}) collective-permute-start(f32[384]{0:T(512)S(1)} %get-tuple-element.13), channel_id=1, source_target_pairs={{0,2},{1,3},{2,4},{3,5},{4,6},{5,7},{6,8},{7,9},{8,10},{9,11},{10,... | collective-permute-start | bytes 4616 | tf_op jit(solution)/shard_map/ppermute | solution.py:20
  288.9 8.4 %collective-permute-start.20 = (f32[384]{0:T(512)S(1)}, f32[384]{0:T(512)S(1)}, u32[]{:S(2)}, u32[]{:S(2)}) collective-permute-start(f32[384]{0:T(512)S(1)} %get-tuple-element.13), channel_id=1, source_target_pairs={{0,5},{1,6},{2,7},{3,8},{4,9},{5,10},{6,11},{7,12},{8,13},{9,14},{... | collective-permute-start | bytes 4616 | tf_op jit(solution)/shard_map/ppermute | solution.py:20
  298.3 4.8 %collective-permute-start.23 = (f32[384]{0:T(512)S(1)}, f32[384]{0:T(512)S(1)}, u32[]{:S(2)}, u32[]{:S(2)}) collective-permute-start(f32[384]{0:T(512)S(1)} %get-tuple-element.13), channel_id=1, source_target_pairs={{0,8},{1,9},{2,10},{3,11},{4,12},{5,13},{6,14},{7,15},{8,0},{9,1},... | collective-permute-start | bytes 4616 | tf_op jit(solution)/shard_map/ppermute | solution.py:20
  303.1 7.7 %collective-permute-start.24 = (f32[384]{0:T(512)S(1)}, f32[384]{0:T(512)S(1)}, u32[]{:S(2)}, u32[]{:S(2)}) collective-permute-start(f32[384]{0:T(512)S(1)} %get-tuple-element.13), channel_id=1, source_target_pairs={{0,9},{1,10},{2,11},{3,12},{4,13},{5,14},{6,15},{7,0},{8,1},{9,2},... | collective-permute-start | bytes 4616 | tf_op jit(solution)/shard_map/ppermute | solution.py:20
  330.0 45.2 %all-gather.5.cloned.1.call-done = bf16[1536,512]{1,0:T(8,128)(2,1)} async-done(((bf16[96,512]{1,0:T(8,128)(2,1)}), bf16[1536,512]{1,0:T(8,128)(2,1)}) %all-gather.5.cloned.1.call-update) | async-done | bytes 1572880 | tf_op jit(solution)/shard_map/all_gather | solution.py:49
  375.2 4.8 %pad_dynamic-slice_fusion.5 = (bf16[1536,512]{1,0:T(8,128)(2,1)S(1)}, bf16[1536,512]{1,0:T(8,128)(2,1)S(1)}, bf16[1536,512]{1,0:T(8,128)(2,1)S(1)}, bf16[1536,512]{1,0:T(8,128)(2,1)S(1)}) fusion(s32[]{:T(128)S(6)} %select_n.16, bf16[1536,512]{1,0:T(8,128)(2,1)} %all-gather.5.cloned.1.call-done, s32[]{:T(128)S(6)} %select_n.17, s32[]{:T(128)S(6)} %select_n.18, ...), kind=kLoop, calls=%fused_computation.18 | loop fusion | bytes 7864336 | tf_op jit(solution)/shard_map/dynamic_slice | solution.py:54
  380.0 7.9 %fusion.9 = f32[2048,640]{1,0:T(8,128)} fusion(bf16[1536,640]{1,0:T(8,128)(2,1)S(1)} %copy-done, bf16[1536,512]{1,0:T(8,128)(2,1)S(1)} %get-tuple-element.8, bf16[1536,512]{1,0:T(8,128)(2,1)S(1)} %get-tuple-element.7, bf16[1536,512]{1,0:T(8,128)(2,1)S(1)} %get-tuple-element.6, bf16[1536,512]{1,0:T(8,128)(2,1)S(1)} %get-tuple-element.5), kind=kOutput, calls=%fused_computation.11 | convolution fusion | flops 4053008384 | bytes 13500416 | tf_op jit(solution)/shard_map/dot_general | solution.py:57
  (86 shorter events, 37.8 us)
Async XLA Ops:
  6.5 250.6 %all-gather.3.cloned.1.call-start = ((), (), s32[]{:S(2)}) async-start(), calls=%async_computation | async-start | bytes 8912896 | tf_op jit(solution)/shard_map/all_gather | solution.py:32
  6.5 48.6 %collective-permute-start.15 = (bf16[512,512]{1,0:T(8,128)(2,1)}, bf16[512,512]{1,0:T(8,128)(2,1)S(1)}, u32[]{:S(2)}, u32[]{:S(2)}) collective-permute-start(bf16[512,512]{1,0:T(8,128)(2,1)} %param.8), channel_id=1, source_target_pairs={{0,0},{16,1},{32,2},{48,3},{64,4},{80,5},{96,6},{112,7},{128,8},{1... | collective-permute-start | bytes 1572872 | tf_op jit(solution)/shard_map/ppermute | solution.py:15
  56.0 319.2 %all-gather.5.cloned.1.call-start = ((), (), s32[]{:S(2)}) async-start(), calls=%async_computation.1 | async-start | bytes 1671168 | tf_op jit(solution)/shard_map/all_gather | solution.py:49
  56.0 23.1 %collective-permute-start = (bf16[384,512]{1,0:T(8,128)(2,1)}, bf16[384,512]{1,0:T(8,128)(2,1)}, u32[]{:S(2)}, u32[]{:S(2)}) collective-permute-start(bf16[384,512]{1,0:T(8,128)(2,1)} %param.7), channel_id=1, source_target_pairs={{0,1},{1,2},{2,3},{3,4},{4,5},{5,6},{6,7},{7,8},{8,9},{9,10},{10,1... | collective-permute-start | bytes 1179656 | tf_op jit(solution)/shard_map/ppermute | solution.py:20
  56.1 24.9 %collective-permute-start.1 = (bf16[384,512]{1,0:T(8,128)(2,1)}, bf16[384,512]{1,0:T(8,128)(2,1)}, u32[]{:S(2)}, u32[]{:S(2)}) collective-permute-start(bf16[384,512]{1,0:T(8,128)(2,1)} %param.7), channel_id=1, source_target_pairs={{0,2},{1,3},{2,4},{3,5},{4,6},{5,7},{6,8},{7,9},{8,10},{9,11},{10,... | collective-permute-start | bytes 1179656 | tf_op jit(solution)/shard_map/ppermute | solution.py:20
  63.1 52.5 %collective-permute-start.2 = (bf16[384,512]{1,0:T(8,128)(2,1)}, bf16[384,512]{1,0:T(8,128)(2,1)}, u32[]{:S(2)}, u32[]{:S(2)}) collective-permute-start(bf16[384,512]{1,0:T(8,128)(2,1)} %param.7), channel_id=1, source_target_pairs={{0,3},{1,4},{2,5},{3,6},{4,7},{5,8},{6,9},{7,10},{8,11},{9,12},{10... | collective-permute-start | bytes 1179656 | tf_op jit(solution)/shard_map/ppermute | solution.py:20
  71.0 46.5 %collective-permute-start.3 = (bf16[384,512]{1,0:T(8,128)(2,1)}, bf16[384,512]{1,0:T(8,128)(2,1)S(1)}, u32[]{:S(2)}, u32[]{:S(2)}) collective-permute-start(bf16[384,512]{1,0:T(8,128)(2,1)} %param.7), channel_id=1, source_target_pairs={{0,4},{1,5},{2,6},{3,7},{4,8},{5,9},{6,10},{7,11},{8,12},{9,13},{1... | collective-permute-start | bytes 1179656 | tf_op jit(solution)/shard_map/ppermute | solution.py:20
  71.0 90.6 %collective-permute-start.4 = (bf16[384,512]{1,0:T(8,128)(2,1)}, bf16[384,512]{1,0:T(8,128)(2,1)S(1)}, u32[]{:S(2)}, u32[]{:S(2)}) collective-permute-start(bf16[384,512]{1,0:T(8,128)(2,1)} %param.7), channel_id=1, source_target_pairs={{0,5},{1,6},{2,7},{3,8},{4,9},{5,10},{6,11},{7,12},{8,13},{9,14},{... | collective-permute-start | bytes 1179656 | tf_op jit(solution)/shard_map/ppermute | solution.py:20
  79.1 83.3 %collective-permute-start.5 = (bf16[384,512]{1,0:T(8,128)(2,1)}, bf16[384,512]{1,0:T(8,128)(2,1)S(1)}, u32[]{:S(2)}, u32[]{:S(2)}) collective-permute-start(bf16[384,512]{1,0:T(8,128)(2,1)} %param.7), channel_id=1, source_target_pairs={{0,6},{1,7},{2,8},{3,9},{4,10},{5,11},{6,12},{7,13},{8,14},{9,15},... | collective-permute-start | bytes 1179656 | tf_op jit(solution)/shard_map/ppermute | solution.py:20
  81.0 110.7 %collective-permute-start.6 = (bf16[384,512]{1,0:T(8,128)(2,1)}, bf16[384,512]{1,0:T(8,128)(2,1)S(1)}, u32[]{:S(2)}, u32[]{:S(2)}) collective-permute-start(bf16[384,512]{1,0:T(8,128)(2,1)} %param.7), channel_id=1, source_target_pairs={{0,7},{1,8},{2,9},{3,10},{4,11},{5,12},{6,13},{7,14},{8,15},{9,0},... | collective-permute-start | bytes 1179656 | tf_op jit(solution)/shard_map/ppermute | solution.py:20
  115.6 76.9 %collective-permute-start.7 = (bf16[384,512]{1,0:T(8,128)(2,1)}, bf16[384,512]{1,0:T(8,128)(2,1)S(1)}, u32[]{:S(2)}, u32[]{:S(2)}) collective-permute-start(bf16[384,512]{1,0:T(8,128)(2,1)} %param.7), channel_id=1, source_target_pairs={{0,8},{1,9},{2,10},{3,11},{4,12},{5,13},{6,14},{7,15},{8,0},{9,1},... | collective-permute-start | bytes 1179656 | tf_op jit(solution)/shard_map/ppermute | solution.py:20
  117.5 94.7 %collective-permute-start.8 = (bf16[384,512]{1,0:T(8,128)(2,1)}, bf16[384,512]{1,0:T(8,128)(2,1)S(1)}, u32[]{:S(2)}, u32[]{:S(2)}) collective-permute-start(bf16[384,512]{1,0:T(8,128)(2,1)} %param.7), channel_id=1, source_target_pairs={{0,9},{1,10},{2,11},{3,12},{4,13},{5,14},{6,15},{7,0},{8,1},{9,2},... | collective-permute-start | bytes 1179656 | tf_op jit(solution)/shard_map/ppermute | solution.py:20
  161.6 51.4 %collective-permute-start.9 = (bf16[384,512]{1,0:T(8,128)(2,1)}, bf16[384,512]{1,0:T(8,128)(2,1)S(1)}, u32[]{:S(2)}, u32[]{:S(2)}) collective-permute-start(bf16[384,512]{1,0:T(8,128)(2,1)} %param.7), channel_id=1, source_target_pairs={{0,10},{1,11},{2,12},{3,13},{4,14},{5,15},{6,0},{7,1},{8,2},{9,3},... | collective-permute-start | bytes 1179656 | tf_op jit(solution)/shard_map/ppermute | solution.py:20
  162.4 51.7 %collective-permute-start.10 = (bf16[384,512]{1,0:T(8,128)(2,1)}, bf16[384,512]{1,0:T(8,128)(2,1)S(1)}, u32[]{:S(2)}, u32[]{:S(2)}) collective-permute-start(bf16[384,512]{1,0:T(8,128)(2,1)} %param.7), channel_id=1, source_target_pairs={{0,11},{1,12},{2,13},{3,14},{4,15},{5,0},{6,1},{7,2},{8,3},{9,4},{... | collective-permute-start | bytes 1179656 | tf_op jit(solution)/shard_map/ppermute | solution.py:20
  191.7 33.9 %collective-permute-start.11 = (bf16[384,512]{1,0:T(8,128)(2,1)}, bf16[384,512]{1,0:T(8,128)(2,1)S(1)}, u32[]{:S(2)}, u32[]{:S(2)}) collective-permute-start(bf16[384,512]{1,0:T(8,128)(2,1)} %param.7), channel_id=1, source_target_pairs={{0,12},{1,13},{2,14},{3,15},{4,0},{5,1},{6,2},{7,3},{8,4},{9,5},{1... | collective-permute-start | bytes 1179656 | tf_op jit(solution)/shard_map/ppermute | solution.py:20
  192.5 40.4 %collective-permute-start.12 = (bf16[384,512]{1,0:T(8,128)(2,1)S(1)}, bf16[384,512]{1,0:T(8,128)(2,1)S(1)}, u32[]{:S(2)}, u32[]{:S(2)}) collective-permute-start(bf16[384,512]{1,0:T(8,128)(2,1)S(1)} %copy-done.2), channel_id=1, source_target_pairs={{0,13},{1,14},{2,15},{3,0},{4,1},{5,2},{6,3},{7,4},{8,5},{9,6},{10... | collective-permute-start | bytes 1179656 | tf_op jit(solution)/shard_map/ppermute | solution.py:20
  212.2 43.3 %collective-permute-start.13 = (bf16[384,512]{1,0:T(8,128)(2,1)S(1)}, bf16[384,512]{1,0:T(8,128)(2,1)S(1)}, u32[]{:S(2)}, u32[]{:S(2)}) collective-permute-start(bf16[384,512]{1,0:T(8,128)(2,1)S(1)} %copy-done.2), channel_id=1, source_target_pairs={{0,14},{1,15},{2,0},{3,1},{4,2},{5,3},{6,4},{7,5},{8,6},{9,7},{10,... | collective-permute-start | bytes 1179656 | tf_op jit(solution)/shard_map/ppermute | solution.py:20
  213.0 43.3 %collective-permute-start.14 = (bf16[384,512]{1,0:T(8,128)(2,1)S(1)}, bf16[384,512]{1,0:T(8,128)(2,1)S(1)}, u32[]{:S(2)}, u32[]{:S(2)}) collective-permute-start(bf16[384,512]{1,0:T(8,128)(2,1)S(1)} %copy-done.2), channel_id=1, source_target_pairs={{0,15},{1,0},{2,1},{3,2},{4,3},{5,4},{6,5},{7,6},{8,7},{9,8},{10,9... | collective-permute-start | bytes 1179656 | tf_op jit(solution)/shard_map/ppermute | solution.py:20
  274.4 22.9 %collective-permute-start.16 = (f32[384]{0:T(512)S(1)}, f32[384]{0:T(512)S(1)}, u32[]{:S(2)}, u32[]{:S(2)}) collective-permute-start(f32[384]{0:T(512)S(1)} %get-tuple-element.13), channel_id=1, source_target_pairs={{0,1},{1,2},{2,3},{3,4},{4,5},{5,6},{6,7},{7,8},{8,9},{9,10},{10,1... | collective-permute-start | bytes 4616 | tf_op jit(solution)/shard_map/ppermute | solution.py:20
  288.9 14.2 %collective-permute-start.19 = (f32[384]{0:T(512)S(1)}, f32[384]{0:T(512)S(1)}, u32[]{:S(2)}, u32[]{:S(2)}) collective-permute-start(f32[384]{0:T(512)S(1)} %get-tuple-element.13), channel_id=1, source_target_pairs={{0,4},{1,5},{2,6},{3,7},{4,8},{5,9},{6,10},{7,11},{8,12},{9,13},{1... | collective-permute-start | bytes 4616 | tf_op jit(solution)/shard_map/ppermute | solution.py:20
  288.9 21.8 %collective-permute-start.20 = (f32[384]{0:T(512)S(1)}, f32[384]{0:T(512)S(1)}, u32[]{:S(2)}, u32[]{:S(2)}) collective-permute-start(f32[384]{0:T(512)S(1)} %get-tuple-element.13), channel_id=1, source_target_pairs={{0,5},{1,6},{2,7},{3,8},{4,9},{5,10},{6,11},{7,12},{8,13},{9,14},{... | collective-permute-start | bytes 4616 | tf_op jit(solution)/shard_map/ppermute | solution.py:20
  297.3 15.9 %collective-permute-start.22 = (f32[384]{0:T(512)S(1)}, f32[384]{0:T(512)S(1)}, u32[]{:S(2)}, u32[]{:S(2)}) collective-permute-start(f32[384]{0:T(512)S(1)} %get-tuple-element.13), channel_id=1, source_target_pairs={{0,7},{1,8},{2,9},{3,10},{4,11},{5,12},{6,13},{7,14},{8,15},{9,0},... | collective-permute-start | bytes 4616 | tf_op jit(solution)/shard_map/ppermute | solution.py:20
  298.3 17.2 %collective-permute-start.23 = (f32[384]{0:T(512)S(1)}, f32[384]{0:T(512)S(1)}, u32[]{:S(2)}, u32[]{:S(2)}) collective-permute-start(f32[384]{0:T(512)S(1)} %get-tuple-element.13), channel_id=1, source_target_pairs={{0,8},{1,9},{2,10},{3,11},{4,12},{5,13},{6,14},{7,15},{8,0},{9,1},... | collective-permute-start | bytes 4616 | tf_op jit(solution)/shard_map/ppermute | solution.py:20
  303.1 14.8 %collective-permute-start.24 = (f32[384]{0:T(512)S(1)}, f32[384]{0:T(512)S(1)}, u32[]{:S(2)}, u32[]{:S(2)}) collective-permute-start(f32[384]{0:T(512)S(1)} %get-tuple-element.13), channel_id=1, source_target_pairs={{0,9},{1,10},{2,11},{3,12},{4,13},{5,14},{6,15},{7,0},{8,1},{9,2},... | collective-permute-start | bytes 4616 | tf_op jit(solution)/shard_map/ppermute | solution.py:20
  (17 other events, 791.5 us)
Sparse Core Ops, SparseCore 0:
  56.1 82.1 all-gather.2
  324.4 50.7 all-gather.4

commit v3 on v1

v3 whole, which is shorter than its diff:
```python
import jax
import jax.numpy as jnp
from jax import lax
from jax.sharding import Mesh, PartitionSpec as P

D = 8192
LAGS = 4
R_DEV = 96
GROUP = ("xlo", "y", "core")
TENSOR = ("z", "xhi")


def transposed_block(block):
    groups = lax.axis_size(GROUP)
    tensors = lax.axis_size(TENSOR)
    route = [(t * tensors + g, g * tensors + t) for g in range(groups) for t in range(tensors)]
    return lax.ppermute(block, GROUP + TENSOR, route)


def on_device(attention, out_weight, residual, gain, token_tr, lag_offsets, responses):
    weight_cols = lax.all_gather(transposed_block(out_weight), GROUP, axis=0, tiled=True)
    rows = lax.all_gather(lax.all_gather(attention, "xhi", axis=1, tiled=True), "z", axis=1, tiled=True)
    summed = jnp.dot(rows, weight_cols, preferred_element_type=jnp.float32)
    hidden = residual.astype(jnp.float32) + summed
    squares = lax.psum(lax.psum(jnp.sum(hidden * hidden, axis=1), "xhi"), "z")
    normed = (hidden * lax.rsqrt(squares[:, None] / D + 1e-05) * gain[None, :]).astype(jnp.bfloat16)
    member = jnp.arange(R_DEV, dtype=jnp.int32)[:, None] == token_tr[0][None, :]
    counts = jnp.sum(member.astype(jnp.float32), axis=1, keepdims=True)
    binned = (
        jnp.dot(member.astype(jnp.bfloat16), normed, preferred_element_type=jnp.float32) / counts
    ).astype(jnp.bfloat16)
    width = binned.shape[1]
    total_trs = responses.shape[0]
    story = lax.all_gather(binned, GROUP, axis=0, tiled=True)
    extended = jnp.concatenate([jnp.zeros((LAGS, width), story.dtype), story], axis=0)
    pieces = []
    for step in range(LAGS):
        start = LAGS - lag_offsets[step]
        pieces.append(lax.dynamic_slice_in_dim(extended, start, total_trs, 0))
    lagged = jnp.concatenate(pieces, axis=1)
    contract = (((0,), (0,)), ((), ()))
    accumulated = lax.dot_general(lagged, responses, contract, preferred_element_type=jnp.float32)
    scaled = accumulated * (1.0 / jnp.sqrt(jnp.float32(total_trs)))
    return scaled.reshape(LAGS, width, responses.shape[1])


def solution(mesh):
    parts = Mesh(mesh.devices.reshape(2, 4, 2, 8, 2), GROUP + TENSOR)
    return jax.shard_map(
        on_device,
        mesh=parts,
        in_specs=(
            P(GROUP, TENSOR),
            P(TENSOR, GROUP),
            P(GROUP, TENSOR),
            P(TENSOR),
            P(GROUP, None),
            P(),
            P(None, GROUP),
        ),
        out_specs=P(None, TENSOR, GROUP),
        check_vma=False,
    )
```

time: 327 us -> 278 us (0.85)
  waiting for transfers between devices: 243 us -> 197 us
    all_gather x3, waiting for transfers between devices: 195 us -> 165 us  [the longest x1 77.2 us: on_device(): lax.all_gather(lax.all_gather(attention, 'xhi', axis=1, tiled=True), 'z',...]
    psum x1 -> x2, blocking collectives: 35.1 us -> 19 us  [on_device(): squares = lax.psum(lax.psum(jnp.sum(hidden * hidden, axis=1), 'xhi'), 'z')]
    ppermute x1, waiting for transfers between devices: 46.8 us -> 31.9 us  [transposed_block(): return lax.ppermute(block, GROUP + TENSOR, route)]
    all_gather x0 -> x1, blocking collectives: none -> 14.8 us  [on_device(): lax.all_gather(attention, 'xhi', axis=1, tiled=True)]
where the time goes in v3:
time: 278 us
  waiting for transfers between devices  197 us (71%)
  blocking collectives  33.8 us (12%)
  between operations  18.2 us (7%)
  matrix products  16.9 us (6%)
  local copies, waits for them, and re-layouts  6.4 us (2%)
  starting transfers between devices  4.8 us (2%)
    all_gather x1, waiting for transfers between devices, on_device(): lax.all_gather(lax.all_gather(attention, 'xhi', axis=1, tiled=True), 'z',...  77.2 us
    all_gather x1, waiting for transfers between devices, on_device(): lax.all_gather(transposed_block(out_weight), GROUP, axis=0, tiled=True)  54.8 us
    all_gather x1, waiting for transfers between devices, on_device(): story = lax.all_gather(binned, GROUP, axis=0, tiled=True)  33.4 us
    ppermute x1, waiting for transfers between devices, transposed_block(): return lax.ppermute(block, GROUP + TENSOR, route)  31.9 us
    psum x2, blocking collectives, on_device(): squares = lax.psum(lax.psum(jnp.sum(hidden * hidden, axis=1), 'xhi'), 'z')  19 us
    all_gather x1, blocking collectives, on_device(): lax.all_gather(attention, 'xhi', axis=1, tiled=True)  14.8 us
    dot_general x1, matrix products, on_device(): summed = jnp.dot(rows, weight_cols, preferred_element_type=jnp.float32)  8.04 us
    dot_general x1, matrix products, on_device(): lax.dot_general(lagged, responses, contract, preferred_element_type=jnp.f...  7.88 us
  transfers between devices with their start and end apart: 4, of which 4 were waited for; matrix products, arithmetic and copies ran while one was open for 0% of the time, Pallas kernels for 0%

profile of v3, /device:TPU:1, one launch (start us, length us, event | category | flops | bytes accessed | tf_op | source)
XLA Modules:
  0.0 277.6 jit_solution(1108428231418364595)
XLA Ops:
  6.5 0.0 copy-start
  6.5 0.0 all-gather.4.cloned.1.call-start
  6.6 14.8 %all_gather.12 = bf16[384,1024]{1,0:T(8,128)(2,1)} all-gather(bf16[384,512]{1,0:T(8,128)(2,1)} %param.7), channel_id=1, replica_groups=mesh['xlo'=2,'y'=4,'core'=2,'z'=8,'xhi'=2] {'xhi'}, dimensions={1}, use_global_device_ids=true | all-gather | bytes 1179648 | tf_op jit(solution)/shard_map/all_gather | solution.py:22
  21.4 0.0 all-gather.4.cloned.1.call-update
  21.4 0.0 all-gather.6.cloned.1.call-start
  21.5 4.7 %collective-permute-start = (bf16[512,512]{1,0:T(8,128)(2,1)S(1)}, bf16[512,512]{1,0:T(8,128)(2,1)S(1)}, u32[]{:S(2)}, u32[]{:S(2)}) collective-permute-start(bf16[512,512]{1,0:T(8,128)(2,1)S(1)} %copy-done.4), channel_id=1, source_target_pairs={{0,0},{16,1},{32,2},{48,3},{64,4},{80,5},{96,6},{112,7},{128,8},{1... | collective-permute-start | bytes 1572872 | tf_op jit(solution)/shard_map/ppermute | solution.py:17
  26.2 31.9 %collective-permute-done = bf16[512,512]{1,0:T(8,128)(2,1)S(1)} collective-permute-done((bf16[512,512]{1,0:T(8,128)(2,1)S(1)}, bf16[512,512]{1,0:T(8,128)(2,1)S(1)}, u32[]{:S(2)}, u32[]{:S(2)}) %collective-permute-start) | collective-permute-done | bytes 524320 | tf_op jit(solution)/shard_map/ppermute | solution.py:17
  58.1 0.8 copy-done.1
  58.9 0.0 all-gather.6.cloned.1.call-update
  58.9 0.0 all-gather.8.cloned.1.call-start
  59.0 0.1 convert_reduce_fusion
  59.1 0.0 copy-start.6
  59.1 0.0 copy-start.2
  59.2 77.2 %all-gather.4.cloned.1.call-done = bf16[384,8192]{1,0:T(8,128)(2,1)} async-done(((bf16[384,1024]{1,0:T(8,128)(2,1)}), bf16[384,8192]{1,0:T(8,128)(2,1)}) %all-gather.4.cloned.1.call-update) | async-done | bytes 6291472 | tf_op jit(solution)/shard_map/all_gather | solution.py:22
  136.4 54.8 %all-gather.6.cloned.1.call-done = bf16[8192,512]{1,0:T(8,128)(2,1)} async-done(((bf16[512,512]{1,0:T(8,128)(2,1)}), bf16[8192,512]{1,0:T(8,128)(2,1)}) %all-gather.6.cloned.1.call-update) | async-done | bytes 8388624 | tf_op jit(solution)/shard_map/all_gather | solution.py:21
  191.2 8.0 %multiply_reduce_fusion = (f32[384]{0:T(512)S(1)}, f32[384,512]{1,0:T(8,128)S(1)}) fusion(bf16[384,8192]{1,0:T(8,128)(2,1)} %all-gather.4.cloned.1.call-done, bf16[8192,512]{1,0:T(8,128)(2,1)} %all-gather.6.cloned.1.call-done, bf16[384,512]{1,0:T(8,128)(2,1)S(1)} %copy-done.5), kind=kOutput, calls=%fused_computation.17 | convolution fusion | flops 3222011392 | bytes 15861248 | tf_op jit(solution)/shard_map/dot_general | solution.py:23
  199.3 5.3 %psum.14 = f32[384]{0:T(512)S(1)} all-reduce(f32[384]{0:T(512)S(1)} %get-tuple-element.13), channel_id=1, replica_groups=mesh['xlo'=2,'y'=4,'core'=2,'z'=8,'xhi'=2] {'xhi'}, use_global_device_ids=true, to_apply=%region_1.0 | all-reduce | flops 384 | bytes 3072 | tf_op jit(solution)/shard_map/psum | solution.py:25
  204.5 13.7 %psum.15 = f32[384]{0:T(512)S(1)} all-reduce(f32[384]{0:T(512)S(1)} %psum.14), channel_id=1, replica_groups=mesh['xlo'=2,'y'=4,'core'=2,'z'=8,'xhi'=2] {'z'}, use_global_device_ids=true, to_apply=%region_2.0 | all-reduce | flops 384 | bytes 3072 | tf_op jit(solution)/shard_map/psum | solution.py:25
  218.2 0.9 fusion.11
  219.2 0.0 all-gather.8.cloned.1.call-update
  219.2 0.7 fusion.16
  224.8 33.4 %all-gather.8.cloned.1.call-done = bf16[1536,512]{1,0:T(8,128)(2,1)} async-done(((bf16[96,512]{1,0:T(8,128)(2,1)}), bf16[1536,512]{1,0:T(8,128)(2,1)}) %all-gather.8.cloned.1.call-update) | async-done | bytes 1572880 | tf_op jit(solution)/shard_map/all_gather | solution.py:34
  258.3 4.9 %pad_dynamic-slice_fusion.3 = (bf16[1536,512]{1,0:T(8,128)(2,1)S(1)}, bf16[1536,512]{1,0:T(8,128)(2,1)S(1)}, bf16[1536,512]{1,0:T(8,128)(2,1)S(1)}, bf16[1536,512]{1,0:T(8,128)(2,1)S(1)}) fusion(s32[]{:T(128)S(6)} %select_n.12, bf16[1536,512]{1,0:T(8,128)(2,1)} %all-gather.8.cloned.1.call-done, s32[]{:T(128)S(6)} %select_n.13, s32[]{:T(128)S(6)} %select_n.14, ...), kind=kLoop, calls=%fused_computation.15 | loop fusion | bytes 7864336 | tf_op jit(solution)/shard_map/dynamic_slice | solution.py:39
  263.2 7.9 %fusion.8 = f32[2048,640]{1,0:T(8,128)} fusion(bf16[1536,640]{1,0:T(8,128)(2,1)S(1)} %copy-done, bf16[1536,512]{1,0:T(8,128)(2,1)S(1)} %get-tuple-element.8, bf16[1536,512]{1,0:T(8,128)(2,1)S(1)} %get-tuple-element.7, bf16[1536,512]{1,0:T(8,128)(2,1)S(1)} %get-tuple-element.6, bf16[1536,512]{1,0:T(8,128)(2,1)S(1)} %get-tuple-element.5), kind=kOutput, calls=%fused_computation.8 | convolution fusion | flops 4053008384 | bytes 13500416 | tf_op jit(solution)/shard_map/dot_general | solution.py:42
  (12 shorter events, 0.0 us)
Async XLA Ops:
  6.5 256.7 %copy-start = (bf16[1536,640]{1,0:T(8,128)(2,1)S(1)}, bf16[1536,640]{1,0:T(8,128)(2,1)}, u32[]{:S(2)}) copy-start(bf16[1536,640]{1,0:T(8,128)(2,1)} %param.13) | copy-start | bytes 5898244
  6.5 14.9 %copy-start.4 = (bf16[512,512]{1,0:T(8,128)(2,1)S(1)}, bf16[512,512]{1,0:T(8,128)(2,1)}, u32[]{:S(2)}) copy-start(bf16[512,512]{1,0:T(8,128)(2,1)} %param.8) | copy-start | bytes 1572868
  6.5 52.4 %copy-start.3 = (s32[1,384]{1,0:T(1,128)S(1)}, s32[1,384]{1,0:T(1,128)}, u32[]{:S(2)}) copy-start(s32[1,384]{1,0:T(1,128)} %param.11) | copy-start | bytes 4612
  6.5 184.7 %copy-start.5 = (bf16[384,512]{1,0:T(8,128)(2,1)S(1)}, bf16[384,512]{1,0:T(8,128)(2,1)}, u32[]{:S(2)}) copy-start(bf16[384,512]{1,0:T(8,128)(2,1)} %param.9) | copy-start | bytes 1179652
  6.5 129.9 %all-gather.4.cloned.1.call-start = ((), (), s32[]{:S(2)}) async-start(), calls=%async_computation | async-start | bytes 7077888 | tf_op jit(solution)/shard_map/all_gather | solution.py:22
  21.4 169.8 %all-gather.6.cloned.1.call-start = ((), (), s32[]{:S(2)}) async-start(), calls=%async_computation.1 | async-start | bytes 8912896 | tf_op jit(solution)/shard_map/all_gather | solution.py:21
  21.5 36.6 %collective-permute-start = (bf16[512,512]{1,0:T(8,128)(2,1)S(1)}, bf16[512,512]{1,0:T(8,128)(2,1)S(1)}, u32[]{:S(2)}, u32[]{:S(2)}) collective-permute-start(bf16[512,512]{1,0:T(8,128)(2,1)S(1)} %copy-done.4), channel_id=1, source_target_pairs={{0,0},{16,1},{32,2},{48,3},{64,4},{80,5},{96,6},{112,7},{128,8},{1... | collective-permute-start | bytes 1572872 | tf_op jit(solution)/shard_map/ppermute | solution.py:17
  58.1 0.8 copy-start.1
  58.9 199.3 %all-gather.8.cloned.1.call-start = ((), (), s32[]{:S(2)}) async-start(), calls=%async_computation.2 | async-start | bytes 1671168 | tf_op jit(solution)/shard_map/all_gather | solution.py:34
  59.1 159.1 %copy-start.6 = (f32[512]{0:T(512)S(1)}, f32[512]{0:T(512)}, u32[]{:S(2)}) copy-start(f32[512]{0:T(512)} %param.10) | copy-start | bytes 6148
  59.1 160.1 %copy-start.2 = (s32[4]{0:T(128)S(1)}, s32[4]{0:T(128)}, u32[]{:S(2)}) copy-start(s32[4]{0:T(128)} %param.12) | copy-start | bytes 52
Sparse Core Ops, SparseCore 0:
  21.5 114.8 all-gather.3
  138.2 52.9 all-gather.5
  219.3 38.8 all-gather.7

commit v4 on v3

--- a/solution.py
+++ b/solution.py
@@ -10,15 +10,28 @@
 TENSOR = ("z", "xhi")
 
 
+def core_last(g, cores, rest):
+    return (g % cores) * rest + g // cores
+
+
 def transposed_block(block):
     groups = lax.axis_size(GROUP)
     tensors = lax.axis_size(TENSOR)
-    route = [(t * tensors + g, g * tensors + t) for g in range(groups) for t in range(tensors)]
+    cores = lax.axis_size("core")
+    route = [
+        (t * tensors + core_last(g, cores, groups // cores), g * tensors + t)
+        for g in range(groups)
+        for t in range(tensors)
+    ]
     return lax.ppermute(block, GROUP + TENSOR, route)
 
 
+def gather_core_last(block, axis):
+    return lax.all_gather(lax.all_gather(block, GROUP[:-1], axis=axis, tiled=True), "core", axis=axis, tiled=True)
+
+
 def on_device(attention, out_weight, residual, gain, token_tr, lag_offsets, responses):
-    weight_cols = lax.all_gather(transposed_block(out_weight), GROUP, axis=0, tiled=True)
+    weight_cols = gather_core_last(transposed_block(out_weight), 0)
     rows = lax.all_gather(lax.all_gather(attention, "xhi", axis=1, tiled=True), "z", axis=1, tiled=True)
     summed = jnp.dot(rows, weight_cols, preferred_element_type=jnp.float32)
     hidden = residual.astype(jnp.float32) + summed
@@ -31,7 +44,8 @@
     ).astype(jnp.bfloat16)
     width = binned.shape[1]
     total_trs = responses.shape[0]
-    story = lax.all_gather(binned, GROUP, axis=0, tiled=True)
+    by_core = lax.all_gather(lax.all_gather(binned, GROUP[:-1], axis=0), "core", axis=0)
+    story = jnp.swapaxes(by_core, 0, 1).reshape(-1, width)
     extended = jnp.concatenate([jnp.zeros((LAGS, width), story.dtype), story], axis=0)
     pieces = []
     for step in range(LAGS):

time: 278 us -> 317 us (1.14)
  blocking collectives: 33.8 us -> 57.3 us
  waiting for transfers between devices: 197 us -> 213 us
    all_gather x0 -> x1, blocking collectives: none -> 26.3 us  [on_device(): lax.all_gather(binned, GROUP[:-1], axis=0)]
    ppermute x1, waiting for transfers between devices: 31.9 us -> 43.2 us  [transposed_block(): return lax.ppermute(block, GROUP + TENSOR, route)]
    all_gather x2 -> x3, waiting for transfers between devices: 88.2 us -> 95.4 us  [the longest x1 50.3 us: gather_core_last(): lax.all_gather(block, GROUP[:-1], axis=axis, tiled=True)]
    dynamic_slice x1, local copies, waits for them, and re-layouts: 4.93 us -> 1.6 us  [on_device(): pieces.append(lax.dynamic_slice_in_dim(extended, start, total_trs, 0))]
  transfers between devices with their start and end apart: 4 -> 5, of which waited for: 4 -> 5; matrix products, arithmetic and copies ran while one was open for 0% -> 0% of each run, Pallas kernels for 0% -> 0%
where the time goes in v4:
time: 317 us; the launch traced here: 316 us
  waiting for transfers between devices  213 us (67%)
  blocking collectives  57.3 us (18%)
  between operations  18.3 us (6%)
  matrix products  16.2 us (5%)
  starting transfers between devices  6.27 us (2%)
  local copies, waits for them, and re-layouts  5.14 us (2%)
    all_gather x1, waiting for transfers between devices, on_device(): lax.all_gather(lax.all_gather(attention, 'xhi', axis=1, tiled=True), 'z',...  74.2 us
    all_gather x1, waiting for transfers between devices, gather_core_last(): lax.all_gather(block, GROUP[:-1], axis=axis, tiled=True)  50.3 us
    ppermute x1, waiting for transfers between devices, transposed_block(): return lax.ppermute(block, GROUP + TENSOR, route)  43.2 us
    all_gather x1, waiting for transfers between devices, gather_core_last(): lax.all_gather(lax.all_gather(block, GROUP[:-1], axis=axis, tiled=True),...  26.5 us
    all_gather x1, blocking collectives, on_device(): lax.all_gather(binned, GROUP[:-1], axis=0)  26.3 us
    psum x2, blocking collectives, on_device(): squares = lax.psum(lax.psum(jnp.sum(hidden * hidden, axis=1), 'xhi'), 'z')  18.7 us
    all_gather x1, waiting for transfers between devices, on_device(): lax.all_gather(lax.all_gather(binned, GROUP[:-1], axis=0), 'core', axis=0)  18.7 us
    all_gather x1, blocking collectives, on_device(): lax.all_gather(attention, 'xhi', axis=1, tiled=True)  12.3 us
  transfers between devices with their start and end apart: 5, of which 5 were waited for; matrix products, arithmetic and copies ran while one was open for 0% of the time, Pallas kernels for 0%

profile of v4, /device:TPU:1, one launch (start us, length us, event | category | flops | bytes accessed | tf_op | source)
XLA Modules:
  0.0 316.3 jit_solution(4495347800730659212)
XLA Ops:
  6.5 6.1 %collective-permute-start = (bf16[512,512]{1,0:T(8,128)(2,1)}, bf16[512,512]{1,0:T(8,128)(2,1)S(1)}, u32[]{:S(2)}, u32[]{:S(2)}) collective-permute-start(bf16[512,512]{1,0:T(8,128)(2,1)} %param.8), channel_id=1, source_target_pairs={{0,0},{16,1},{32,2},{48,3},{64,4},{80,5},{96,6},{112,7},{128,8},{1... | collective-permute-start | bytes 1572872 | tf_op jit(solution)/shard_map/ppermute | solution.py:26
  12.7 43.2 %collective-permute-done = bf16[512,512]{1,0:T(8,128)(2,1)S(1)} collective-permute-done((bf16[512,512]{1,0:T(8,128)(2,1)}, bf16[512,512]{1,0:T(8,128)(2,1)S(1)}, u32[]{:S(2)}, u32[]{:S(2)}) %collective-permute-start) | collective-permute-done | bytes 524320 | tf_op jit(solution)/shard_map/ppermute | solution.py:26
  55.9 0.8 copy-done.1
  56.7 0.0 all-gather.7.cloned.1.call-start
  56.8 12.3 %all_gather.24 = bf16[384,1024]{1,0:T(8,128)(2,1)} all-gather(bf16[384,512]{1,0:T(8,128)(2,1)} %param.7), channel_id=1, replica_groups=mesh['xlo'=2,'y'=4,'core'=2,'z'=8,'xhi'=2] {'xhi'}, dimensions={1}, use_global_device_ids=true | all-gather | bytes 1179648 | tf_op jit(solution)/shard_map/all_gather | solution.py:35
  69.1 0.0 all-gather.7.cloned.1.call-update
  69.1 0.0 all-gather.11.cloned.1.call-start
  69.1 50.3 %all-gather.9.cloned.1.call-done = bf16[4096,512]{1,0:T(8,128)(2,1)} async-done(((bf16[512,512]{1,0:T(8,128)(2,1)}), bf16[4096,512]{1,0:T(8,128)(2,1)}) %all-gather.9.cloned.1.call-update) | async-done | bytes 4194320 | tf_op jit(solution)/shard_map/all_gather | solution.py:30
  119.4 0.0 all-gather.13.cloned.1.call-start
  119.5 0.6 copy-done.3
  120.1 0.1 convert_reduce_fusion
  120.2 74.2 %all-gather.7.cloned.1.call-done = bf16[384,8192]{1,0:T(8,128)(2,1)} async-done(((bf16[384,1024]{1,0:T(8,128)(2,1)}), bf16[384,8192]{1,0:T(8,128)(2,1)}) %all-gather.7.cloned.1.call-update) | async-done | bytes 6291472 | tf_op jit(solution)/shard_map/all_gather | solution.py:35
  194.5 26.5 %all-gather.11.cloned.1.call-done = bf16[8192,512]{1,0:T(8,128)(2,1)} async-done(((bf16[4096,512]{1,0:T(8,128)(2,1)}), bf16[8192,512]{1,0:T(8,128)(2,1)}) %all-gather.11.cloned.1.call-update) | async-done | bytes 8388624 | tf_op jit(solution)/shard_map/all_gather | solution.py:30
  221.0 8.0 %multiply_reduce_fusion = (f32[384]{0:T(512)S(1)}, f32[384,512]{1,0:T(8,128)S(1)}) fusion(bf16[384,8192]{1,0:T(8,128)(2,1)} %all-gather.7.cloned.1.call-done, bf16[8192,512]{1,0:T(8,128)(2,1)} %all-gather.11.cloned.1.call-done, bf16[384,512]{1,0:T(8,128)(2,1)S(1)} %copy-done.4), kind=kOutput, calls=%fused_computation.17 | convolution fusion | flops 3222011392 | bytes 15861248 | tf_op jit(solution)/shard_map/dot_general | solution.py:36
  229.0 5.3 %psum.14 = f32[384]{0:T(512)S(1)} all-reduce(f32[384]{0:T(512)S(1)} %get-tuple-element.13), channel_id=1, replica_groups=mesh['xlo'=2,'y'=4,'core'=2,'z'=8,'xhi'=2] {'xhi'}, use_global_device_ids=true, to_apply=%region_1.0 | all-reduce | flops 384 | bytes 3072 | tf_op jit(solution)/shard_map/psum | solution.py:38
  234.3 13.4 %psum.15 = f32[384]{0:T(512)S(1)} all-reduce(f32[384]{0:T(512)S(1)} %psum.14), channel_id=1, replica_groups=mesh['xlo'=2,'y'=4,'core'=2,'z'=8,'xhi'=2] {'z'}, use_global_device_ids=true, to_apply=%region_2.0 | all-reduce | flops 384 | bytes 3072 | tf_op jit(solution)/shard_map/psum | solution.py:38
  247.7 0.3 fusion.11
  248.1 26.3 %all-gather = bf16[768,512]{1,0:T(8,128)(2,1)} all-gather(bf16[96,512]{1,0:T(8,128)(2,1)S(1)} %fusion.11), channel_id=2, replica_groups=mesh['xlo'=2,'y'=4,'core'=2,'z'=8,'xhi'=2] {'xlo','y'}, dimensions={0}, use_global_device_ids=true | all-gather | bytes 884736 | tf_op jit(solution)/shard_map/all_gather | solution.py:47
  274.4 0.0 all-gather.13.cloned.1.call-update
  274.4 0.6 fusion.16
  280.1 18.7 %all-gather.13.cloned.1.call-done = bf16[16,96,512]{2,1,0:T(8,128)(2,1)} async-done(((bf16[8,96,512]{2,1,0:T(8,128)(2,1)}), bf16[16,96,512]{2,1,0:T(8,128)(2,1)}) %all-gather.13.cloned.1.call-update) | async-done | bytes 1572880 | tf_op jit(solution)/shard_map/all_gather | solution.py:47
  298.8 1.5 copy.10
  300.3 1.6 pad_dynamic-slice_fusion.3
  301.9 7.9 %fusion.8 = f32[2048,640]{1,0:T(8,128)} fusion(bf16[1536,640]{1,0:T(8,128)(2,1)S(1)} %copy-done, bf16[1536,512]{1,0:T(8,128)(2,1)S(1)} %get-tuple-element.8, bf16[1536,512]{1,0:T(8,128)(2,1)S(1)} %get-tuple-element.7, bf16[1536,512]{1,0:T(8,128)(2,1)S(1)} %get-tuple-element.6, bf16[1536,512]{1,0:T(8,128)(2,1)S(1)} %get-tuple-element.5), kind=kOutput, calls=%fused_computation.8 | convolution fusion | flops 4053008384 | bytes 13500416 | tf_op jit(solution)/shard_map/dot_general | solution.py:56
  (15 shorter events, 0.1 us)
Async XLA Ops:
  6.5 295.4 %copy-start = (bf16[1536,640]{1,0:T(8,128)(2,1)S(1)}, bf16[1536,640]{1,0:T(8,128)(2,1)}, u32[]{:S(2)}) copy-start(bf16[1536,640]{1,0:T(8,128)(2,1)} %param.13) | copy-start | bytes 5898244
  6.5 112.9 %all-gather.9.cloned.1.call-start = ((), (), s32[]{:S(2)}) async-start(), calls=%async_computation.1 | async-start | bytes 4718592 | tf_op jit(solution)/shard_map/all_gather | solution.py:30
  6.5 49.4 %collective-permute-start = (bf16[512,512]{1,0:T(8,128)(2,1)}, bf16[512,512]{1,0:T(8,128)(2,1)S(1)}, u32[]{:S(2)}, u32[]{:S(2)}) collective-permute-start(bf16[512,512]{1,0:T(8,128)(2,1)} %param.8), channel_id=1, source_target_pairs={{0,0},{16,1},{32,2},{48,3},{64,4},{80,5},{96,6},{112,7},{128,8},{1... | collective-permute-start | bytes 1572872 | tf_op jit(solution)/shard_map/ppermute | solution.py:26
  55.9 0.8 copy-start.1
  56.7 137.7 %all-gather.7.cloned.1.call-start = ((), (), s32[]{:S(2)}) async-start(), calls=%async_computation | async-start | bytes 7077888 | tf_op jit(solution)/shard_map/all_gather | solution.py:35
  69.1 151.9 %all-gather.11.cloned.1.call-start = ((), (), s32[]{:S(2)}) async-start(), calls=%async_computation.2 | async-start | bytes 12582912 | tf_op jit(solution)/shard_map/all_gather | solution.py:30
  119.4 0.7 copy-start.3
  119.4 101.6 %copy-start.4 = (bf16[384,512]{1,0:T(8,128)(2,1)S(1)}, bf16[384,512]{1,0:T(8,128)(2,1)}, u32[]{:S(2)}) copy-start(bf16[384,512]{1,0:T(8,128)(2,1)} %param.9) | copy-start | bytes 1179652
  119.4 179.4 %all-gather.13.cloned.1.call-start = ((), (), s32[]{:S(2)}) async-start(), calls=%async_computation.3 | async-start | bytes 2359296 | tf_op jit(solution)/shard_map/all_gather | solution.py:47
  120.2 127.5 %copy-start.5 = (f32[512]{0:T(512)S(1)}, f32[512]{0:T(512)}, u32[]{:S(2)}) copy-start(f32[512]{0:T(512)} %param.10) | copy-start | bytes 6148
  229.0 45.4 %copy-start.2 = (s32[4]{0:T(128)S(1)}, s32[4]{0:T(128)}, u32[]{:S(2)}) copy-start(s32[4]{0:T(128)} %param.12) | copy-start | bytes 52
Sparse Core Ops, SparseCore 0:
  56.9 62.5 all-gather.8
  121.2 73.2 all-gather.6
  196.3 24.6 all-gather.10
  274.5 24.2 all-gather.12

commit v5 on v3

--- a/solution.py
+++ b/solution.py
@@ -10,17 +10,30 @@
 TENSOR = ("z", "xhi")
 
 
-def transposed_block(block):
+def z_ring_block(block):
     groups = lax.axis_size(GROUP)
     tensors = lax.axis_size(TENSOR)
-    route = [(t * tensors + g, g * tensors + t) for g in range(groups) for t in range(tensors)]
+    xs = lax.axis_size("xhi")
+    route = []
+    for g in range(groups):
+        for t in range(tensors):
+            z, x = t // xs, t % xs
+            source = (xs * (g // xs) + x) * tensors + xs * z + g % xs
+            route.append((source, g * tensors + t))
     return lax.ppermute(block, GROUP + TENSOR, route)
 
 
 def on_device(attention, out_weight, residual, gain, token_tr, lag_offsets, responses):
-    weight_cols = lax.all_gather(transposed_block(out_weight), GROUP, axis=0, tiled=True)
-    rows = lax.all_gather(lax.all_gather(attention, "xhi", axis=1, tiled=True), "z", axis=1, tiled=True)
-    summed = jnp.dot(rows, weight_cols, preferred_element_type=jnp.float32)
+    xs = lax.axis_size("xhi")
+    zs = lax.axis_size("z")
+    heads = attention.shape[1]
+    slab = lax.all_gather(attention, "xhi", axis=1, tiled=True)
+    blocks = lax.all_gather(z_ring_block(out_weight), GROUP, axis=0).reshape(zs, xs, heads, -1)
+    partial = jnp.einsum(
+        "ich,zchf->izf", slab.reshape(-1, xs, heads), blocks, preferred_element_type=jnp.float32
+    )
+    received = lax.all_to_all(partial.astype(jnp.bfloat16), "z", 1, 1, tiled=True)
+    summed = jnp.sum(received.astype(jnp.float32), axis=1)
     hidden = residual.astype(jnp.float32) + summed
     squares = lax.psum(lax.psum(jnp.sum(hidden * hidden, axis=1), "xhi"), "z")
     normed = (hidden * lax.rsqrt(squares[:, None] / D + 1e-05) * gain[None, :]).astype(jnp.bfloat16)

time: 278 us -> 247 us (0.89)
  waiting for transfers between devices: 197 us -> 158 us
  starting transfers between devices: 4.8 us -> 13.1 us
  blocking collectives: 33.8 us -> 28.7 us
    all_gather x2 -> x1, waiting for transfers between devices: 132 us -> 44.1 us  [on_device(): lax.all_gather(z_ring_block(out_weight), GROUP, axis=0)]
    all_to_all x0 -> x1, waiting for transfers between devices: none -> 74.2 us  [on_device(): lax.all_to_all(partial.astype(jnp.bfloat16), 'z', 1, 1, tiled=True)]
    ppermute x1, waiting for transfers between devices: 31.9 us -> 7.06 us  [z_ring_block(): return lax.ppermute(block, GROUP + TENSOR, route)]
    all_to_all x0 -> x1, starting transfers between devices: none -> 6.86 us  [on_device(): lax.all_to_all(partial.astype(jnp.bfloat16), 'z', 1, 1, tiled=True)]
    psum x2, blocking collectives: 19 us -> 15.9 us  [on_device(): squares = lax.psum(lax.psum(jnp.sum(hidden * hidden, axis=1), 'xhi'), 'z')]
  transfers between devices with their start and end apart: 4 -> 4, of which waited for: 4 -> 4; matrix products, arithmetic and copies ran while one was open for 0% -> 1% of each run, Pallas kernels for 0% -> 0%
where the time goes in v5:
time: 247 us; the launch traced here: 246 us
  waiting for transfers between devices  158 us (64%)
  blocking collectives  28.7 us (12%)
  between operations  18.6 us (8%)
  matrix products  17.4 us (7%)
  starting transfers between devices  13.1 us (5%)
  local copies, waits for them, and re-layouts  7.48 us (3%)
  other arithmetic  2.76 us (1%)
    all_to_all x1, waiting for transfers between devices, on_device(): lax.all_to_all(partial.astype(jnp.bfloat16), 'z', 1, 1, tiled=True)  74.2 us
    all_gather x1, waiting for transfers between devices, on_device(): lax.all_gather(z_ring_block(out_weight), GROUP, axis=0)  44.1 us
    all_gather x1, waiting for transfers between devices, on_device(): story = lax.all_gather(binned, GROUP, axis=0, tiled=True)  32.9 us
    psum x2, blocking collectives, on_device(): squares = lax.psum(lax.psum(jnp.sum(hidden * hidden, axis=1), 'xhi'), 'z')  15.9 us
    all_gather x1, blocking collectives, on_device(): slab = lax.all_gather(attention, 'xhi', axis=1, tiled=True)  12.7 us
    dot_general x1, matrix products, on_device(): jnp.einsum('ich,zchf->izf', slab.reshape(-1, xs, heads), blocks, preferre...  8.5 us
    dot_general x1, matrix products, on_device(): lax.dot_general(lagged, responses, contract, preferred_element_type=jnp.f...  7.88 us
    ppermute x1, waiting for transfers between devices, z_ring_block(): return lax.ppermute(block, GROUP + TENSOR, route)  7.06 us
  transfers between devices with their start and end apart: 4, of which 4 were waited for; matrix products, arithmetic and copies ran while one was open for 1% of the time, Pallas kernels for 0%

profile of v5, /device:TPU:1, one launch (start us, length us, event | category | flops | bytes accessed | tf_op | source)
XLA Modules:
  0.0 246.2 jit_solution(5074529129434377182)
XLA Ops:
  6.5 6.1 %collective-permute-start = (bf16[512,512]{1,0:T(8,128)(2,1)}, bf16[512,512]{1,0:T(8,128)(2,1)S(1)}, u32[]{:S(2)}, u32[]{:S(2)}) collective-permute-start(bf16[512,512]{1,0:T(8,128)(2,1)} %param.8), channel_id=1, source_target_pairs={{0,0},{16,1},{2,2},{18,3},{4,4},{20,5},{6,6},{22,7},{8,8},{24,9},{... | collective-permute-start | bytes 1572872 | tf_op jit(solution)/shard_map/ppermute | solution.py:23
  12.7 7.1 %collective-permute-done = bf16[512,512]{1,0:T(8,128)(2,1)S(1)} collective-permute-done((bf16[512,512]{1,0:T(8,128)(2,1)}, bf16[512,512]{1,0:T(8,128)(2,1)S(1)}, u32[]{:S(2)}, u32[]{:S(2)}) %collective-permute-start) | collective-permute-done | bytes 524320 | tf_op jit(solution)/shard_map/ppermute | solution.py:23
  19.8 0.8 copy-done.1
  20.6 0.0 all-gather.6.cloned.1.call-update
  20.6 1.2 copy.10
  21.8 12.7 %all_gather.12 = bf16[384,1024]{0,1:T(8,128)(2,1)S(1)} all-gather(bf16[384,512]{0,1:T(8,128)(2,1)S(1)} %copy.10), channel_id=1, replica_groups=mesh['xlo'=2,'y'=4,'core'=2,'z'=8,'xhi'=2] {'xhi'}, dimensions={1}, use_global_device_ids=true | all-gather | bytes 1179648 | tf_op jit(solution)/shard_map/all_gather | solution.py:30
  34.5 44.1 %all-gather.6.cloned.1.call-done = bf16[8192,512]{1,0:T(8,128)(2,1)} async-done(((bf16[512,512]{1,0:T(8,128)(2,1)}), bf16[8192,512]{1,0:T(8,128)(2,1)}) %all-gather.6.cloned.1.call-update) | async-done | bytes 8388624 | tf_op jit(solution)/shard_map/all_gather | solution.py:31
  78.6 8.5 %bitcast_convert_fusion = bf16[384,8,512]{2,0,1:T(8,128)(2,1)} fusion(bf16[384,2,512,1]{0,2,1,3:T(8,128)(2,1)S(1)} %bitcast.19, bf16[8,2,512,512]{3,2,1,0:T(8,128)(2,1)} %bitcast.20), kind=kOutput, calls=%fused_computation.8 | convolution fusion | flops 3222798336 | bytes 12320768 | tf_op jit(solution)/shard_map/ich,zchf->izf/dot_general | solution.py:32
  87.1 6.9 %all-to-all-start = ((bf16[384,8,512]{2,0,1:T(8,128)(2,1)}), bf16[384,8,512]{2,0,1:T(8,128)(2,1)}, u32[]{:S(2)}, u32[]{:S(2)}) async-start(bf16[384,8,512]{2,0,1:T(8,128)(2,1)} %bitcast_convert_fusion), calls=%async_computation | async-start | bytes 6291456 | tf_op jit(solution)/shard_map/all_to_all | solution.py:35
  94.0 0.0 copy-start.5
  94.0 0.0 all-gather.4.cloned.1.call-start
  94.1 0.1 convert_reduce_fusion.1
  94.2 0.0 copy-start.3
  94.2 74.2 %all-to-all-done = bf16[384,8,512]{2,0,1:T(8,128)(2,1)} async-done(((bf16[384,8,512]{2,0,1:T(8,128)(2,1)}), bf16[384,8,512]{2,0,1:T(8,128)(2,1)}, u32[]{:S(2)}, u32[]{:S(2)}) %all-to-all-start) | async-done | bytes 3145760 | tf_op jit(solution)/shard_map/all_to_all | solution.py:35
  168.4 2.4 convert_reduce_fusion
  170.8 0.2 multiply_reduce_fusion
  171.0 5.3 %psum.14 = f32[384]{0:T(512)S(1)} all-reduce(f32[384]{0:T(512)S(1)} %multiply_reduce_fusion), channel_id=1, replica_groups=mesh['xlo'=2,'y'=4,'core'=2,'z'=8,'xhi'=2] {'xhi'}, use_global_device_ids=true, to_apply=%region_2.0 | all-reduce | flops 384 | bytes 3072 | tf_op jit(solution)/shard_map/psum | solution.py:38
  176.3 10.7 %psum.15 = f32[384]{0:T(512)S(1)} all-reduce(f32[384]{0:T(512)S(1)} %psum.14), channel_id=1, replica_groups=mesh['xlo'=2,'y'=4,'core'=2,'z'=8,'xhi'=2] {'z'}, use_global_device_ids=true, to_apply=%region_3.0 | all-reduce | flops 384 | bytes 3072 | tf_op jit(solution)/shard_map/psum | solution.py:38
  187.0 1.0 fusion.11
  187.9 0.0 all-gather.4.cloned.1.call-update
  188.0 0.7 fusion.16
  193.8 32.9 %all-gather.4.cloned.1.call-done = bf16[1536,512]{1,0:T(8,128)(2,1)} async-done(((bf16[96,512]{1,0:T(8,128)(2,1)}), bf16[1536,512]{1,0:T(8,128)(2,1)}) %all-gather.4.cloned.1.call-update) | async-done | bytes 1572880 | tf_op jit(solution)/shard_map/all_gather | solution.py:47
  226.7 4.8 %pad_dynamic-slice_fusion.3 = (bf16[1536,512]{1,0:T(8,128)(2,1)S(1)}, bf16[1536,512]{1,0:T(8,128)(2,1)S(1)}, bf16[1536,512]{1,0:T(8,128)(2,1)S(1)}, bf16[1536,512]{1,0:T(8,128)(2,1)S(1)}) fusion(s32[]{:T(128)S(6)} %select_n.12, bf16[1536,512]{1,0:T(8,128)(2,1)} %all-gather.4.cloned.1.call-done, s32[]{:T(128)S(6)} %select_n.13, s32[]{:T(128)S(6)} %select_n.14, ...), kind=kLoop, calls=%fused_computation.16 | loop fusion | bytes 7864336 | tf_op jit(solution)/shard_map/dynamic_slice | solution.py:52
  231.5 7.9 %fusion.8 = f32[2048,640]{1,0:T(8,128)} fusion(bf16[1536,640]{1,0:T(8,128)(2,1)S(1)} %copy-done, bf16[1536,512]{1,0:T(8,128)(2,1)S(1)} %get-tuple-element.8, bf16[1536,512]{1,0:T(8,128)(2,1)S(1)} %get-tuple-element.7, bf16[1536,512]{1,0:T(8,128)(2,1)S(1)} %get-tuple-element.6, bf16[1536,512]{1,0:T(8,128)(2,1)S(1)} %get-tuple-element.5), kind=kOutput, calls=%fused_computation.10 | convolution fusion | flops 4053008384 | bytes 13500416 | tf_op jit(solution)/shard_map/dot_general | solution.py:55
  (12 shorter events, 0.0 us)
Async XLA Ops:
  6.5 224.9 %copy-start = (bf16[1536,640]{1,0:T(8,128)(2,1)S(1)}, bf16[1536,640]{1,0:T(8,128)(2,1)}, u32[]{:S(2)}) copy-start(bf16[1536,640]{1,0:T(8,128)(2,1)} %param.13) | copy-start | bytes 5898244
  6.5 72.1 %all-gather.6.cloned.1.call-start = ((), (), s32[]{:S(2)}) async-start(), calls=%async_computation.2 | async-start | bytes 8912896 | tf_op jit(solution)/shard_map/all_gather | solution.py:31
  6.5 13.2 %collective-permute-start = (bf16[512,512]{1,0:T(8,128)(2,1)}, bf16[512,512]{1,0:T(8,128)(2,1)S(1)}, u32[]{:S(2)}, u32[]{:S(2)}) collective-permute-start(bf16[512,512]{1,0:T(8,128)(2,1)} %param.8), channel_id=1, source_target_pairs={{0,0},{16,1},{2,2},{18,3},{4,4},{20,5},{6,6},{22,7},{8,8},{24,9},{... | collective-permute-start | bytes 1572872 | tf_op jit(solution)/shard_map/ppermute | solution.py:23
  19.8 0.8 copy-start.1
  87.1 6.9 %copy-start.4 = (s32[1,384]{1,0:T(1,128)S(1)}, s32[1,384]{1,0:T(1,128)}, u32[]{:S(2)}) copy-start(s32[1,384]{1,0:T(1,128)} %param.11) | copy-start | bytes 4612
  87.1 81.2 %all-to-all-start = ((bf16[384,8,512]{2,0,1:T(8,128)(2,1)}), bf16[384,8,512]{2,0,1:T(8,128)(2,1)}, u32[]{:S(2)}, u32[]{:S(2)}) async-start(bf16[384,8,512]{2,0,1:T(8,128)(2,1)} %bitcast_convert_fusion), calls=%async_computation | async-start | bytes 6291456 | tf_op jit(solution)/shard_map/all_to_all | solution.py:35
  94.0 76.8 %copy-start.2 = (bf16[384,512]{1,0:T(8,128)(2,1)S(1)}, bf16[384,512]{1,0:T(8,128)(2,1)}, u32[]{:S(2)}) copy-start(bf16[384,512]{1,0:T(8,128)(2,1)} %param.9) | copy-start | bytes 1179652
  94.0 93.0 %copy-start.5 = (f32[512]{0:T(512)S(1)}, f32[512]{0:T(512)}, u32[]{:S(2)}) copy-start(f32[512]{0:T(512)} %param.10) | copy-start | bytes 6148
  94.0 132.7 %all-gather.4.cloned.1.call-start = ((), (), s32[]{:S(2)}) async-start(), calls=%async_computation.1 | async-start | bytes 1671168 | tf_op jit(solution)/shard_map/all_gather | solution.py:47
  94.2 93.8 %copy-start.3 = (s32[4]{0:T(128)S(1)}, s32[4]{0:T(128)}, u32[]{:S(2)}) copy-start(s32[4]{0:T(128)} %param.12) | copy-start | bytes 52
Sparse Core Ops, SparseCore 0:
  20.7 57.8 all-gather.5
  188.1 38.5 all-gather.3

commit v6 on v5

--- a/solution.py
+++ b/solution.py
@@ -35,7 +35,7 @@
     received = lax.all_to_all(partial.astype(jnp.bfloat16), "z", 1, 1, tiled=True)
     summed = jnp.sum(received.astype(jnp.float32), axis=1)
     hidden = residual.astype(jnp.float32) + summed
-    squares = lax.psum(lax.psum(jnp.sum(hidden * hidden, axis=1), "xhi"), "z")
+    squares = jnp.sum(lax.all_gather(jnp.sum(hidden * hidden, axis=1), TENSOR, axis=0), axis=0)
     normed = (hidden * lax.rsqrt(squares[:, None] / D + 1e-05) * gain[None, :]).astype(jnp.bfloat16)
     member = jnp.arange(R_DEV, dtype=jnp.int32)[:, None] == token_tr[0][None, :]
     counts = jnp.sum(member.astype(jnp.float32), axis=1, keepdims=True)

time: 247 us -> 261 us (1.057)
  blocking collectives: 28.7 us -> 44.3 us
    all_gather x0 -> x1, blocking collectives: none -> 31.6 us  [on_device(): lax.all_gather(jnp.sum(hidden * hidden, axis=1), TENSOR, axis=0)]
    psum x2 -> x0, blocking collectives: 15.9 us -> none  [on_device(): squares = lax.psum(lax.psum(jnp.sum(hidden * hidden, axis=1), 'xhi'), 'z')]
where the time goes in v6:
time: 261 us; the launch traced here: 260 us
  waiting for transfers between devices  157 us (60%)
  blocking collectives  44.3 us (17%)
  between operations  18.6 us (7%)
  matrix products  17.4 us (7%)
  starting transfers between devices  13.1 us (5%)
  local copies, waits for them, and re-layouts  7.5 us (3%)
  other arithmetic  2.8 us (1%)
    all_to_all x1, waiting for transfers between devices, on_device(): lax.all_to_all(partial.astype(jnp.bfloat16), 'z', 1, 1, tiled=True)  74.2 us
    all_gather x1, waiting for transfers between devices, on_device(): lax.all_gather(z_ring_block(out_weight), GROUP, axis=0)  44.1 us
    all_gather x1, blocking collectives, on_device(): lax.all_gather(jnp.sum(hidden * hidden, axis=1), TENSOR, axis=0)  31.6 us
    all_gather x1, waiting for transfers between devices, on_device(): story = lax.all_gather(binned, GROUP, axis=0, tiled=True)  31.3 us
    all_gather x1, blocking collectives, on_device(): slab = lax.all_gather(attention, 'xhi', axis=1, tiled=True)  12.7 us
    dot_general x1, matrix products, on_device(): jnp.einsum('ich,zchf->izf', slab.reshape(-1, xs, heads), blocks, preferre...  8.5 us
    dot_general x1, matrix products, on_device(): lax.dot_general(lagged, responses, contract, preferred_element_type=jnp.f...  7.88 us
    ppermute x1, waiting for transfers between devices, z_ring_block(): return lax.ppermute(block, GROUP + TENSOR, route)  7.06 us
  transfers between devices with their start and end apart: 4, of which 4 were waited for; matrix products, arithmetic and copies ran while one was open for 1% of the time, Pallas kernels for 0%

profile of v6, /device:TPU:1, one launch (start us, length us, event | category | flops | bytes accessed | tf_op | source)
XLA Modules:
  0.0 260.3 jit_solution(18060427075221595889)
XLA Ops:
  6.5 0.0 all-gather.8.cloned.1.call-start
  6.5 6.1 %collective-permute-start = (bf16[512,512]{1,0:T(8,128)(2,1)}, bf16[512,512]{1,0:T(8,128)(2,1)S(1)}, u32[]{:S(2)}, u32[]{:S(2)}) collective-permute-start(bf16[512,512]{1,0:T(8,128)(2,1)} %param.8), channel_id=1, source_target_pairs={{0,0},{16,1},{2,2},{18,3},{4,4},{20,5},{6,6},{22,7},{8,8},{24,9},{... | collective-permute-start | bytes 1572872 | tf_op jit(solution)/shard_map/ppermute | solution.py:23
  12.7 7.1 %collective-permute-done = bf16[512,512]{1,0:T(8,128)(2,1)S(1)} collective-permute-done((bf16[512,512]{1,0:T(8,128)(2,1)}, bf16[512,512]{1,0:T(8,128)(2,1)S(1)}, u32[]{:S(2)}, u32[]{:S(2)}) %collective-permute-start) | collective-permute-done | bytes 524320 | tf_op jit(solution)/shard_map/ppermute | solution.py:23
  19.8 0.8 copy-done.1
  20.6 0.0 all-gather.8.cloned.1.call-update
  20.6 1.2 copy.12
  21.8 12.7 %all_gather.18 = bf16[384,1024]{0,1:T(8,128)(2,1)S(1)} all-gather(bf16[384,512]{0,1:T(8,128)(2,1)S(1)} %copy.12), channel_id=1, replica_groups=mesh['xlo'=2,'y'=4,'core'=2,'z'=8,'xhi'=2] {'xhi'}, dimensions={1}, use_global_device_ids=true | all-gather | bytes 1179648 | tf_op jit(solution)/shard_map/all_gather | solution.py:30
  34.5 44.1 %all-gather.8.cloned.1.call-done = bf16[8192,512]{1,0:T(8,128)(2,1)} async-done(((bf16[512,512]{1,0:T(8,128)(2,1)}), bf16[8192,512]{1,0:T(8,128)(2,1)}) %all-gather.8.cloned.1.call-update) | async-done | bytes 8388624 | tf_op jit(solution)/shard_map/all_gather | solution.py:31
  78.6 8.5 %bitcast_convert_fusion = bf16[384,8,512]{2,0,1:T(8,128)(2,1)} fusion(bf16[384,2,512,1]{0,2,1,3:T(8,128)(2,1)S(1)} %bitcast.19, bf16[8,2,512,512]{3,2,1,0:T(8,128)(2,1)} %bitcast.20), kind=kOutput, calls=%fused_computation.8 | convolution fusion | flops 3222798336 | bytes 12320768 | tf_op jit(solution)/shard_map/ich,zchf->izf/dot_general | solution.py:32
  87.1 6.9 %all-to-all-start = ((bf16[384,8,512]{2,0,1:T(8,128)(2,1)}), bf16[384,8,512]{2,0,1:T(8,128)(2,1)}, u32[]{:S(2)}, u32[]{:S(2)}) async-start(bf16[384,8,512]{2,0,1:T(8,128)(2,1)} %bitcast_convert_fusion), calls=%async_computation | async-start | bytes 6291456 | tf_op jit(solution)/shard_map/all_to_all | solution.py:35
  94.0 0.0 copy-start.5
  94.0 0.0 all-gather.6.cloned.1.call-start
  94.1 0.1 convert_reduce_fusion.1
  94.2 0.0 copy-start.3
  94.2 74.2 %all-to-all-done = bf16[384,8,512]{2,0,1:T(8,128)(2,1)} async-done(((bf16[384,8,512]{2,0,1:T(8,128)(2,1)}), bf16[384,8,512]{2,0,1:T(8,128)(2,1)}, u32[]{:S(2)}, u32[]{:S(2)}) %all-to-all-start) | async-done | bytes 3145760 | tf_op jit(solution)/shard_map/all_to_all | solution.py:35
  168.4 2.4 convert_reduce_fusion
  170.8 0.2 multiply_reduce_fusion
  171.0 31.6 %all-gather.2 = f32[16,1,384]{2,1,0:T(1,128)S(1)} all-gather(f32[1,1,384]{2,1,0:T(1,128)S(1)} %reshape.41), channel_id=3, replica_groups=mesh['xlo'=2,'y'=4,'core'=2,'z'=8,'xhi'=2] {'z','xhi'}, dimensions={0}, use_global_device_ids=true | all-gather | bytes 26112 | tf_op jit(solution)/shard_map/all_gather | solution.py:38
  202.6 1.0 fusion.11
  203.6 0.0 all-gather.6.cloned.1.call-update
  203.7 0.7 fusion.16
  209.4 31.3 %all-gather.6.cloned.1.call-done = bf16[1536,512]{1,0:T(8,128)(2,1)} async-done(((bf16[96,512]{1,0:T(8,128)(2,1)}), bf16[1536,512]{1,0:T(8,128)(2,1)}) %all-gather.6.cloned.1.call-update) | async-done | bytes 1572880 | tf_op jit(solution)/shard_map/all_gather | solution.py:47
  240.8 4.8 %pad_dynamic-slice_fusion.3 = (bf16[1536,512]{1,0:T(8,128)(2,1)S(1)}, bf16[1536,512]{1,0:T(8,128)(2,1)S(1)}, bf16[1536,512]{1,0:T(8,128)(2,1)S(1)}, bf16[1536,512]{1,0:T(8,128)(2,1)S(1)}) fusion(s32[]{:T(128)S(6)} %select_n.12, bf16[1536,512]{1,0:T(8,128)(2,1)} %all-gather.6.cloned.1.call-done, s32[]{:T(128)S(6)} %select_n.13, s32[]{:T(128)S(6)} %select_n.14, ...), kind=kLoop, calls=%fused_computation.16 | loop fusion | bytes 7864336 | tf_op jit(solution)/shard_map/dynamic_slice | solution.py:52
  245.6 7.9 %fusion.8 = f32[2048,640]{1,0:T(8,128)} fusion(bf16[1536,640]{1,0:T(8,128)(2,1)S(1)} %copy-done, bf16[1536,512]{1,0:T(8,128)(2,1)S(1)} %get-tuple-element.8, bf16[1536,512]{1,0:T(8,128)(2,1)S(1)} %get-tuple-element.7, bf16[1536,512]{1,0:T(8,128)(2,1)S(1)} %get-tuple-element.6, bf16[1536,512]{1,0:T(8,128)(2,1)S(1)} %get-tuple-element.5), kind=kOutput, calls=%fused_computation.10 | convolution fusion | flops 4053008384 | bytes 13500416 | tf_op jit(solution)/shard_map/dot_general | solution.py:55
  (13 shorter events, 0.1 us)
Async XLA Ops:
  6.5 239.0 %copy-start = (bf16[1536,640]{1,0:T(8,128)(2,1)S(1)}, bf16[1536,640]{1,0:T(8,128)(2,1)}, u32[]{:S(2)}) copy-start(bf16[1536,640]{1,0:T(8,128)(2,1)} %param.13) | copy-start | bytes 5898244
  6.5 72.1 %all-gather.8.cloned.1.call-start = ((), (), s32[]{:S(2)}) async-start(), calls=%async_computation.2 | async-start | bytes 8912896 | tf_op jit(solution)/shard_map/all_gather | solution.py:31
  6.5 13.2 %collective-permute-start = (bf16[512,512]{1,0:T(8,128)(2,1)}, bf16[512,512]{1,0:T(8,128)(2,1)S(1)}, u32[]{:S(2)}, u32[]{:S(2)}) collective-permute-start(bf16[512,512]{1,0:T(8,128)(2,1)} %param.8), channel_id=1, source_target_pairs={{0,0},{16,1},{2,2},{18,3},{4,4},{20,5},{6,6},{22,7},{8,8},{24,9},{... | collective-permute-start | bytes 1572872 | tf_op jit(solution)/shard_map/ppermute | solution.py:23
  19.8 0.8 copy-start.1
  87.1 6.9 %copy-start.4 = (s32[1,384]{1,0:T(1,128)S(1)}, s32[1,384]{1,0:T(1,128)}, u32[]{:S(2)}) copy-start(s32[1,384]{1,0:T(1,128)} %param.11) | copy-start | bytes 4612
  87.1 81.2 %all-to-all-start = ((bf16[384,8,512]{2,0,1:T(8,128)(2,1)}), bf16[384,8,512]{2,0,1:T(8,128)(2,1)}, u32[]{:S(2)}, u32[]{:S(2)}) async-start(bf16[384,8,512]{2,0,1:T(8,128)(2,1)} %bitcast_convert_fusion), calls=%async_computation | async-start | bytes 6291456 | tf_op jit(solution)/shard_map/all_to_all | solution.py:35
  94.0 76.8 %copy-start.2 = (bf16[384,512]{1,0:T(8,128)(2,1)S(1)}, bf16[384,512]{1,0:T(8,128)(2,1)}, u32[]{:S(2)}) copy-start(bf16[384,512]{1,0:T(8,128)(2,1)} %param.9) | copy-start | bytes 1179652
  94.0 108.6 %copy-start.5 = (f32[512]{0:T(512)S(1)}, f32[512]{0:T(512)}, u32[]{:S(2)}) copy-start(f32[512]{0:T(512)} %param.10) | copy-start | bytes 6148
  94.0 146.7 %all-gather.6.cloned.1.call-start = ((), (), s32[]{:S(2)}) async-start(), calls=%async_computation.1 | async-start | bytes 1671168 | tf_op jit(solution)/shard_map/all_gather | solution.py:47
  94.2 109.4 %copy-start.3 = (s32[4]{0:T(128)S(1)}, s32[4]{0:T(128)}, u32[]{:S(2)}) copy-start(s32[4]{0:T(128)} %param.12) | copy-start | bytes 52
Sparse Core Ops, SparseCore 0:
  20.7 57.8 all-gather.7
  203.8 36.9 all-gather.5

commit v7 on v6

--- a/solution.py
+++ b/solution.py
@@ -7,35 +7,35 @@
 LAGS = 4
 R_DEV = 96
 GROUP = ("xlo", "y", "core")
-TENSOR = ("z", "xhi")
+TENSOR = ("zhi", "zlo", "xhi")
 
 
-def z_ring_block(block):
+def ring_block(block):
     groups = lax.axis_size(GROUP)
     tensors = lax.axis_size(TENSOR)
-    xs = lax.axis_size("xhi")
+    quad = lax.axis_size(("zlo", "xhi"))
     route = []
     for g in range(groups):
         for t in range(tensors):
-            z, x = t // xs, t % xs
-            source = (xs * (g // xs) + x) * tensors + xs * z + g % xs
+            ring, q = t // quad, t % quad
+            source = (quad * (g // quad) + q) * tensors + quad * ring + g % quad
             route.append((source, g * tensors + t))
     return lax.ppermute(block, GROUP + TENSOR, route)
 
 
 def on_device(attention, out_weight, residual, gain, token_tr, lag_offsets, responses):
-    xs = lax.axis_size("xhi")
-    zs = lax.axis_size("z")
+    quad = lax.axis_size(("zlo", "xhi"))
+    ring = lax.axis_size("zhi")
     heads = attention.shape[1]
-    slab = lax.all_gather(attention, "xhi", axis=1, tiled=True)
-    blocks = lax.all_gather(z_ring_block(out_weight), GROUP, axis=0).reshape(zs, xs, heads, -1)
+    slab = lax.all_gather(attention, ("zlo", "xhi"), axis=1, tiled=True)
+    blocks = lax.all_gather(ring_block(out_weight), GROUP, axis=0).reshape(ring, quad, heads, -1)
     partial = jnp.einsum(
-        "ich,zchf->izf", slab.reshape(-1, xs, heads), blocks, preferred_element_type=jnp.float32
+        "iqh,rqhf->irf", slab.reshape(-1, quad, heads), blocks, preferred_element_type=jnp.float32
     )
-    received = lax.all_to_all(partial.astype(jnp.bfloat16), "z", 1, 1, tiled=True)
+    received = lax.all_to_all(partial.astype(jnp.bfloat16), "zhi", 1, 1, tiled=True)
     summed = jnp.sum(received.astype(jnp.float32), axis=1)
     hidden = residual.astype(jnp.float32) + summed
-    squares = jnp.sum(lax.all_gather(jnp.sum(hidden * hidden, axis=1), TENSOR, axis=0), axis=0)
+    squares = lax.psum(lax.psum(jnp.sum(hidden * hidden, axis=1), "xhi"), ("zhi", "zlo"))
     normed = (hidden * lax.rsqrt(squares[:, None] / D + 1e-05) * gain[None, :]).astype(jnp.bfloat16)
     member = jnp.arange(R_DEV, dtype=jnp.int32)[:, None] == token_tr[0][None, :]
     counts = jnp.sum(member.astype(jnp.float32), axis=1, keepdims=True)
@@ -58,7 +58,7 @@
 
 
 def solution(mesh):
-    parts = Mesh(mesh.devices.reshape(2, 4, 2, 8, 2), GROUP + TENSOR)
+    parts = Mesh(mesh.devices.reshape(2, 4, 2, 4, 2, 2), GROUP + TENSOR)
     return jax.shard_map(
         on_device,
         mesh=parts,

time: 261 us -> 247 us (0.946)
  blocking collectives: 44.3 us -> 16.7 us
  waiting for transfers between devices: 157 us -> 170 us
    all_gather x2 -> x0, blocking collectives: 44.3 us -> none  [the longest x1 31.6 us: on_device(): lax.all_gather(jnp.sum(hidden * hidden, axis=1), TENSOR, axis=0)]
    all_gather x1 -> x2, waiting for transfers between devices: 44.1 us -> 86.4 us  [the longest x1 57.9 us: on_device(): lax.all_gather(ring_block(out_weight), GROUP, axis=0)]
    all_to_all x1, waiting for transfers between devices: 74.2 us -> 37.2 us  [on_device(): lax.all_to_all(partial.astype(jnp.bfloat16), 'zhi', 1, 1, tiled=True)]
    psum x0 -> x2, blocking collectives: none -> 16.7 us  [the longest x1 11.4 us: on_device(): lax.psum(lax.psum(jnp.sum(hidden * hidden, axis=1), 'xhi'), ('zhi', 'zlo'))]
    all_gather x1, waiting for transfers between devices: 31.3 us -> 36 us  [on_device(): story = lax.all_gather(binned, GROUP, axis=0, tiled=True)]
    ppermute x1, waiting for transfers between devices: 7.06 us -> 10.8 us  [ring_block(): return lax.ppermute(block, GROUP + TENSOR, route)]
  transfers between devices with their start and end apart: 4 -> 5, of which waited for: 4 -> 5; matrix products, arithmetic and copies ran while one was open for 1% -> 0% of each run, Pallas kernels for 0% -> 0%
where the time goes in v7:
time: 247 us; the launch traced here: 246 us
  waiting for transfers between devices  170 us (69%)
  matrix products  18.5 us (7%)
  between operations  18.1 us (7%)
  blocking collectives  16.7 us (7%)
  starting transfers between devices  12.9 us (5%)
  local copies, waits for them, and re-layouts  9.18 us (4%)
    all_gather x1, waiting for transfers between devices, on_device(): lax.all_gather(ring_block(out_weight), GROUP, axis=0)  57.9 us
    all_to_all x1, waiting for transfers between devices, on_device(): lax.all_to_all(partial.astype(jnp.bfloat16), 'zhi', 1, 1, tiled=True)  37.2 us
    all_gather x1, waiting for transfers between devices, on_device(): story = lax.all_gather(binned, GROUP, axis=0, tiled=True)  36 us
    all_gather x1, waiting for transfers between devices, on_device(): slab = lax.all_gather(attention, ('zlo', 'xhi'), axis=1, tiled=True)  28.5 us
    psum x1, blocking collectives, on_device(): lax.psum(lax.psum(jnp.sum(hidden * hidden, axis=1), 'xhi'), ('zhi', 'zlo'))  11.4 us
    ppermute x1, waiting for transfers between devices, ring_block(): return lax.ppermute(block, GROUP + TENSOR, route)  10.8 us
    dot_general x1, matrix products, on_device(): jnp.einsum('iqh,rqhf->irf', slab.reshape(-1, quad, heads), blocks, prefer...  8.47 us
    dot_general x1, matrix products, on_device(): lax.dot_general(lagged, responses, contract, preferred_element_type=jnp.f...  7.88 us
  transfers between devices with their start and end apart: 5, of which 5 were waited for; matrix products, arithmetic and copies ran while one was open for 0% of the time, Pallas kernels for 0%

profile of v7, /device:TPU:1, one launch (start us, length us, event | category | flops | bytes accessed | tf_op | source)
XLA Modules:
  0.0 246.4 jit_solution(12800013740493513069)
XLA Ops:
  6.5 2.1 copy.10
  8.6 0.0 all-gather.5.cloned.1.call-update
  8.6 0.0 all-gather.9.cloned.1.call-start
  8.7 6.0 %collective-permute-start = (bf16[512,512]{1,0:T(8,128)(2,1)}, bf16[512,512]{1,0:T(8,128)(2,1)S(1)}, u32[]{:S(2)}, u32[]{:S(2)}) collective-permute-start(bf16[512,512]{1,0:T(8,128)(2,1)} %param.8), channel_id=1, source_target_pairs={{0,0},{16,1},{32,2},{48,3},{4,4},{20,5},{36,6},{52,7},{8,8},{24,9}... | collective-permute-start | bytes 1572872 | tf_op jit(solution)/shard_map/ppermute | solution.py:23
  14.7 10.8 %collective-permute-done = bf16[512,512]{1,0:T(8,128)(2,1)S(1)} collective-permute-done((bf16[512,512]{1,0:T(8,128)(2,1)}, bf16[512,512]{1,0:T(8,128)(2,1)S(1)}, u32[]{:S(2)}, u32[]{:S(2)}) %collective-permute-start) | collective-permute-done | bytes 524320 | tf_op jit(solution)/shard_map/ppermute | solution.py:23
  25.5 0.8 copy-done.2
  26.3 0.0 all-gather.9.cloned.1.call-update
  26.4 28.5 %all-gather.5.cloned.1.call-done = bf16[384,2048]{0,1:T(8,128)(2,1)} async-done(((bf16[384,512]{0,1:T(8,128)(2,1)}), bf16[384,2048]{0,1:T(8,128)(2,1)}) %all-gather.5.cloned.1.call-update) | async-done | bytes 1572880 | tf_op jit(solution)/shard_map/all_gather | solution.py:30
  54.9 57.9 %all-gather.9.cloned.1.call-done = bf16[8192,512]{1,0:T(8,128)(2,1)} async-done(((bf16[512,512]{1,0:T(8,128)(2,1)}), bf16[8192,512]{1,0:T(8,128)(2,1)}) %all-gather.9.cloned.1.call-update) | async-done | bytes 8388624 | tf_op jit(solution)/shard_map/all_gather | solution.py:31
  112.8 8.5 %bitcast_convert_fusion = bf16[384,4,512]{2,0,1:T(8,128)(2,1)} fusion(bf16[384,4,512,1]{0,2,1,3:T(8,128)(2,1)} %bitcast.20, bf16[4,4,512,512]{3,2,1,0:T(8,128)(2,1)} %bitcast.19), kind=kOutput, calls=%fused_computation.9 | convolution fusion | flops 3222011904 | bytes 11534336 | tf_op jit(solution)/shard_map/iqh,rqhf->irf/dot_general | solution.py:32
  121.3 6.9 %all-to-all-start = ((bf16[384,4,512]{2,0,1:T(8,128)(2,1)}), bf16[384,4,512]{2,0,1:T(8,128)(2,1)S(1)}, u32[]{:S(2)}, u32[]{:S(2)}) async-start(bf16[384,4,512]{2,0,1:T(8,128)(2,1)} %bitcast_convert_fusion), calls=%async_computation | async-start | bytes 3145728 | tf_op jit(solution)/shard_map/all_to_all | solution.py:35
  128.2 0.1 convert_reduce_fusion.1
  128.3 37.2 %all-to-all-done = bf16[384,4,512]{2,0,1:T(8,128)(2,1)S(1)} async-done(((bf16[384,4,512]{2,0,1:T(8,128)(2,1)}), bf16[384,4,512]{2,0,1:T(8,128)(2,1)S(1)}, u32[]{:S(2)}, u32[]{:S(2)}) %all-to-all-start) | async-done | bytes 1572896 | tf_op jit(solution)/shard_map/all_to_all | solution.py:35
  165.5 0.2 convert_reduce_fusion
  165.7 0.9 copy-done.1
  166.6 0.2 multiply_reduce_fusion
  166.8 5.3 %psum.14 = f32[384]{0:T(512)S(1)} all-reduce(f32[384]{0:T(512)S(1)} %multiply_reduce_fusion), channel_id=1, replica_groups=mesh['xlo'=2,'y'=4,'core'=2,'zhi'=4,'zlo'=2,'xhi'=2] {'xhi'}, use_global_device_ids=true, to_apply=%region_2.0 | all-reduce | flops 384 | bytes 3072 | tf_op jit(solution)/shard_map/psum | solution.py:38
  172.0 11.4 %psum.15 = f32[384]{0:T(512)S(1)} all-reduce(f32[384]{0:T(512)S(1)} %psum.14), channel_id=1, replica_groups=mesh['xlo'=2,'y'=4,'core'=2,'zhi'=4,'zlo'=2,'xhi'=2] {'zhi','zlo'}, use_global_device_ids=true, to_apply=%region_3.0 | all-reduce | flops 384 | bytes 3072 | tf_op jit(solution)/shard_map/psum | solution.py:38
  183.5 2.2 fusion.11
  185.6 0.0 all-gather.7.cloned.1.call-update
  185.7 0.6 fusion.16
  191.2 36.0 %all-gather.7.cloned.1.call-done = bf16[1536,512]{1,0:T(8,128)(2,1)} async-done(((bf16[96,512]{1,0:T(8,128)(2,1)}), bf16[1536,512]{1,0:T(8,128)(2,1)}) %all-gather.7.cloned.1.call-update) | async-done | bytes 1572880 | tf_op jit(solution)/shard_map/all_gather | solution.py:47
  227.2 4.8 %pad_dynamic-slice_fusion.3 = (bf16[1536,512]{1,0:T(8,128)(2,1)S(1)}, bf16[1536,512]{1,0:T(8,128)(2,1)S(1)}, bf16[1536,512]{1,0:T(8,128)(2,1)S(1)}, bf16[1536,512]{1,0:T(8,128)(2,1)S(1)}) fusion(s32[]{:T(128)S(6)} %select_n.12, bf16[1536,512]{1,0:T(8,128)(2,1)} %all-gather.7.cloned.1.call-done, s32[]{:T(128)S(6)} %select_n.13, s32[]{:T(128)S(6)} %select_n.14, ...), kind=kLoop, calls=%fused_computation.16 | loop fusion | bytes 7864336 | tf_op jit(solution)/shard_map/dynamic_slice | solution.py:52
  232.0 7.9 %fusion.8 = f32[2048,640]{1,0:T(8,128)} fusion(bf16[1536,640]{1,0:T(8,128)(2,1)S(1)} %copy-done, bf16[1536,512]{1,0:T(8,128)(2,1)S(1)} %get-tuple-element.8, bf16[1536,512]{1,0:T(8,128)(2,1)S(1)} %get-tuple-element.7, bf16[1536,512]{1,0:T(8,128)(2,1)S(1)} %get-tuple-element.6, bf16[1536,512]{1,0:T(8,128)(2,1)S(1)} %get-tuple-element.5), kind=kOutput, calls=%fused_computation.8 | convolution fusion | flops 4053008384 | bytes 13500416 | tf_op jit(solution)/shard_map/dot_general | solution.py:55
  (16 shorter events, 0.1 us)
Async XLA Ops:
  6.5 225.5 %copy-start = (bf16[1536,640]{1,0:T(8,128)(2,1)S(1)}, bf16[1536,640]{1,0:T(8,128)(2,1)}, u32[]{:S(2)}) copy-start(bf16[1536,640]{1,0:T(8,128)(2,1)} %param.13) | copy-start | bytes 5898244
  6.5 48.4 %all-gather.5.cloned.1.call-start = ((), (), s32[]{:S(2)}) async-start(), calls=%async_computation.1 | async-start | bytes 1966080 | tf_op jit(solution)/shard_map/all_gather | solution.py:30
  8.6 104.2 %all-gather.9.cloned.1.call-start = ((), (), s32[]{:S(2)}) async-start(), calls=%async_computation.3 | async-start | bytes 8912896 | tf_op jit(solution)/shard_map/all_gather | solution.py:31
  8.7 16.9 %collective-permute-start = (bf16[512,512]{1,0:T(8,128)(2,1)}, bf16[512,512]{1,0:T(8,128)(2,1)S(1)}, u32[]{:S(2)}, u32[]{:S(2)}) collective-permute-start(bf16[512,512]{1,0:T(8,128)(2,1)} %param.8), channel_id=1, source_target_pairs={{0,0},{16,1},{32,2},{48,3},{4,4},{20,5},{36,6},{52,7},{8,8},{24,9}... | collective-permute-start | bytes 1572872 | tf_op jit(solution)/shard_map/ppermute | solution.py:23
  25.5 0.8 copy-start.2
  121.3 6.9 %copy-start.5 = (s32[1,384]{1,0:T(1,128)S(1)}, s32[1,384]{1,0:T(1,128)}, u32[]{:S(2)}) copy-start(s32[1,384]{1,0:T(1,128)} %param.11) | copy-start | bytes 4612
  121.3 44.2 %all-to-all-start = ((bf16[384,4,512]{2,0,1:T(8,128)(2,1)}), bf16[384,4,512]{2,0,1:T(8,128)(2,1)S(1)}, u32[]{:S(2)}, u32[]{:S(2)}) async-start(bf16[384,4,512]{2,0,1:T(8,128)(2,1)} %bitcast_convert_fusion), calls=%async_computation | async-start | bytes 3145728 | tf_op jit(solution)/shard_map/all_to_all | solution.py:35
  128.1 99.0 %all-gather.7.cloned.1.call-start = ((), (), s32[]{:S(2)}) async-start(), calls=%async_computation.2 | async-start | bytes 1671168 | tf_op jit(solution)/shard_map/all_gather | solution.py:47
  128.3 55.2 %copy-start.6 = (f32[512]{0:T(512)S(1)}, f32[512]{0:T(512)}, u32[]{:S(2)}) copy-start(f32[512]{0:T(512)} %param.10) | copy-start | bytes 6148
  165.5 1.1 copy-start.3
  165.7 0.9 copy-start.1
  166.6 19.1 %copy-start.4 = (s32[4]{0:T(128)S(1)}, s32[4]{0:T(128)}, u32[]{:S(2)}) copy-start(s32[4]{0:T(128)} %param.12) | copy-start | bytes 52
Sparse Core Ops, SparseCore 0:
  9.1 45.7 all-gather.4
  56.7 56.0 all-gather.8
  185.8 41.3 all-gather.6

commit v8 on v7

--- a/solution.py
+++ b/solution.py
@@ -27,7 +27,10 @@
     quad = lax.axis_size(("zlo", "xhi"))
     ring = lax.axis_size("zhi")
     heads = attention.shape[1]
-    slab = lax.all_gather(attention, ("zlo", "xhi"), axis=1, tiled=True)
+    pair = lax.all_gather(attention, "xhi", axis=1, tiled=True)
+    other = lax.ppermute(pair, "zlo", [(0, 1), (1, 0)])
+    low = lax.axis_index("zlo") == 0
+    slab = jnp.concatenate([jnp.where(low, pair, other), jnp.where(low, other, pair)], axis=1)
     blocks = lax.all_gather(ring_block(out_weight), GROUP, axis=0).reshape(ring, quad, heads, -1)
     partial = jnp.einsum(
         "iqh,rqhf->irf", slab.reshape(-1, quad, heads), blocks, preferred_element_type=jnp.float32

time: 247 us -> 218 us (0.88)
  waiting for transfers between devices: 170 us -> 125 us
  blocking collectives: 16.7 us -> 29.5 us
  starting transfers between devices: 12.9 us -> 17.4 us
    all_gather x1, waiting for transfers between devices: 57.9 us -> 23.7 us  [on_device(): lax.all_gather(ring_block(out_weight), GROUP, axis=0)]
    all_gather x1 -> x0, waiting for transfers between devices: 28.5 us -> none  [on_device(): slab = lax.all_gather(attention, ('zlo', 'xhi'), axis=1, tiled=True)]
    ppermute x0 -> x1, waiting for transfers between devices: none -> 17.9 us  [on_device(): other = lax.ppermute(pair, 'zlo', [(0, 1), (1, 0)])]
    all_gather x0 -> x1, blocking collectives: none -> 12.8 us  [on_device(): pair = lax.all_gather(attention, 'xhi', axis=1, tiled=True)]
    ppermute x0 -> x1, starting transfers between devices: none -> 4.39 us  [on_device(): other = lax.ppermute(pair, 'zlo', [(0, 1), (1, 0)])]
  transfers between devices with their start and end apart: 5 -> 5, of which waited for: 5 -> 5; matrix products, arithmetic and copies ran while one was open for 0% -> 1% of each run, Pallas kernels for 0% -> 0%
where the time goes in v8:
time: 218 us
  waiting for transfers between devices  125 us (57%)
  blocking collectives  29.5 us (14%)
  between operations  18.5 us (8%)
  matrix products  18 us (8%)
  starting transfers between devices  17.4 us (8%)
  local copies, waits for them, and re-layouts  8.39 us (4%)
    all_to_all x1, waiting for transfers between devices, on_device(): lax.all_to_all(partial.astype(jnp.bfloat16), 'zhi', 1, 1, tiled=True)  37.2 us
    all_gather x1, waiting for transfers between devices, on_device(): story = lax.all_gather(binned, GROUP, axis=0, tiled=True)  35.8 us
    all_gather x1, waiting for transfers between devices, on_device(): lax.all_gather(ring_block(out_weight), GROUP, axis=0)  23.7 us
    ppermute x1, waiting for transfers between devices, on_device(): other = lax.ppermute(pair, 'zlo', [(0, 1), (1, 0)])  17.9 us
    all_gather x1, blocking collectives, on_device(): pair = lax.all_gather(attention, 'xhi', axis=1, tiled=True)  12.8 us
    psum x1, blocking collectives, on_device(): lax.psum(lax.psum(jnp.sum(hidden * hidden, axis=1), 'xhi'), ('zhi', 'zlo'))  11.4 us
    ppermute x1, waiting for transfers between devices, ring_block(): return lax.ppermute(block, GROUP + TENSOR, route)  10.8 us
    dot_general x1, matrix products, on_device(): jnp.einsum('iqh,rqhf->irf', slab.reshape(-1, quad, heads), blocks, prefer...  7.98 us
  transfers between devices with their start and end apart: 5, of which 5 were waited for; matrix products, arithmetic and copies ran while one was open for 1% of the time, Pallas kernels for 0%

profile of v8, /device:TPU:1, one launch (start us, length us, event | category | flops | bytes accessed | tf_op | source)
XLA Modules:
  0.0 218.0 jit_solution(9678322842171168544)
XLA Ops:
  6.5 6.1 %collective-permute-start.1 = (bf16[512,512]{1,0:T(8,128)(2,1)}, bf16[512,512]{1,0:T(8,128)(2,1)S(1)}, u32[]{:S(2)}, u32[]{:S(2)}) collective-permute-start(bf16[512,512]{1,0:T(8,128)(2,1)} %param.8), channel_id=1, source_target_pairs={{0,0},{16,1},{32,2},{48,3},{4,4},{20,5},{36,6},{52,7},{8,8},{24,9}... | collective-permute-start | bytes 1572872 | tf_op jit(solution)/shard_map/ppermute | solution.py:23
  12.7 10.8 %collective-permute-done.1 = bf16[512,512]{1,0:T(8,128)(2,1)S(1)} collective-permute-done((bf16[512,512]{1,0:T(8,128)(2,1)}, bf16[512,512]{1,0:T(8,128)(2,1)S(1)}, u32[]{:S(2)}, u32[]{:S(2)}) %collective-permute-start.1) | collective-permute-done | bytes 524320 | tf_op jit(solution)/shard_map/ppermute | solution.py:23
  23.5 0.8 copy-done.2
  24.3 1.2 copy.10
  25.6 12.8 %all_gather.12 = bf16[384,1024]{0,1:T(8,128)(2,1)S(1)} all-gather(bf16[384,512]{0,1:T(8,128)(2,1)S(1)} %copy.10), channel_id=1, replica_groups=mesh['xlo'=2,'y'=4,'core'=2,'zhi'=4,'zlo'=2,'xhi'=2] {'xhi'}, dimensions={1}, use_global_device_ids=true | all-gather | bytes 1179648 | tf_op jit(solution)/shard_map/all_gather | solution.py:30
  38.3 4.4 %collective-permute-start = (bf16[384,1024]{0,1:T(8,128)(2,1)S(1)}, bf16[384,1024]{0,1:T(8,128)(2,1)S(1)}, u32[]{:S(2)}, u32[]{:S(2)}) collective-permute-start(bf16[384,1024]{0,1:T(8,128)(2,1)S(1)} %all_gather.12), channel_id=1, source_target_pairs={{0,2},{2,0},{1,3},{3,1},{4,6},{6,4},{5,7},{7,5},{8,10},{10,8},{9,1... | collective-permute-start | bytes 2359304 | tf_op jit(solution)/shard_map/ppermute | solution.py:31
  42.7 17.9 %collective-permute-done = bf16[384,1024]{0,1:T(8,128)(2,1)S(1)} collective-permute-done((bf16[384,1024]{0,1:T(8,128)(2,1)S(1)}, bf16[384,1024]{0,1:T(8,128)(2,1)S(1)}, u32[]{:S(2)}, u32[]{:S(2)}) %collective-permute-start) | collective-permute-done | bytes 786464 | tf_op jit(solution)/shard_map/ppermute | solution.py:31
  60.6 0.1 broadcast_select_fusion.1
  60.8 0.2 pad_maximum_fusion
  60.9 23.7 %all-gather.6.cloned.1.call-done = bf16[8192,512]{1,0:T(8,128)(2,1)} async-done(((bf16[512,512]{1,0:T(8,128)(2,1)}), bf16[8192,512]{1,0:T(8,128)(2,1)}) %all-gather.6.cloned.1.call-update) | async-done | bytes 8388624 | tf_op jit(solution)/shard_map/all_gather | solution.py:34
  84.6 8.0 %bitcast_convert_fusion = bf16[384,4,512]{2,0,1:T(8,128)(2,1)} fusion(bf16[384,4,512,1]{0,2,1,3:T(8,128)(2,1)S(1)} %bitcast.19, bf16[4,4,512,512]{3,2,1,0:T(8,128)(2,1)} %bitcast.20), kind=kOutput, calls=%fused_computation.9 | convolution fusion | flops 3222011904 | bytes 11534336 | tf_op jit(solution)/shard_map/iqh,rqhf->irf/dot_general | solution.py:35
  92.6 6.9 %all-to-all-start = ((bf16[384,4,512]{2,0,1:T(8,128)(2,1)}), bf16[384,4,512]{2,0,1:T(8,128)(2,1)S(1)}, u32[]{:S(2)}, u32[]{:S(2)}) async-start(bf16[384,4,512]{2,0,1:T(8,128)(2,1)} %bitcast_convert_fusion), calls=%async_computation | async-start | bytes 3145728 | tf_op jit(solution)/shard_map/all_to_all | solution.py:38
  99.5 0.1 convert_reduce_fusion.1
  99.6 37.2 %all-to-all-done = bf16[384,4,512]{2,0,1:T(8,128)(2,1)S(1)} async-done(((bf16[384,4,512]{2,0,1:T(8,128)(2,1)}), bf16[384,4,512]{2,0,1:T(8,128)(2,1)S(1)}, u32[]{:S(2)}, u32[]{:S(2)}) %all-to-all-start) | async-done | bytes 1572896 | tf_op jit(solution)/shard_map/all_to_all | solution.py:38
  136.8 0.2 convert_reduce_fusion
  137.0 0.9 copy-done.1
  137.9 0.2 multiply_reduce_fusion
  138.1 5.3 %psum.14 = f32[384]{0:T(512)S(1)} all-reduce(f32[384]{0:T(512)S(1)} %multiply_reduce_fusion), channel_id=1, replica_groups=mesh['xlo'=2,'y'=4,'core'=2,'zhi'=4,'zlo'=2,'xhi'=2] {'xhi'}, use_global_device_ids=true, to_apply=%region_2.3 | all-reduce | flops 384 | bytes 3072 | tf_op jit(solution)/shard_map/psum | solution.py:41
  143.4 11.4 %psum.15 = f32[384]{0:T(512)S(1)} all-reduce(f32[384]{0:T(512)S(1)} %psum.14), channel_id=1, replica_groups=mesh['xlo'=2,'y'=4,'core'=2,'zhi'=4,'zlo'=2,'xhi'=2] {'zhi','zlo'}, use_global_device_ids=true, to_apply=%region_3.4 | all-reduce | flops 384 | bytes 3072 | tf_op jit(solution)/shard_map/psum | solution.py:41
  154.8 2.2 fusion.11
  157.0 0.7 fusion.16
  162.7 35.8 %all-gather.4.cloned.1.call-done = bf16[1536,512]{1,0:T(8,128)(2,1)} async-done(((bf16[96,512]{1,0:T(8,128)(2,1)}), bf16[1536,512]{1,0:T(8,128)(2,1)}) %all-gather.4.cloned.1.call-update) | async-done | bytes 1572880 | tf_op jit(solution)/shard_map/all_gather | solution.py:50
  198.5 4.8 %pad_dynamic-slice_fusion.3 = (bf16[1536,512]{1,0:T(8,128)(2,1)S(1)}, bf16[1536,512]{1,0:T(8,128)(2,1)S(1)}, bf16[1536,512]{1,0:T(8,128)(2,1)S(1)}, bf16[1536,512]{1,0:T(8,128)(2,1)S(1)}) fusion(s32[]{:T(128)S(6)} %select_n.27, bf16[1536,512]{1,0:T(8,128)(2,1)} %all-gather.4.cloned.1.call-done, s32[]{:T(128)S(6)} %select_n.28, s32[]{:T(128)S(6)} %select_n.29, ...), kind=kLoop, calls=%fused_computation.17 | loop fusion | bytes 7864336 | tf_op jit(solution)/shard_map/dynamic_slice | solution.py:55
  203.3 7.9 %fusion.8 = f32[2048,640]{1,0:T(8,128)} fusion(bf16[1536,640]{1,0:T(8,128)(2,1)S(1)} %copy-done, bf16[1536,512]{1,0:T(8,128)(2,1)S(1)} %get-tuple-element.8, bf16[1536,512]{1,0:T(8,128)(2,1)S(1)} %get-tuple-element.7, bf16[1536,512]{1,0:T(8,128)(2,1)S(1)} %get-tuple-element.6, bf16[1536,512]{1,0:T(8,128)(2,1)S(1)} %get-tuple-element.5), kind=kOutput, calls=%fused_computation.8 | convolution fusion | flops 4053008384 | bytes 13500416 | tf_op jit(solution)/shard_map/dot_general | solution.py:58
  (18 shorter events, 0.1 us)
Async XLA Ops:
  6.5 196.8 %copy-start = (bf16[1536,640]{1,0:T(8,128)(2,1)S(1)}, bf16[1536,640]{1,0:T(8,128)(2,1)}, u32[]{:S(2)}) copy-start(bf16[1536,640]{1,0:T(8,128)(2,1)} %param.13) | copy-start | bytes 5898244
  6.5 78.1 %all-gather.6.cloned.1.call-start = ((), (), s32[]{:S(2)}) async-start(), calls=%async_computation.2 | async-start | bytes 8912896 | tf_op jit(solution)/shard_map/all_gather | solution.py:34
  6.5 17.0 %collective-permute-start.1 = (bf16[512,512]{1,0:T(8,128)(2,1)}, bf16[512,512]{1,0:T(8,128)(2,1)S(1)}, u32[]{:S(2)}, u32[]{:S(2)}) collective-permute-start(bf16[512,512]{1,0:T(8,128)(2,1)} %param.8), channel_id=1, source_target_pairs={{0,0},{16,1},{32,2},{48,3},{4,4},{20,5},{36,6},{52,7},{8,8},{24,9}... | collective-permute-start | bytes 1572872 | tf_op jit(solution)/shard_map/ppermute | solution.py:23
  23.5 0.8 copy-start.2
  38.3 22.3 %collective-permute-start = (bf16[384,1024]{0,1:T(8,128)(2,1)S(1)}, bf16[384,1024]{0,1:T(8,128)(2,1)S(1)}, u32[]{:S(2)}, u32[]{:S(2)}) collective-permute-start(bf16[384,1024]{0,1:T(8,128)(2,1)S(1)} %all_gather.12), channel_id=1, source_target_pairs={{0,2},{2,0},{1,3},{3,1},{4,6},{6,4},{5,7},{7,5},{8,10},{10,8},{9,1... | collective-permute-start | bytes 2359304 | tf_op jit(solution)/shard_map/ppermute | solution.py:31
  92.6 6.9 %copy-start.5 = (s32[1,384]{1,0:T(1,128)S(1)}, s32[1,384]{1,0:T(1,128)}, u32[]{:S(2)}) copy-start(s32[1,384]{1,0:T(1,128)} %param.11) | copy-start | bytes 4612
  92.6 44.2 %all-to-all-start = ((bf16[384,4,512]{2,0,1:T(8,128)(2,1)}), bf16[384,4,512]{2,0,1:T(8,128)(2,1)S(1)}, u32[]{:S(2)}, u32[]{:S(2)}) async-start(bf16[384,4,512]{2,0,1:T(8,128)(2,1)} %bitcast_convert_fusion), calls=%async_computation | async-start | bytes 3145728 | tf_op jit(solution)/shard_map/all_to_all | solution.py:38
  99.5 99.0 %all-gather.4.cloned.1.call-start = ((), (), s32[]{:S(2)}) async-start(), calls=%async_computation.1 | async-start | bytes 1671168 | tf_op jit(solution)/shard_map/all_gather | solution.py:50
  99.6 55.2 %copy-start.6 = (f32[512]{0:T(512)S(1)}, f32[512]{0:T(512)}, u32[]{:S(2)}) copy-start(f32[512]{0:T(512)} %param.10) | copy-start | bytes 6148
  136.8 1.1 copy-start.3
  137.0 0.9 copy-start.1
  137.9 19.1 %copy-start.4 = (s32[4]{0:T(128)S(1)}, s32[4]{0:T(128)}, u32[]{:S(2)}) copy-start(s32[4]{0:T(128)} %param.12) | copy-start | bytes 52
Sparse Core Ops, SparseCore 0:
  24.5 60.0 all-gather.5
  157.1 41.3 all-gather.3

commit v9 on v8

--- a/solution.py
+++ b/solution.py
@@ -38,7 +38,10 @@
     received = lax.all_to_all(partial.astype(jnp.bfloat16), "zhi", 1, 1, tiled=True)
     summed = jnp.sum(received.astype(jnp.float32), axis=1)
     hidden = residual.astype(jnp.float32) + summed
-    squares = lax.psum(lax.psum(jnp.sum(hidden * hidden, axis=1), "xhi"), ("zhi", "zlo"))
+    squares = jnp.sum(hidden * hidden, axis=1)
+    for axis, mask in (("xhi", 1), ("zlo", 1), ("zhi", 1), ("zhi", 2)):
+        size = lax.axis_size(axis)
+        squares = squares + lax.ppermute(squares, axis, [(i, i ^ mask) for i in range(size)])
     normed = (hidden * lax.rsqrt(squares[:, None] / D + 1e-05) * gain[None, :]).astype(jnp.bfloat16)
     member = jnp.arange(R_DEV, dtype=jnp.int32)[:, None] == token_tr[0][None, :]
     counts = jnp.sum(member.astype(jnp.float32), axis=1, keepdims=True)

time: 218 us -> 213 us (0.977)
  waiting for transfers between devices: 125 us -> 94.7 us
  blocking collectives: 29.5 us -> 57.2 us
  matrix products: 18 us -> 15.7 us
    all_to_all x0 -> x1, blocking collectives: none -> 44.4 us  [on_device(): lax.all_to_all(partial.astype(jnp.bfloat16), 'zhi', 1, 1, tiled=True)]
    all_to_all x1 -> x0, waiting for transfers between devices: 37.2 us -> none  [on_device(): lax.all_to_all(partial.astype(jnp.bfloat16), 'zhi', 1, 1, tiled=True)]
    psum x2 -> x0, blocking collectives: 16.7 us -> none  [the longest x1 11.4 us: on_device(): lax.psum(lax.psum(jnp.sum(hidden * hidden, axis=1), 'xhi'), ('zhi', 'zlo'))]
    ppermute x0 -> x4, waiting for transfers between devices: none -> 9.14 us  [on_device(): lax.ppermute(squares, axis, [(i, i ^ mask) for i in range(size)])]
    ppermute x0 -> x4, starting transfers between devices: none -> 7.15 us  [on_device(): lax.ppermute(squares, axis, [(i, i ^ mask) for i in range(size)])]
    all_to_all x1 -> x0, starting transfers between devices: 6.86 us -> none  [on_device(): lax.all_to_all(partial.astype(jnp.bfloat16), 'zhi', 1, 1, tiled=True)]
    all_gather x1, waiting for transfers between devices: 35.8 us -> 33.2 us  [on_device(): story = lax.all_gather(binned, GROUP, axis=0, tiled=True)]
  transfers between devices with their start and end apart: 5 -> 8, of which waited for: 5 -> 8; matrix products, arithmetic and copies ran while one was open for 1% -> 1% of each run, Pallas kernels for 0% -> 0%
where the time goes in v9:
time: 213 us
  waiting for transfers between devices  94.7 us (44%)
  blocking collectives  57.2 us (27%)
  between operations  18.3 us (9%)
  starting transfers between devices  17.7 us (8%)
  matrix products  15.7 us (7%)
  local copies, waits for them, and re-layouts  8.15 us (4%)
    all_to_all x1, blocking collectives, on_device(): lax.all_to_all(partial.astype(jnp.bfloat16), 'zhi', 1, 1, tiled=True)  44.4 us
    all_gather x1, waiting for transfers between devices, on_device(): story = lax.all_gather(binned, GROUP, axis=0, tiled=True)  33.2 us
    all_gather x1, waiting for transfers between devices, on_device(): lax.all_gather(ring_block(out_weight), GROUP, axis=0)  23.6 us
    ppermute x1, waiting for transfers between devices, on_device(): other = lax.ppermute(pair, 'zlo', [(0, 1), (1, 0)])  17.9 us
    all_gather x1, blocking collectives, on_device(): pair = lax.all_gather(attention, 'xhi', axis=1, tiled=True)  12.8 us
    ppermute x1, waiting for transfers between devices, ring_block(): return lax.ppermute(block, GROUP + TENSOR, route)  10.8 us
    ppermute x4, waiting for transfers between devices, on_device(): lax.ppermute(squares, axis, [(i, i ^ mask) for i in range(size)])  9.14 us
    dot_general x1, matrix products, on_device(): lax.dot_general(lagged, responses, contract, preferred_element_type=jnp.f...  7.88 us
  transfers between devices with their start and end apart: 8, of which 8 were waited for; matrix products, arithmetic and copies ran while one was open for 1% of the time, Pallas kernels for 0%

profile of v9, /device:TPU:1, one launch (start us, length us, event | category | flops | bytes accessed | tf_op | source)
XLA Modules:
  0.0 212.7 jit_solution(1478928880450097937)
XLA Ops:
  6.5 6.1 %collective-permute-start.1 = (bf16[512,512]{1,0:T(8,128)(2,1)}, bf16[512,512]{1,0:T(8,128)(2,1)S(1)}, u32[]{:S(2)}, u32[]{:S(2)}) collective-permute-start(bf16[512,512]{1,0:T(8,128)(2,1)} %param.8), channel_id=1, source_target_pairs={{0,0},{16,1},{32,2},{48,3},{4,4},{20,5},{36,6},{52,7},{8,8},{24,9}... | collective-permute-start | bytes 1572872 | tf_op jit(solution)/shard_map/ppermute | solution.py:23
  12.7 10.8 %collective-permute-done.1 = bf16[512,512]{1,0:T(8,128)(2,1)S(1)} collective-permute-done((bf16[512,512]{1,0:T(8,128)(2,1)}, bf16[512,512]{1,0:T(8,128)(2,1)S(1)}, u32[]{:S(2)}, u32[]{:S(2)}) %collective-permute-start.1) | collective-permute-done | bytes 524320 | tf_op jit(solution)/shard_map/ppermute | solution.py:23
  23.5 0.8 copy-done.1
  24.4 1.2 copy.10
  25.6 12.8 %all_gather.12 = bf16[384,1024]{0,1:T(8,128)(2,1)S(1)} all-gather(bf16[384,512]{0,1:T(8,128)(2,1)S(1)} %copy.10), channel_id=1, replica_groups=mesh['xlo'=2,'y'=4,'core'=2,'zhi'=4,'zlo'=2,'xhi'=2] {'xhi'}, dimensions={1}, use_global_device_ids=true | all-gather | bytes 1179648 | tf_op jit(solution)/shard_map/all_gather | solution.py:30
  38.4 4.4 %collective-permute-start = (bf16[384,1024]{0,1:T(8,128)(2,1)S(1)}, bf16[384,1024]{0,1:T(8,128)(2,1)S(1)}, u32[]{:S(2)}, u32[]{:S(2)}) collective-permute-start(bf16[384,1024]{0,1:T(8,128)(2,1)S(1)} %all_gather.12), channel_id=1, source_target_pairs={{0,2},{2,0},{1,3},{3,1},{4,6},{6,4},{5,7},{7,5},{8,10},{10,8},{9,1... | collective-permute-start | bytes 2359304 | tf_op jit(solution)/shard_map/ppermute | solution.py:31
  42.8 17.9 %collective-permute-done = bf16[384,1024]{0,1:T(8,128)(2,1)S(1)} collective-permute-done((bf16[384,1024]{0,1:T(8,128)(2,1)S(1)}, bf16[384,1024]{0,1:T(8,128)(2,1)S(1)}, u32[]{:S(2)}, u32[]{:S(2)}) %collective-permute-start) | collective-permute-done | bytes 786464 | tf_op jit(solution)/shard_map/ppermute | solution.py:31
  61.0 23.6 %all-gather.6.cloned.1.call-done = bf16[8192,512]{1,0:T(8,128)(2,1)} async-done(((bf16[512,512]{1,0:T(8,128)(2,1)}), bf16[8192,512]{1,0:T(8,128)(2,1)}) %all-gather.6.cloned.1.call-update) | async-done | bytes 8388624 | tf_op jit(solution)/shard_map/all_gather | solution.py:34
  84.6 6.8 %bitcast_convert_fusion = bf16[384,4,512]{2,0,1:T(8,128)(2,1)S(1)} fusion(bf16[384,4,512,1]{0,2,1,3:T(8,128)(2,1)S(1)} %bitcast.19, bf16[4,4,512,512]{3,2,1,0:T(8,128)(2,1)} %bitcast.20), kind=kOutput, calls=%fused_computation.9 | convolution fusion | flops 3222011904 | bytes 11534336 | tf_op jit(solution)/shard_map/iqh,rqhf->irf/dot_general | solution.py:35
  91.4 44.4 %all_to_all.5 = bf16[384,4,512]{2,0,1:T(8,128)(2,1)S(1)} all-to-all(bf16[384,4,512]{2,0,1:T(8,128)(2,1)S(1)} %bitcast_convert_fusion), channel_id=1, replica_groups=mesh['xlo'=2,'y'=4,'core'=2,'zhi'=4,'zlo'=2,'xhi'=2] {'zhi'}, dimensions={1} | all-to-all | bytes 3145728 | tf_op jit(solution)/shard_map/all_to_all | solution.py:38
  135.9 0.3 convert_reduce_fusion
  136.2 0.7 copy-done.2
  137.1 2.8 %collective-permute-start.2 = (f32[384]{0:T(512)S(1)}, f32[384]{0:T(512)S(1)}, u32[]{:S(2)}, u32[]{:S(2)}) collective-permute-start(f32[384]{0:T(512)S(1)} %multiply_reduce_fusion), channel_id=1, source_target_pairs={{0,1},{1,0},{2,3},{3,2},{4,5},{5,4},{6,7},{7,6},{8,9},{9,8},{10,11... | collective-permute-start | bytes 4616 | tf_op jit(solution)/shard_map/ppermute | solution.py:44
  139.8 1.2 collective-permute-done.2
  141.1 2.7 %collective-permute-done.3 = f32[384]{0:T(512)S(1)} collective-permute-done((f32[384]{0:T(512)S(1)}, f32[384]{0:T(512)S(1)}, u32[]{:S(2)}, u32[]{:S(2)}) %collective-permute-start.3) | collective-permute-done | bytes 1568 | tf_op jit(solution)/shard_map/ppermute | solution.py:44
  143.8 2.2 %collective-permute-start.4 = (f32[384]{0:T(512)S(1)}, f32[384]{0:T(512)S(1)}, u32[]{:S(2)}, u32[]{:S(2)}) collective-permute-start(f32[384]{0:T(512)S(1)} %add.50), channel_id=1, source_target_pairs={{0,4},{4,0},{8,12},{12,8},{1,5},{5,1},{9,13},{13,9},{2,6},{6,2},{1... | collective-permute-start | bytes 4616 | tf_op jit(solution)/shard_map/ppermute | solution.py:44
  146.0 1.1 collective-permute-done.4
  147.2 2.2 %collective-permute-start.5 = (f32[384]{0:T(512)S(1)}, f32[384]{0:T(512)S(1)}, u32[]{:S(2)}, u32[]{:S(2)}) collective-permute-start(f32[384]{0:T(512)S(1)} %add.51), channel_id=1, source_target_pairs={{0,8},{4,12},{8,0},{12,4},{1,9},{5,13},{9,1},{13,5},{2,10},{6,14},... | collective-permute-start | bytes 4616 | tf_op jit(solution)/shard_map/ppermute | solution.py:44
  149.5 4.0 %collective-permute-done.5 = f32[384]{0:T(512)S(1)} collective-permute-done((f32[384]{0:T(512)S(1)}, f32[384]{0:T(512)S(1)}, u32[]{:S(2)}, u32[]{:S(2)}) %collective-permute-start.5) | collective-permute-done | bytes 1568 | tf_op jit(solution)/shard_map/ppermute | solution.py:44
  153.5 1.0 fusion.11
  154.5 0.6 fusion.16
  160.0 33.2 %all-gather.4.cloned.1.call-done = bf16[1536,512]{1,0:T(8,128)(2,1)} async-done(((bf16[96,512]{1,0:T(8,128)(2,1)}), bf16[1536,512]{1,0:T(8,128)(2,1)}) %all-gather.4.cloned.1.call-update) | async-done | bytes 1572880 | tf_op jit(solution)/shard_map/all_gather | solution.py:53
  193.2 4.8 %pad_dynamic-slice_fusion.3 = (bf16[1536,512]{1,0:T(8,128)(2,1)S(1)}, bf16[1536,512]{1,0:T(8,128)(2,1)S(1)}, bf16[1536,512]{1,0:T(8,128)(2,1)S(1)}, bf16[1536,512]{1,0:T(8,128)(2,1)S(1)}) fusion(s32[]{:T(128)S(6)} %select_n.27, bf16[1536,512]{1,0:T(8,128)(2,1)} %all-gather.4.cloned.1.call-done, s32[]{:T(128)S(6)} %select_n.28, s32[]{:T(128)S(6)} %select_n.29, ...), kind=kLoop, calls=%fused_computation.17 | loop fusion | bytes 7864336 | tf_op jit(solution)/shard_map/dynamic_slice | solution.py:58
  198.0 7.9 %fusion.8 = f32[2048,640]{1,0:T(8,128)} fusion(bf16[1536,640]{1,0:T(8,128)(2,1)S(1)} %copy-done, bf16[1536,512]{1,0:T(8,128)(2,1)S(1)} %get-tuple-element.8, bf16[1536,512]{1,0:T(8,128)(2,1)S(1)} %get-tuple-element.7, bf16[1536,512]{1,0:T(8,128)(2,1)S(1)} %get-tuple-element.6, bf16[1536,512]{1,0:T(8,128)(2,1)S(1)} %get-tuple-element.5), kind=kOutput, calls=%fused_computation.8 | convolution fusion | flops 4053008384 | bytes 13500416 | tf_op jit(solution)/shard_map/dot_general | solution.py:61
  (24 shorter events, 0.7 us)
Async XLA Ops:
  6.5 191.4 %copy-start = (bf16[1536,640]{1,0:T(8,128)(2,1)S(1)}, bf16[1536,640]{1,0:T(8,128)(2,1)}, u32[]{:S(2)}) copy-start(bf16[1536,640]{1,0:T(8,128)(2,1)} %param.13) | copy-start | bytes 5898244
  6.5 78.1 %all-gather.6.cloned.1.call-start = ((), (), s32[]{:S(2)}) async-start(), calls=%async_computation.2 | async-start | bytes 8912896 | tf_op jit(solution)/shard_map/all_gather | solution.py:34
  6.5 17.0 %collective-permute-start.1 = (bf16[512,512]{1,0:T(8,128)(2,1)}, bf16[512,512]{1,0:T(8,128)(2,1)S(1)}, u32[]{:S(2)}, u32[]{:S(2)}) collective-permute-start(bf16[512,512]{1,0:T(8,128)(2,1)} %param.8), channel_id=1, source_target_pairs={{0,0},{16,1},{32,2},{48,3},{4,4},{20,5},{36,6},{52,7},{8,8},{24,9}... | collective-permute-start | bytes 1572872 | tf_op jit(solution)/shard_map/ppermute | solution.py:23
  23.5 0.8 copy-start.1
  24.3 168.8 %all-gather.4.cloned.1.call-start = ((), (), s32[]{:S(2)}) async-start(), calls=%async_computation.1 | async-start | bytes 1671168 | tf_op jit(solution)/shard_map/all_gather | solution.py:53
  38.4 22.3 %collective-permute-start = (bf16[384,1024]{0,1:T(8,128)(2,1)S(1)}, bf16[384,1024]{0,1:T(8,128)(2,1)S(1)}, u32[]{:S(2)}, u32[]{:S(2)}) collective-permute-start(bf16[384,1024]{0,1:T(8,128)(2,1)S(1)} %all_gather.12), channel_id=1, source_target_pairs={{0,2},{2,0},{1,3},{3,1},{4,6},{6,4},{5,7},{7,5},{8,10},{10,8},{9,1... | collective-permute-start | bytes 2359304 | tf_op jit(solution)/shard_map/ppermute | solution.py:31
  135.9 1.0 copy-start.2
  135.9 10.1 %copy-start.4 = (s32[1,384]{1,0:T(1,128)S(1)}, s32[1,384]{1,0:T(1,128)}, u32[]{:S(2)}) copy-start(s32[1,384]{1,0:T(1,128)} %param.11) | copy-start | bytes 4612
  135.9 17.6 %copy-start.5 = (f32[512]{0:T(512)S(1)}, f32[512]{0:T(512)}, u32[]{:S(2)}) copy-start(f32[512]{0:T(512)} %param.10) | copy-start | bytes 6148
  136.9 17.6 %copy-start.3 = (s32[4]{0:T(128)S(1)}, s32[4]{0:T(128)}, u32[]{:S(2)}) copy-start(s32[4]{0:T(128)} %param.12) | copy-start | bytes 52
  137.1 4.0 %collective-permute-start.2 = (f32[384]{0:T(512)S(1)}, f32[384]{0:T(512)S(1)}, u32[]{:S(2)}, u32[]{:S(2)}) collective-permute-start(f32[384]{0:T(512)S(1)} %multiply_reduce_fusion), channel_id=1, source_target_pairs={{0,1},{1,0},{2,3},{3,2},{4,5},{5,4},{6,7},{7,6},{8,9},{9,8},{10,11... | collective-permute-start | bytes 4616 | tf_op jit(solution)/shard_map/ppermute | solution.py:44
  141.1 2.7 %collective-permute-start.3 = (f32[384]{0:T(512)S(1)}, f32[384]{0:T(512)S(1)}, u32[]{:S(2)}, u32[]{:S(2)}) collective-permute-start(f32[384]{0:T(512)S(1)} %add.49), channel_id=1, source_target_pairs={{0,2},{2,0},{1,3},{3,1},{4,6},{6,4},{5,7},{7,5},{8,10},{10,8},{9,1... | collective-permute-start | bytes 4616 | tf_op jit(solution)/shard_map/ppermute | solution.py:44
  143.8 3.3 %collective-permute-start.4 = (f32[384]{0:T(512)S(1)}, f32[384]{0:T(512)S(1)}, u32[]{:S(2)}, u32[]{:S(2)}) collective-permute-start(f32[384]{0:T(512)S(1)} %add.50), channel_id=1, source_target_pairs={{0,4},{4,0},{8,12},{12,8},{1,5},{5,1},{9,13},{13,9},{2,6},{6,2},{1... | collective-permute-start | bytes 4616 | tf_op jit(solution)/shard_map/ppermute | solution.py:44
  147.2 6.3 %collective-permute-start.5 = (f32[384]{0:T(512)S(1)}, f32[384]{0:T(512)S(1)}, u32[]{:S(2)}, u32[]{:S(2)}) collective-permute-start(f32[384]{0:T(512)S(1)} %add.51), channel_id=1, source_target_pairs={{0,8},{4,12},{8,0},{12,4},{1,9},{5,13},{9,1},{13,5},{2,10},{6,14},... | collective-permute-start | bytes 4616 | tf_op jit(solution)/shard_map/ppermute | solution.py:44
Sparse Core Ops, SparseCore 0:
  24.5 60.0 all-gather.5
  154.6 38.5 all-gather.3

commit v10 on v9

--- a/solution.py
+++ b/solution.py
@@ -52,14 +52,13 @@
     total_trs = responses.shape[0]
     story = lax.all_gather(binned, GROUP, axis=0, tiled=True)
     extended = jnp.concatenate([jnp.zeros((LAGS, width), story.dtype), story], axis=0)
-    pieces = []
+    contract = (((0,), (0,)), ((), ()))
+    products = []
     for step in range(LAGS):
         start = LAGS - lag_offsets[step]
-        pieces.append(lax.dynamic_slice_in_dim(extended, start, total_trs, 0))
-    lagged = jnp.concatenate(pieces, axis=1)
-    contract = (((0,), (0,)), ((), ()))
-    accumulated = lax.dot_general(lagged, responses, contract, preferred_element_type=jnp.float32)
-    scaled = accumulated * (1.0 / jnp.sqrt(jnp.float32(total_trs)))
+        lagged = lax.dynamic_slice_in_dim(extended, start, total_trs, 0)
+        products.append(lax.dot_general(lagged, responses, contract, preferred_element_type=jnp.float32))
+    scaled = jnp.stack(products) * (1.0 / jnp.sqrt(jnp.float32(total_trs)))
     return scaled.reshape(LAGS, width, responses.shape[1])
 
 

time: 213 us -> 211 us (level)
  local copies, waits for them, and re-layouts: 8.15 us -> 3.41 us
  other arithmetic: 0.89 us -> 3.7 us
    dynamic_slice x1 -> x0, local copies, waits for them, and re-layouts: 4.79 us -> none  [on_device(): pieces.append(lax.dynamic_slice_in_dim(extended, start, total_trs, 0))]
    mul x0 -> x1, other arithmetic: none -> 2.81 us  [on_device(): scaled = jnp.stack(products) * (1.0 / jnp.sqrt(jnp.float32(total_trs)))]
    dot_general x1 -> x4, matrix products: 7.88 us -> 7.43 us  [on_device(): lax.dot_general(lagged, responses, contract, preferred_element_type=jnp.f...]
where the time goes in v10:
time: 211 us; the launch traced here: 210 us
  waiting for transfers between devices  94.6 us (45%)
  blocking collectives  57.2 us (27%)
  between operations  18.4 us (9%)
  starting transfers between devices  17.7 us (8%)
  matrix products  15.2 us (7%)
  other arithmetic  3.7 us (2%)
  local copies, waits for them, and re-layouts  3.41 us (2%)
    all_to_all x1, blocking collectives, on_device(): lax.all_to_all(partial.astype(jnp.bfloat16), 'zhi', 1, 1, tiled=True)  44.4 us
    all_gather x1, waiting for transfers between devices, on_device(): story = lax.all_gather(binned, GROUP, axis=0, tiled=True)  33.1 us
    all_gather x1, waiting for transfers between devices, on_device(): lax.all_gather(ring_block(out_weight), GROUP, axis=0)  23.6 us
    ppermute x1, waiting for transfers between devices, on_device(): other = lax.ppermute(pair, 'zlo', [(0, 1), (1, 0)])  17.9 us
    all_gather x1, blocking collectives, on_device(): pair = lax.all_gather(attention, 'xhi', axis=1, tiled=True)  12.8 us
    ppermute x1, waiting for transfers between devices, ring_block(): return lax.ppermute(block, GROUP + TENSOR, route)  10.8 us
    ppermute x4, waiting for transfers between devices, on_device(): lax.ppermute(squares, axis, [(i, i ^ mask) for i in range(size)])  9.14 us
    dot_general x4, matrix products, on_device(): lax.dot_general(lagged, responses, contract, preferred_element_type=jnp.f...  7.43 us
  transfers between devices with their start and end apart: 8, of which 8 were waited for; matrix products, arithmetic and copies ran while one was open for 1% of the time, Pallas kernels for 0%

profile of v10, /device:TPU:1, one launch (start us, length us, event | category | flops | bytes accessed | tf_op | source)
XLA Modules:
  0.0 210.3 jit_solution(2395834816978081532)
XLA Ops:
  6.5 6.1 %collective-permute-start.1 = (bf16[512,512]{1,0:T(8,128)(2,1)}, bf16[512,512]{1,0:T(8,128)(2,1)S(1)}, u32[]{:S(2)}, u32[]{:S(2)}) collective-permute-start(bf16[512,512]{1,0:T(8,128)(2,1)} %param.8), channel_id=1, source_target_pairs={{0,0},{16,1},{32,2},{48,3},{4,4},{20,5},{36,6},{52,7},{8,8},{24,9}... | collective-permute-start | bytes 1572872 | tf_op jit(solution)/shard_map/ppermute | solution.py:23
  12.7 10.8 %collective-permute-done.1 = bf16[512,512]{1,0:T(8,128)(2,1)S(1)} collective-permute-done((bf16[512,512]{1,0:T(8,128)(2,1)}, bf16[512,512]{1,0:T(8,128)(2,1)S(1)}, u32[]{:S(2)}, u32[]{:S(2)}) %collective-permute-start.1) | collective-permute-done | bytes 524320 | tf_op jit(solution)/shard_map/ppermute | solution.py:23
  23.5 0.8 copy-done.2
  24.4 1.2 copy.10
  25.6 12.8 %all_gather.12 = bf16[384,1024]{0,1:T(8,128)(2,1)S(1)} all-gather(bf16[384,512]{0,1:T(8,128)(2,1)S(1)} %copy.10), channel_id=1, replica_groups=mesh['xlo'=2,'y'=4,'core'=2,'zhi'=4,'zlo'=2,'xhi'=2] {'xhi'}, dimensions={1}, use_global_device_ids=true | all-gather | bytes 1179648 | tf_op jit(solution)/shard_map/all_gather | solution.py:30
  38.4 4.4 %collective-permute-start = (bf16[384,1024]{0,1:T(8,128)(2,1)S(1)}, bf16[384,1024]{0,1:T(8,128)(2,1)S(1)}, u32[]{:S(2)}, u32[]{:S(2)}) collective-permute-start(bf16[384,1024]{0,1:T(8,128)(2,1)S(1)} %all_gather.12), channel_id=1, source_target_pairs={{0,2},{2,0},{1,3},{3,1},{4,6},{6,4},{5,7},{7,5},{8,10},{10,8},{9,1... | collective-permute-start | bytes 2359304 | tf_op jit(solution)/shard_map/ppermute | solution.py:31
  42.8 17.9 %collective-permute-done = bf16[384,1024]{0,1:T(8,128)(2,1)S(1)} collective-permute-done((bf16[384,1024]{0,1:T(8,128)(2,1)S(1)}, bf16[384,1024]{0,1:T(8,128)(2,1)S(1)}, u32[]{:S(2)}, u32[]{:S(2)}) %collective-permute-start) | collective-permute-done | bytes 786464 | tf_op jit(solution)/shard_map/ppermute | solution.py:31
  61.0 23.6 %all-gather.6.cloned.1.call-done = bf16[8192,512]{1,0:T(8,128)(2,1)} async-done(((bf16[512,512]{1,0:T(8,128)(2,1)}), bf16[8192,512]{1,0:T(8,128)(2,1)}) %all-gather.6.cloned.1.call-update) | async-done | bytes 8388624 | tf_op jit(solution)/shard_map/all_gather | solution.py:34
  84.6 6.8 %bitcast_convert_fusion = bf16[384,4,512]{2,0,1:T(8,128)(2,1)S(1)} fusion(bf16[384,4,512,1]{0,2,1,3:T(8,128)(2,1)S(1)} %bitcast.29, bf16[4,4,512,512]{3,2,1,0:T(8,128)(2,1)} %bitcast.30), kind=kOutput, calls=%fused_computation.1 | convolution fusion | flops 3222011904 | bytes 11534336 | tf_op jit(solution)/shard_map/iqh,rqhf->irf/dot_general | solution.py:35
  91.4 44.4 %all_to_all.5 = bf16[384,4,512]{2,0,1:T(8,128)(2,1)S(1)} all-to-all(bf16[384,4,512]{2,0,1:T(8,128)(2,1)S(1)} %bitcast_convert_fusion), channel_id=1, replica_groups=mesh['xlo'=2,'y'=4,'core'=2,'zhi'=4,'zlo'=2,'xhi'=2] {'zhi'}, dimensions={1} | all-to-all | bytes 3145728 | tf_op jit(solution)/shard_map/all_to_all | solution.py:38
  137.1 2.8 %collective-permute-start.2 = (f32[384]{0:T(512)S(1)}, f32[384]{0:T(512)S(1)}, u32[]{:S(2)}, u32[]{:S(2)}) collective-permute-start(f32[384]{0:T(512)S(1)} %multiply_reduce_fusion), channel_id=1, source_target_pairs={{0,1},{1,0},{2,3},{3,2},{4,5},{5,4},{6,7},{7,6},{8,9},{9,8},{10,11... | collective-permute-start | bytes 4616 | tf_op jit(solution)/shard_map/ppermute | solution.py:44
  139.8 1.2 collective-permute-done.2
  141.1 2.7 %collective-permute-done.3 = f32[384]{0:T(512)S(1)} collective-permute-done((f32[384]{0:T(512)S(1)}, f32[384]{0:T(512)S(1)}, u32[]{:S(2)}, u32[]{:S(2)}) %collective-permute-start.3) | collective-permute-done | bytes 1568 | tf_op jit(solution)/shard_map/ppermute | solution.py:44
  143.8 2.2 %collective-permute-start.4 = (f32[384]{0:T(512)S(1)}, f32[384]{0:T(512)S(1)}, u32[]{:S(2)}, u32[]{:S(2)}) collective-permute-start(f32[384]{0:T(512)S(1)} %add.50), channel_id=1, source_target_pairs={{0,4},{4,0},{8,12},{12,8},{1,5},{5,1},{9,13},{13,9},{2,6},{6,2},{1... | collective-permute-start | bytes 4616 | tf_op jit(solution)/shard_map/ppermute | solution.py:44
  146.0 1.1 collective-permute-done.4
  147.2 2.2 %collective-permute-start.5 = (f32[384]{0:T(512)S(1)}, f32[384]{0:T(512)S(1)}, u32[]{:S(2)}, u32[]{:S(2)}) collective-permute-start(f32[384]{0:T(512)S(1)} %add.51), channel_id=1, source_target_pairs={{0,8},{4,12},{8,0},{12,4},{1,9},{5,13},{9,1},{13,5},{2,10},{6,14},... | collective-permute-start | bytes 4616 | tf_op jit(solution)/shard_map/ppermute | solution.py:44
  149.5 4.0 %collective-permute-done.5 = f32[384]{0:T(512)S(1)} collective-permute-done((f32[384]{0:T(512)S(1)}, f32[384]{0:T(512)S(1)}, u32[]{:S(2)}, u32[]{:S(2)}) %collective-permute-start.5) | collective-permute-done | bytes 1568 | tf_op jit(solution)/shard_map/ppermute | solution.py:44
  153.5 1.0 fusion.20
  160.0 33.1 %all-gather.4.cloned.1.call-done = bf16[1536,512]{1,0:T(8,128)(2,1)} async-done(((bf16[96,512]{1,0:T(8,128)(2,1)}), bf16[1536,512]{1,0:T(8,128)(2,1)}) %all-gather.4.cloned.1.call-update) | async-done | bytes 1572880 | tf_op jit(solution)/shard_map/all_gather | solution.py:53
  193.2 3.0 %fusion.11 = f32[1,512,640]{2,1,0:T(8,128)S(1)} fusion(bf16[1536,640]{1,0:T(8,128)(2,1)S(1)} %copy-done, s32[]{:T(128)S(6)} %select_n.28, bf16[1536,512]{1,0:T(8,128)(2,1)} %all-gather.4.cloned.1.call-done), kind=kOutput, calls=%fused_computation.13 | convolution fusion | flops 1006632960 | bytes 4849668 | tf_op jit(solution)/shard_map/dot_general | solution.py:60
  196.2 1.5 fusion.14
  197.6 1.5 fusion.8
  199.1 1.5 fusion.17
  200.6 2.8 %maximum_multiply_fusion = f32[4,512,640]{2,1,0:T(8,128)} fusion(f32[1,512,640]{2,1,0:T(8,128)S(1)} %fusion.17, f32[1,512,640]{2,1,0:T(8,128)S(1)} %fusion.14, f32[1,512,640]{2,1,0:T(8,128)S(1)} %fusion.11, f32[1,512,640]{2,1,0:T(8,128)S(1)} %fusion.8), kind=kLoop, calls=%fused_computation | loop fusion | flops 5242880 | bytes 10485760 | tf_op jit(solution)/shard_map/mul | solution.py:61
  (29 shorter events, 2.4 us)
Async XLA Ops:
  6.5 186.6 %copy-start = (bf16[1536,640]{1,0:T(8,128)(2,1)S(1)}, bf16[1536,640]{1,0:T(8,128)(2,1)}, u32[]{:S(2)}) copy-start(bf16[1536,640]{1,0:T(8,128)(2,1)} %param.13) | copy-start | bytes 5898244
  6.5 78.1 %all-gather.6.cloned.1.call-start = ((), (), s32[]{:S(2)}) async-start(), calls=%async_computation.2 | async-start | bytes 8912896 | tf_op jit(solution)/shard_map/all_gather | solution.py:34
  6.5 17.0 %collective-permute-start.1 = (bf16[512,512]{1,0:T(8,128)(2,1)}, bf16[512,512]{1,0:T(8,128)(2,1)S(1)}, u32[]{:S(2)}, u32[]{:S(2)}) collective-permute-start(bf16[512,512]{1,0:T(8,128)(2,1)} %param.8), channel_id=1, source_target_pairs={{0,0},{16,1},{32,2},{48,3},{4,4},{20,5},{36,6},{52,7},{8,8},{24,9}... | collective-permute-start | bytes 1572872 | tf_op jit(solution)/shard_map/ppermute | solution.py:23
  23.5 0.8 copy-start.2
  24.3 168.8 %all-gather.4.cloned.1.call-start = ((), (), s32[]{:S(2)}) async-start(), calls=%async_computation.1 | async-start | bytes 1671168 | tf_op jit(solution)/shard_map/all_gather | solution.py:53
  38.4 22.3 %collective-permute-start = (bf16[384,1024]{0,1:T(8,128)(2,1)S(1)}, bf16[384,1024]{0,1:T(8,128)(2,1)S(1)}, u32[]{:S(2)}, u32[]{:S(2)}) collective-permute-start(bf16[384,1024]{0,1:T(8,128)(2,1)S(1)} %all_gather.12), channel_id=1, source_target_pairs={{0,2},{2,0},{1,3},{3,1},{4,6},{6,4},{5,7},{7,5},{8,10},{10,8},{9,1... | collective-permute-start | bytes 2359304 | tf_op jit(solution)/shard_map/ppermute | solution.py:31
  135.9 1.0 copy-start.3
  135.9 10.1 %copy-start.5 = (s32[1,384]{1,0:T(1,128)S(1)}, s32[1,384]{1,0:T(1,128)}, u32[]{:S(2)}) copy-start(s32[1,384]{1,0:T(1,128)} %param.11) | copy-start | bytes 4612
  135.9 17.6 %copy-start.6 = (f32[512]{0:T(512)S(1)}, f32[512]{0:T(512)}, u32[]{:S(2)}) copy-start(f32[512]{0:T(512)} %param.10) | copy-start | bytes 6148
  136.9 17.6 %copy-start.4 = (s32[4]{0:T(128)S(1)}, s32[4]{0:T(128)}, u32[]{:S(2)}) copy-start(s32[4]{0:T(128)} %param.12) | copy-start | bytes 52
  137.1 4.0 %collective-permute-start.2 = (f32[384]{0:T(512)S(1)}, f32[384]{0:T(512)S(1)}, u32[]{:S(2)}, u32[]{:S(2)}) collective-permute-start(f32[384]{0:T(512)S(1)} %multiply_reduce_fusion), channel_id=1, source_target_pairs={{0,1},{1,0},{2,3},{3,2},{4,5},{5,4},{6,7},{7,6},{8,9},{9,8},{10,11... | collective-permute-start | bytes 4616 | tf_op jit(solution)/shard_map/ppermute | solution.py:44
  141.1 2.7 %collective-permute-start.3 = (f32[384]{0:T(512)S(1)}, f32[384]{0:T(512)S(1)}, u32[]{:S(2)}, u32[]{:S(2)}) collective-permute-start(f32[384]{0:T(512)S(1)} %add.49), channel_id=1, source_target_pairs={{0,2},{2,0},{1,3},{3,1},{4,6},{6,4},{5,7},{7,5},{8,10},{10,8},{9,1... | collective-permute-start | bytes 4616 | tf_op jit(solution)/shard_map/ppermute | solution.py:44
  143.8 3.3 %collective-permute-start.4 = (f32[384]{0:T(512)S(1)}, f32[384]{0:T(512)S(1)}, u32[]{:S(2)}, u32[]{:S(2)}) collective-permute-start(f32[384]{0:T(512)S(1)} %add.50), channel_id=1, source_target_pairs={{0,4},{4,0},{8,12},{12,8},{1,5},{5,1},{9,13},{13,9},{2,6},{6,2},{1... | collective-permute-start | bytes 4616 | tf_op jit(solution)/shard_map/ppermute | solution.py:44
  147.2 6.3 %collective-permute-start.5 = (f32[384]{0:T(512)S(1)}, f32[384]{0:T(512)S(1)}, u32[]{:S(2)}, u32[]{:S(2)}) collective-permute-start(f32[384]{0:T(512)S(1)} %add.51), channel_id=1, source_target_pairs={{0,8},{4,12},{8,0},{12,4},{1,9},{5,13},{9,1},{13,5},{2,10},{6,14},... | collective-permute-start | bytes 4616 | tf_op jit(solution)/shard_map/ppermute | solution.py:44
  193.2 3.0 %copy-start.1 = (bf16[1536,512]{1,0:T(8,128)(2,1)S(1)}, bf16[1536,512]{1,0:T(8,128)(2,1)}, u32[]{:S(2)}) copy-start(bf16[1536,512]{1,0:T(8,128)(2,1)} %all-gather.4.cloned.1.call-done) | copy-start | bytes 4718596
Sparse Core Ops, SparseCore 0:
  24.5 60.0 all-gather.5
  154.6 38.5 all-gather.3

commit v11 on v10

--- a/solution.py
+++ b/solution.py
@@ -32,11 +32,17 @@
     low = lax.axis_index("zlo") == 0
     slab = jnp.concatenate([jnp.where(low, pair, other), jnp.where(low, other, pair)], axis=1)
     blocks = lax.all_gather(ring_block(out_weight), GROUP, axis=0).reshape(ring, quad, heads, -1)
-    partial = jnp.einsum(
-        "iqh,rqhf->irf", slab.reshape(-1, quad, heads), blocks, preferred_element_type=jnp.float32
-    )
-    received = lax.all_to_all(partial.astype(jnp.bfloat16), "zhi", 1, 1, tiled=True)
-    summed = jnp.sum(received.astype(jnp.float32), axis=1)
+    own = lax.axis_index("zhi")
+    lhs = slab.reshape(-1, quad, heads)
+    summed = None
+    for shift in range(ring):
+        cols = lax.dynamic_index_in_dim(blocks, (own + shift) % ring, 0, keepdims=False)
+        part = jnp.einsum("iqh,qhf->if", lhs, cols, preferred_element_type=jnp.float32)
+        if shift == 0:
+            summed = part
+        else:
+            route = [(i, (i + shift) % ring) for i in range(ring)]
+            summed = summed + lax.ppermute(part.astype(jnp.bfloat16), "zhi", route).astype(jnp.float32)
     hidden = residual.astype(jnp.float32) + summed
     squares = jnp.sum(hidden * hidden, axis=1)
     for axis, mask in (("xhi", 1), ("zlo", 1), ("zhi", 1), ("zhi", 2)):

time: 211 us -> 213 us (level)
  blocking collectives: 57.2 us -> 12.8 us
  waiting for transfers between devices: 94.6 us -> 123 us
  starting transfers between devices: 17.7 us -> 29.1 us
  matrix products: 15.2 us -> 23.5 us
    all_to_all x1 -> x0, blocking collectives: 44.4 us -> none  [on_device(): lax.all_to_all(partial.astype(jnp.bfloat16), 'zhi', 1, 1, tiled=True)]
    ppermute x0 -> x3, waiting for transfers between devices: none -> 29.5 us  [on_device(): lax.ppermute(part.astype(jnp.bfloat16), 'zhi', route).astype(jnp.float32)]
    ppermute x0 -> x3, starting transfers between devices: none -> 9.03 us  [on_device(): lax.ppermute(part.astype(jnp.bfloat16), 'zhi', route).astype(jnp.float32)]
    dot_general x1 -> x4, matrix products: 6.83 us -> 14 us  [on_device(): jnp.einsum('iqh,qhf->if', lhs, cols, preferred_element_type=jnp.float32)]
    ppermute x4, waiting for transfers between devices: 9.14 us -> 6.42 us  [on_device(): lax.ppermute(squares, axis, [(i, i ^ mask) for i in range(size)])]
    ppermute x4, starting transfers between devices: 7.15 us -> 9.5 us  [on_device(): lax.ppermute(squares, axis, [(i, i ^ mask) for i in range(size)])]
  transfers between devices with their start and end apart: 8 -> 11, of which waited for: 8 -> 11; matrix products, arithmetic and copies ran while one was open for 1% -> 4% of each run, Pallas kernels for 0% -> 0%
where the time goes in v11:
time: 213 us
  waiting for transfers between devices  123 us (58%)
  starting transfers between devices  29.1 us (14%)
  matrix products  23.5 us (11%)
  between operations  18.6 us (9%)
  blocking collectives  12.8 us (6%)
  other arithmetic  3.26 us (2%)
  local copies, waits for them, and re-layouts  2.67 us (1%)
    all_gather x1, waiting for transfers between devices, on_device(): story = lax.all_gather(binned, GROUP, axis=0, tiled=True)  34.9 us
    ppermute x3, waiting for transfers between devices, on_device(): lax.ppermute(part.astype(jnp.bfloat16), 'zhi', route).astype(jnp.float32)  29.5 us
    all_gather x1, waiting for transfers between devices, on_device(): lax.all_gather(ring_block(out_weight), GROUP, axis=0)  23.6 us
    ppermute x1, waiting for transfers between devices, on_device(): other = lax.ppermute(pair, 'zlo', [(0, 1), (1, 0)])  17.9 us
    dot_general x4, matrix products, on_device(): jnp.einsum('iqh,qhf->if', lhs, cols, preferred_element_type=jnp.float32)  14 us
    all_gather x1, blocking collectives, on_device(): pair = lax.all_gather(attention, 'xhi', axis=1, tiled=True)  12.8 us
    ppermute x1, waiting for transfers between devices, ring_block(): return lax.ppermute(block, GROUP + TENSOR, route)  10.8 us
    ppermute x4, starting transfers between devices, on_device(): lax.ppermute(squares, axis, [(i, i ^ mask) for i in range(size)])  9.5 us
  transfers between devices with their start and end apart: 11, of which 11 were waited for; matrix products, arithmetic and copies ran while one was open for 4% of the time, Pallas kernels for 0%

profile of v11, /device:TPU:1, one launch (start us, length us, event | category | flops | bytes accessed | tf_op | source)
XLA Modules:
  0.0 213.1 jit_solution(9958133755083960963)
XLA Ops:
  6.5 6.1 %collective-permute-start.1 = (bf16[512,512]{1,0:T(8,128)(2,1)}, bf16[512,512]{1,0:T(8,128)(2,1)S(1)}, u32[]{:S(2)}, u32[]{:S(2)}) collective-permute-start(bf16[512,512]{1,0:T(8,128)(2,1)} %param.8), channel_id=1, source_target_pairs={{0,0},{16,1},{32,2},{48,3},{4,4},{20,5},{36,6},{52,7},{8,8},{24,9}... | collective-permute-start | bytes 1572872 | tf_op jit(solution)/shard_map/ppermute | solution.py:23
  12.7 10.8 %collective-permute-done.1 = bf16[512,512]{1,0:T(8,128)(2,1)S(1)} collective-permute-done((bf16[512,512]{1,0:T(8,128)(2,1)}, bf16[512,512]{1,0:T(8,128)(2,1)S(1)}, u32[]{:S(2)}, u32[]{:S(2)}) %collective-permute-start.1) | collective-permute-done | bytes 524320 | tf_op jit(solution)/shard_map/ppermute | solution.py:23
  25.6 12.8 %all_gather.12 = bf16[384,1024]{0,1:T(8,128)(2,1)S(1)} all-gather(bf16[384,512]{0,1:T(8,128)(2,1)S(1)} %copy.13), channel_id=1, replica_groups=mesh['xlo'=2,'y'=4,'core'=2,'zhi'=4,'zlo'=2,'xhi'=2] {'xhi'}, dimensions={1}, use_global_device_ids=true | all-gather | bytes 1179648 | tf_op jit(solution)/shard_map/all_gather | solution.py:30
  38.4 4.4 %collective-permute-start = (bf16[384,1024]{0,1:T(8,128)(2,1)S(1)}, bf16[384,1024]{0,1:T(8,128)(2,1)S(1)}, u32[]{:S(2)}, u32[]{:S(2)}) collective-permute-start(bf16[384,1024]{0,1:T(8,128)(2,1)S(1)} %all_gather.12), channel_id=1, source_target_pairs={{0,2},{2,0},{1,3},{3,1},{4,6},{6,4},{5,7},{7,5},{8,10},{10,8},{9,1... | collective-permute-start | bytes 2359304 | tf_op jit(solution)/shard_map/ppermute | solution.py:31
  42.8 17.9 %collective-permute-done = bf16[384,1024]{0,1:T(8,128)(2,1)S(1)} collective-permute-done((bf16[384,1024]{0,1:T(8,128)(2,1)S(1)}, bf16[384,1024]{0,1:T(8,128)(2,1)S(1)}, u32[]{:S(2)}, u32[]{:S(2)}) %collective-permute-start) | collective-permute-done | bytes 786464 | tf_op jit(solution)/shard_map/ppermute | solution.py:31
  61.0 23.6 %all-gather.6.cloned.1.call-done = bf16[8192,512]{1,0:T(8,128)(2,1)} async-done(((bf16[512,512]{1,0:T(8,128)(2,1)}), bf16[8192,512]{1,0:T(8,128)(2,1)}) %all-gather.6.cloned.1.call-update) | async-done | bytes 8388624 | tf_op jit(solution)/shard_map/all_gather | solution.py:34
  84.6 3.4 %fusion.62 = bf16[384,512]{1,0:T(8,128)(2,1)} fusion(bf16[384,4,512]{0,2,1:T(8,128)(2,1)S(1)} %bitcast.84, bf16[4,4,512,512]{3,2,1,0:T(8,128)(2,1)} %bitcast.88, s32[]{:T(128)S(6)} %select_n.62), kind=kOutput, calls=%fused_computation.36 | convolution fusion | flops 805502976 | bytes 4063236 | tf_op jit(solution)/shard_map/iqh,qhf->if/dot_general | solution.py:40
  88.0 2.3 %collective-permute-start.2 = (bf16[384,512]{1,0:T(8,128)(2,1)}, bf16[384,512]{1,0:T(8,128)(2,1)}, u32[]{:S(2)}, u32[]{:S(2)}) collective-permute-start(bf16[384,512]{1,0:T(8,128)(2,1)} %fusion.62), channel_id=1, source_target_pairs={{0,4},{4,8},{8,12},{12,0},{1,5},{5,9},{9,13},{13,1},{2,6},{6,10},{... | collective-permute-start | bytes 1179656 | tf_op jit(solution)/shard_map/ppermute | solution.py:45
  90.2 3.3 %fusion.59 = bf16[384,512]{1,0:T(8,128)(2,1)} fusion(bf16[384,4,512]{0,2,1:T(8,128)(2,1)S(1)} %bitcast.85, bf16[4,4,512,512]{3,2,1,0:T(8,128)(2,1)} %bitcast.89, s32[]{:T(128)S(6)} %select_n.64), kind=kOutput, calls=%fused_computation.35 | convolution fusion | flops 805502976 | bytes 4063236 | tf_op jit(solution)/shard_map/iqh,qhf->if/dot_general | solution.py:40
  93.6 3.7 %collective-permute-start.3 = (bf16[384,512]{1,0:T(8,128)(2,1)}, bf16[384,512]{1,0:T(8,128)(2,1)}, u32[]{:S(2)}, u32[]{:S(2)}) collective-permute-start(bf16[384,512]{1,0:T(8,128)(2,1)} %fusion.59), channel_id=1, source_target_pairs={{0,8},{4,12},{8,0},{12,4},{1,9},{5,13},{9,1},{13,5},{2,10},{6,14},... | collective-permute-start | bytes 1179656 | tf_op jit(solution)/shard_map/ppermute | solution.py:45
  97.2 3.3 %fusion.56 = bf16[384,512]{1,0:T(8,128)(2,1)} fusion(bf16[384,4,512]{0,2,1:T(8,128)(2,1)S(1)} %bitcast.86, bf16[4,4,512,512]{3,2,1,0:T(8,128)(2,1)} %bitcast.90, s32[]{:T(128)S(6)} %select_n.66), kind=kOutput, calls=%fused_computation.34 | convolution fusion | flops 805502976 | bytes 4063236 | tf_op jit(solution)/shard_map/iqh,qhf->if/dot_general | solution.py:40
  100.6 3.1 %collective-permute-start.4 = (bf16[384,512]{1,0:T(8,128)(2,1)}, bf16[384,512]{1,0:T(8,128)(2,1)}, u32[]{:S(2)}, u32[]{:S(2)}) collective-permute-start(bf16[384,512]{1,0:T(8,128)(2,1)} %fusion.56), channel_id=1, source_target_pairs={{0,12},{4,0},{8,4},{12,8},{1,13},{5,1},{9,5},{13,9},{2,14},{6,2},{... | collective-permute-start | bytes 1179656 | tf_op jit(solution)/shard_map/ppermute | solution.py:45
  103.7 2.8 %collective-permute-done.2 = bf16[384,512]{1,0:T(8,128)(2,1)} collective-permute-done((bf16[384,512]{1,0:T(8,128)(2,1)}, bf16[384,512]{1,0:T(8,128)(2,1)}, u32[]{:S(2)}, u32[]{:S(2)}) %collective-permute-start.2) | collective-permute-done | bytes 393248 | tf_op jit(solution)/shard_map/ppermute | solution.py:45
  106.5 15.0 %collective-permute-done.3 = bf16[384,512]{1,0:T(8,128)(2,1)} collective-permute-done((bf16[384,512]{1,0:T(8,128)(2,1)}, bf16[384,512]{1,0:T(8,128)(2,1)}, u32[]{:S(2)}, u32[]{:S(2)}) %collective-permute-start.3) | collective-permute-done | bytes 393248 | tf_op jit(solution)/shard_map/ppermute | solution.py:45
  121.5 11.7 %collective-permute-done.4 = bf16[384,512]{1,0:T(8,128)(2,1)} collective-permute-done((bf16[384,512]{1,0:T(8,128)(2,1)}, bf16[384,512]{1,0:T(8,128)(2,1)}, u32[]{:S(2)}, u32[]{:S(2)}) %collective-permute-start.4) | collective-permute-done | bytes 393248 | tf_op jit(solution)/shard_map/ppermute | solution.py:45
  133.2 4.0 %multiply_reduce_fusion = (f32[384]{0:T(512)S(1)}, f32[384,512]{1,0:T(8,128)}) fusion(bf16[384,512]{1,0:T(8,128)(2,1)} %collective-permute-done.4, bf16[384,512]{1,0:T(8,128)(2,1)} %collective-permute-done.3, bf16[384,512]{1,0:T(8,128)(2,1)} %collective-permute-done.2, bf16[384,4,512]{0,2,1:T(8,128)(2,1)S(1)} %bitcast.87, ...), kind=kOutput, calls=%fused_computation.44 | convolution fusion | flops 807272064 | bytes 6030852 | tf_op jit(solution)/shard_map/iqh,qhf->if/dot_general | solution.py:40
  137.2 2.7 %collective-permute-start.5 = (f32[384]{0:T(512)S(1)}, f32[384]{0:T(512)S(1)}, u32[]{:S(2)}, u32[]{:S(2)}) collective-permute-start(f32[384]{0:T(512)S(1)} %get-tuple-element.11), channel_id=1, source_target_pairs={{0,1},{1,0},{2,3},{3,2},{4,5},{5,4},{6,7},{7,6},{8,9},{9,8},{10,11... | collective-permute-start | bytes 4616 | tf_op jit(solution)/shard_map/ppermute | solution.py:50
  141.1 2.4 %collective-permute-done.6 = f32[384]{0:T(512)S(1)} collective-permute-done((f32[384]{0:T(512)S(1)}, f32[384]{0:T(512)S(1)}, u32[]{:S(2)}, u32[]{:S(2)}) %collective-permute-start.6) | collective-permute-done | bytes 1568 | tf_op jit(solution)/shard_map/ppermute | solution.py:50
  143.6 2.3 %collective-permute-start.7 = (f32[384]{0:T(512)S(1)}, f32[384]{0:T(512)S(1)}, u32[]{:S(2)}, u32[]{:S(2)}) collective-permute-start(f32[384]{0:T(512)S(1)} %add.108), channel_id=1, source_target_pairs={{0,4},{4,0},{8,12},{12,8},{1,5},{5,1},{9,13},{13,9},{2,6},{6,2},{1... | collective-permute-start | bytes 4616 | tf_op jit(solution)/shard_map/ppermute | solution.py:50
  146.9 4.5 %collective-permute-start.8 = (f32[384]{0:T(512)S(1)}, f32[384]{0:T(512)S(1)}, u32[]{:S(2)}, u32[]{:S(2)}) collective-permute-start(f32[384]{0:T(512)S(1)} %add.109), channel_id=1, source_target_pairs={{0,8},{4,12},{8,0},{12,4},{1,9},{5,13},{9,1},{13,5},{2,10},{6,14},... | collective-permute-start | bytes 4616 | tf_op jit(solution)/shard_map/ppermute | solution.py:50
  153.3 2.1 fusion.65
  161.1 34.9 %all-gather.4.cloned.1.call-done = bf16[1536,512]{1,0:T(8,128)(2,1)} async-done(((bf16[96,512]{1,0:T(8,128)(2,1)}), bf16[1536,512]{1,0:T(8,128)(2,1)}) %all-gather.4.cloned.1.call-update) | async-done | bytes 1572880 | tf_op jit(solution)/shard_map/all_gather | solution.py:59
  196.0 3.0 %fusion.20 = f32[1,512,640]{2,1,0:T(8,128)S(1)} fusion(bf16[1536,640]{1,0:T(8,128)(2,1)S(1)} %copy-done, s32[]{:T(128)S(6)} %select_n.67, bf16[1536,512]{1,0:T(8,128)(2,1)} %all-gather.4.cloned.1.call-done), kind=kOutput, calls=%fused_computation.22 | convolution fusion | flops 1006632960 | bytes 4849668 | tf_op jit(solution)/shard_map/dot_general | solution.py:66
  203.5 2.8 %maximum_multiply_fusion = f32[4,512,640]{2,1,0:T(8,128)} fusion(f32[1,512,640]{2,1,0:T(8,128)S(1)} %fusion.29, f32[1,512,640]{2,1,0:T(8,128)S(1)} %fusion.26, f32[1,512,640]{2,1,0:T(8,128)S(1)} %fusion.23, f32[1,512,640]{2,1,0:T(8,128)S(1)} %fusion.20), kind=kLoop, calls=%fused_computation | loop fusion | flops 5242880 | bytes 10485760 | tf_op jit(solution)/shard_map/mul | solution.py:67
  (33 shorter events, 11.6 us)
Async XLA Ops:
  6.5 189.5 %copy-start = (bf16[1536,640]{1,0:T(8,128)(2,1)S(1)}, bf16[1536,640]{1,0:T(8,128)(2,1)}, u32[]{:S(2)}) copy-start(bf16[1536,640]{1,0:T(8,128)(2,1)} %param.13) | copy-start | bytes 5898244
  6.5 78.1 %all-gather.6.cloned.1.call-start = ((), (), s32[]{:S(2)}) async-start(), calls=%async_computation.1 | async-start | bytes 8912896 | tf_op jit(solution)/shard_map/all_gather | solution.py:34
  6.5 17.0 %collective-permute-start.1 = (bf16[512,512]{1,0:T(8,128)(2,1)}, bf16[512,512]{1,0:T(8,128)(2,1)S(1)}, u32[]{:S(2)}, u32[]{:S(2)}) collective-permute-start(bf16[512,512]{1,0:T(8,128)(2,1)} %param.8), channel_id=1, source_target_pairs={{0,0},{16,1},{32,2},{48,3},{4,4},{20,5},{36,6},{52,7},{8,8},{24,9}... | collective-permute-start | bytes 1572872 | tf_op jit(solution)/shard_map/ppermute | solution.py:23
  23.5 0.8 copy-start.2
  24.3 171.7 %all-gather.4.cloned.1.call-start = ((), (), s32[]{:S(2)}) async-start(), calls=%async_computation | async-start | bytes 1671168 | tf_op jit(solution)/shard_map/all_gather | solution.py:59
  38.4 22.3 %collective-permute-start = (bf16[384,1024]{0,1:T(8,128)(2,1)S(1)}, bf16[384,1024]{0,1:T(8,128)(2,1)S(1)}, u32[]{:S(2)}, u32[]{:S(2)}) collective-permute-start(bf16[384,1024]{0,1:T(8,128)(2,1)S(1)} %all_gather.12), channel_id=1, source_target_pairs={{0,2},{2,0},{1,3},{3,1},{4,6},{6,4},{5,7},{7,5},{8,10},{10,8},{9,1... | collective-permute-start | bytes 2359304 | tf_op jit(solution)/shard_map/ppermute | solution.py:31
  88.0 18.5 %collective-permute-start.2 = (bf16[384,512]{1,0:T(8,128)(2,1)}, bf16[384,512]{1,0:T(8,128)(2,1)}, u32[]{:S(2)}, u32[]{:S(2)}) collective-permute-start(bf16[384,512]{1,0:T(8,128)(2,1)} %fusion.62), channel_id=1, source_target_pairs={{0,4},{4,8},{8,12},{12,0},{1,5},{5,9},{9,13},{13,1},{2,6},{6,10},{... | collective-permute-start | bytes 1179656 | tf_op jit(solution)/shard_map/ppermute | solution.py:45
  93.6 27.9 %collective-permute-start.3 = (bf16[384,512]{1,0:T(8,128)(2,1)}, bf16[384,512]{1,0:T(8,128)(2,1)}, u32[]{:S(2)}, u32[]{:S(2)}) collective-permute-start(bf16[384,512]{1,0:T(8,128)(2,1)} %fusion.59), channel_id=1, source_target_pairs={{0,8},{4,12},{8,0},{12,4},{1,9},{5,13},{9,1},{13,5},{2,10},{6,14},... | collective-permute-start | bytes 1179656 | tf_op jit(solution)/shard_map/ppermute | solution.py:45
  100.6 32.6 %collective-permute-start.4 = (bf16[384,512]{1,0:T(8,128)(2,1)}, bf16[384,512]{1,0:T(8,128)(2,1)}, u32[]{:S(2)}, u32[]{:S(2)}) collective-permute-start(bf16[384,512]{1,0:T(8,128)(2,1)} %fusion.56), channel_id=1, source_target_pairs={{0,12},{4,0},{8,4},{12,8},{1,13},{5,1},{9,5},{13,9},{2,14},{6,2},{... | collective-permute-start | bytes 1179656 | tf_op jit(solution)/shard_map/ppermute | solution.py:45
  103.7 42.2 %copy-start.4 = (s32[1,384]{1,0:T(1,128)S(1)}, s32[1,384]{1,0:T(1,128)}, u32[]{:S(2)}) copy-start(s32[1,384]{1,0:T(1,128)} %param.11) | copy-start | bytes 4612
  103.7 49.6 %copy-start.5 = (f32[512]{0:T(512)S(1)}, f32[512]{0:T(512)}, u32[]{:S(2)}) copy-start(f32[512]{0:T(512)} %param.10) | copy-start | bytes 6148
  103.7 51.7 %copy-start.3 = (s32[4]{0:T(128)S(1)}, s32[4]{0:T(128)}, u32[]{:S(2)}) copy-start(s32[4]{0:T(128)} %param.12) | copy-start | bytes 52
  137.2 3.9 %collective-permute-start.5 = (f32[384]{0:T(512)S(1)}, f32[384]{0:T(512)S(1)}, u32[]{:S(2)}, u32[]{:S(2)}) collective-permute-start(f32[384]{0:T(512)S(1)} %get-tuple-element.11), channel_id=1, source_target_pairs={{0,1},{1,0},{2,3},{3,2},{4,5},{5,4},{6,7},{7,6},{8,9},{9,8},{10,11... | collective-permute-start | bytes 4616 | tf_op jit(solution)/shard_map/ppermute | solution.py:50
  141.1 2.4 %collective-permute-start.6 = (f32[384]{0:T(512)S(1)}, f32[384]{0:T(512)S(1)}, u32[]{:S(2)}, u32[]{:S(2)}) collective-permute-start(f32[384]{0:T(512)S(1)} %add.107), channel_id=1, source_target_pairs={{0,2},{2,0},{1,3},{3,1},{4,6},{6,4},{5,7},{7,5},{8,10},{10,8},{9,1... | collective-permute-start | bytes 4616 | tf_op jit(solution)/shard_map/ppermute | solution.py:50
  143.6 3.3 %collective-permute-start.7 = (f32[384]{0:T(512)S(1)}, f32[384]{0:T(512)S(1)}, u32[]{:S(2)}, u32[]{:S(2)}) collective-permute-start(f32[384]{0:T(512)S(1)} %add.108), channel_id=1, source_target_pairs={{0,4},{4,0},{8,12},{12,8},{1,5},{5,1},{9,13},{13,9},{2,6},{6,2},{1... | collective-permute-start | bytes 4616 | tf_op jit(solution)/shard_map/ppermute | solution.py:50
  146.9 6.3 %collective-permute-start.8 = (f32[384]{0:T(512)S(1)}, f32[384]{0:T(512)S(1)}, u32[]{:S(2)}, u32[]{:S(2)}) collective-permute-start(f32[384]{0:T(512)S(1)} %add.109), channel_id=1, source_target_pairs={{0,8},{4,12},{8,0},{12,4},{1,9},{5,13},{9,1},{13,5},{2,10},{6,14},... | collective-permute-start | bytes 4616 | tf_op jit(solution)/shard_map/ppermute | solution.py:50
  196.0 3.0 %copy-start.1 = (bf16[1536,512]{1,0:T(8,128)(2,1)S(1)}, bf16[1536,512]{1,0:T(8,128)(2,1)}, u32[]{:S(2)}) copy-start(bf16[1536,512]{1,0:T(8,128)(2,1)} %all-gather.4.cloned.1.call-done) | copy-start | bytes 4718596
Sparse Core Ops, SparseCore 0:
  24.5 60.0 all-gather.5
  155.5 40.5 all-gather.3

commit v12 on v10

--- a/solution.py
+++ b/solution.py
@@ -27,10 +27,15 @@
     quad = lax.axis_size(("zlo", "xhi"))
     ring = lax.axis_size("zhi")
     heads = attention.shape[1]
-    pair = lax.all_gather(attention, "xhi", axis=1, tiled=True)
-    other = lax.ppermute(pair, "zlo", [(0, 1), (1, 0)])
-    low = lax.axis_index("zlo") == 0
-    slab = jnp.concatenate([jnp.where(low, pair, other), jnp.where(low, other, pair)], axis=1)
+    quad_axes = ("zlo", "xhi")
+    by_xor = jnp.stack(
+        [attention]
+        + [lax.ppermute(attention, quad_axes, [(i, i ^ m) for i in range(quad)]) for m in range(1, quad)]
+    )
+    mine = lax.axis_index(quad_axes)
+    slab = jnp.concatenate(
+        [lax.dynamic_index_in_dim(by_xor, q ^ mine, 0, keepdims=False) for q in range(quad)], axis=1
+    )
     blocks = lax.all_gather(ring_block(out_weight), GROUP, axis=0).reshape(ring, quad, heads, -1)
     partial = jnp.einsum(
         "iqh,rqhf->irf", slab.reshape(-1, quad, heads), blocks, preferred_element_type=jnp.float32

time: 211 us -> 217 us (1.028)
  blocking collectives: 57.2 us -> 40.1 us
  waiting for transfers between devices: 94.6 us -> 111 us
  starting transfers between devices: 17.7 us -> 24.5 us
    all_gather x1, waiting for transfers between devices: 23.6 us -> 37.9 us  [on_device(): lax.all_gather(ring_block(out_weight), GROUP, axis=0)]
    all_gather x1 -> x0, blocking collectives: 12.8 us -> none  [on_device(): pair = lax.all_gather(attention, 'xhi', axis=1, tiled=True)]
    all_to_all x1, blocking collectives: 44.4 us -> 40.1 us  [on_device(): lax.all_to_all(partial.astype(jnp.bfloat16), 'zhi', 1, 1, tiled=True)]
    ppermute x4, starting transfers between devices: 7.15 us -> 10.9 us  [on_device(): lax.ppermute(squares, axis, [(i, i ^ mask) for i in range(size)])]
    ppermute x1 -> x3, starting transfers between devices: 4.39 us -> 7.47 us  [on_device(): lax.ppermute(attention, quad_axes, [(i, i ^ m) for i in range(quad)])]
    ppermute x1 -> x3, waiting for transfers between devices: 17.9 us -> 17.7 us  [on_device(): lax.ppermute(attention, quad_axes, [(i, i ^ m) for i in range(quad)])]
  transfers between devices with their start and end apart: 8 -> 10, of which waited for: 8 -> 9; matrix products, arithmetic and copies ran while one was open for 1% -> 1% of each run, Pallas kernels for 0% -> 0%
where the time goes in v12:
time: 217 us
  waiting for transfers between devices  111 us (51%)
  blocking collectives  40.1 us (18%)
  starting transfers between devices  24.5 us (11%)
  between operations  18.7 us (9%)
  matrix products  15.2 us (7%)
  other arithmetic  4.59 us (2%)
  local copies, waits for them, and re-layouts  2.32 us (1%)
    all_to_all x1, blocking collectives, on_device(): lax.all_to_all(partial.astype(jnp.bfloat16), 'zhi', 1, 1, tiled=True)  40.1 us
    all_gather x1, waiting for transfers between devices, on_device(): lax.all_gather(ring_block(out_weight), GROUP, axis=0)  37.9 us
    all_gather x1, waiting for transfers between devices, on_device(): story = lax.all_gather(binned, GROUP, axis=0, tiled=True)  33.9 us
    ppermute x3, waiting for transfers between devices, on_device(): lax.ppermute(attention, quad_axes, [(i, i ^ m) for i in range(quad)])  17.7 us
    ppermute x4, waiting for transfers between devices, on_device(): lax.ppermute(squares, axis, [(i, i ^ mask) for i in range(size)])  11 us
    ppermute x4, starting transfers between devices, on_device(): lax.ppermute(squares, axis, [(i, i ^ mask) for i in range(size)])  10.9 us
    ppermute x1, waiting for transfers between devices, ring_block(): return lax.ppermute(block, GROUP + TENSOR, route)  10.8 us
    ppermute x3, starting transfers between devices, on_device(): lax.ppermute(attention, quad_axes, [(i, i ^ m) for i in range(quad)])  7.47 us
  transfers between devices with their start and end apart: 10, of which 9 were waited for; matrix products, arithmetic and copies ran while one was open for 1% of the time, Pallas kernels for 0%

profile of v12, /device:TPU:1, one launch (start us, length us, event | category | flops | bytes accessed | tf_op | source)
XLA Modules:
  0.0 216.7 jit_solution(9467682581662071850)
XLA Ops:
  6.5 6.1 %collective-permute-start.3 = (bf16[512,512]{1,0:T(8,128)(2,1)}, bf16[512,512]{1,0:T(8,128)(2,1)S(1)}, u32[]{:S(2)}, u32[]{:S(2)}) collective-permute-start(bf16[512,512]{1,0:T(8,128)(2,1)} %param.8), channel_id=1, source_target_pairs={{0,0},{16,1},{32,2},{48,3},{4,4},{20,5},{36,6},{52,7},{8,8},{24,9}... | collective-permute-start | bytes 1572872 | tf_op jit(solution)/shard_map/ppermute | solution.py:23
  12.7 10.8 %collective-permute-done.3 = bf16[512,512]{1,0:T(8,128)(2,1)S(1)} collective-permute-done((bf16[512,512]{1,0:T(8,128)(2,1)}, bf16[512,512]{1,0:T(8,128)(2,1)S(1)}, u32[]{:S(2)}, u32[]{:S(2)}) %collective-permute-start.3) | collective-permute-done | bytes 524320 | tf_op jit(solution)/shard_map/ppermute | solution.py:23
  24.5 4.8 %collective-permute-start.1 = (bf16[384,512]{1,0:T(8,128)(2,1)}, bf16[384,512]{1,0:T(8,128)(2,1)S(1)}, u32[]{:S(2)}, u32[]{:S(2)}) collective-permute-start(bf16[384,512]{1,0:T(8,128)(2,1)} %param.7), channel_id=1, source_target_pairs={{0,2},{1,3},{2,0},{3,1},{4,6},{5,7},{6,4},{7,5},{8,10},{9,11},{10,... | collective-permute-start | bytes 1179656 | tf_op jit(solution)/shard_map/ppermute | solution.py:33
  29.3 2.6 %collective-permute-start.2 = (bf16[384,512]{1,0:T(8,128)(2,1)}, bf16[384,512]{1,0:T(8,128)(2,1)S(1)}, u32[]{:S(2)}, u32[]{:S(2)}) collective-permute-start(bf16[384,512]{1,0:T(8,128)(2,1)} %param.7), channel_id=1, source_target_pairs={{0,3},{1,2},{2,1},{3,0},{4,7},{5,6},{6,5},{7,4},{8,11},{9,10},{10,... | collective-permute-start | bytes 1179656 | tf_op jit(solution)/shard_map/ppermute | solution.py:33
  31.9 5.0 %collective-permute-done = bf16[384,512]{1,0:T(8,128)(2,1)S(1)} collective-permute-done((bf16[384,512]{1,0:T(8,128)(2,1)}, bf16[384,512]{1,0:T(8,128)(2,1)S(1)}, u32[]{:S(2)}, u32[]{:S(2)}) %collective-permute-start) | collective-permute-done | bytes 393248 | tf_op jit(solution)/shard_map/ppermute | solution.py:33
  36.8 12.7 %collective-permute-done.2 = bf16[384,512]{1,0:T(8,128)(2,1)S(1)} collective-permute-done((bf16[384,512]{1,0:T(8,128)(2,1)}, bf16[384,512]{1,0:T(8,128)(2,1)S(1)}, u32[]{:S(2)}, u32[]{:S(2)}) %collective-permute-start.2) | collective-permute-done | bytes 393248 | tf_op jit(solution)/shard_map/ppermute | solution.py:33
  49.5 1.2 pad_maximum_fusion
  50.9 37.9 %all-gather.6.cloned.1.call-done = bf16[8192,512]{1,0:T(8,128)(2,1)} async-done(((bf16[512,512]{1,0:T(8,128)(2,1)}), bf16[8192,512]{1,0:T(8,128)(2,1)}) %all-gather.6.cloned.1.call-update) | async-done | bytes 8388624 | tf_op jit(solution)/shard_map/all_gather | solution.py:39
  88.8 6.8 %bitcast_convert_fusion = bf16[384,4,512]{2,0,1:T(8,128)(2,1)S(1)} fusion(bf16[4,4,512,512]{3,2,1,0:T(8,128)(2,1)} %bitcast.44, bf16[384,1,512]{2,0,1:T(8,128)(2,1)S(1)} %get-tuple-element.6, bf16[384,1,512]{2,0,1:T(8,128)(2,1)S(1)} %get-tuple-element.7, bf16[384,1,512]{2,0,1:T(8,128)(2,1)S(1)} %get-tuple-element.8, ...), kind=kOutput, calls=%fused_computation.1 | convolution fusion | flops 3228303360 | bytes 11534336 | tf_op jit(solution)/shard_map/iqh,rqhf->irf/dot_general | solution.py:40
  95.5 40.1 %all_to_all.5 = bf16[384,4,512]{2,0,1:T(8,128)(2,1)S(1)} all-to-all(bf16[384,4,512]{2,0,1:T(8,128)(2,1)S(1)} %bitcast_convert_fusion), channel_id=1, replica_groups=mesh['xlo'=2,'y'=4,'core'=2,'zhi'=4,'zlo'=2,'xhi'=2] {'zhi'}, dimensions={1} | all-to-all | bytes 3145728 | tf_op jit(solution)/shard_map/all_to_all | solution.py:43
  136.8 1.3 collective-permute-start.4
  138.1 2.8 %collective-permute-done.4 = f32[384]{0:T(512)S(1)} collective-permute-done((f32[384]{0:T(512)S(1)}, f32[384]{0:T(512)S(1)}, u32[]{:S(2)}, u32[]{:S(2)}) %collective-permute-start.4) | collective-permute-done | bytes 1568 | tf_op jit(solution)/shard_map/ppermute | solution.py:49
  140.9 7.3 %collective-permute-start.5 = (f32[384]{0:T(512)S(1)}, f32[384]{0:T(512)S(1)}, u32[]{:S(2)}, u32[]{:S(2)}) collective-permute-start(f32[384]{0:T(512)S(1)} %add.70), channel_id=1, source_target_pairs={{0,2},{2,0},{1,3},{3,1},{4,6},{6,4},{5,7},{7,5},{8,10},{10,8},{9,1... | collective-permute-start | bytes 4616 | tf_op jit(solution)/shard_map/ppermute | solution.py:49
  148.2 1.0 collective-permute-done.5
  149.6 2.9 %collective-permute-done.6 = f32[384]{0:T(512)S(1)} collective-permute-done((f32[384]{0:T(512)S(1)}, f32[384]{0:T(512)S(1)}, u32[]{:S(2)}, u32[]{:S(2)}) %collective-permute-start.6) | collective-permute-done | bytes 1568 | tf_op jit(solution)/shard_map/ppermute | solution.py:49
  152.5 1.8 collective-permute-start.7
  154.4 4.4 %collective-permute-done.7 = f32[384]{0:T(512)S(1)} collective-permute-done((f32[384]{0:T(512)S(1)}, f32[384]{0:T(512)S(1)}, u32[]{:S(2)}, u32[]{:S(2)}) %collective-permute-start.7) | collective-permute-done | bytes 1568 | tf_op jit(solution)/shard_map/ppermute | solution.py:49
  158.9 1.0 fusion.26
  165.7 33.9 %all-gather.4.cloned.1.call-done = bf16[1536,512]{1,0:T(8,128)(2,1)} async-done(((bf16[96,512]{1,0:T(8,128)(2,1)}), bf16[1536,512]{1,0:T(8,128)(2,1)}) %all-gather.4.cloned.1.call-update) | async-done | bytes 1572880 | tf_op jit(solution)/shard_map/all_gather | solution.py:58
  199.6 3.0 %fusion.14 = f32[1,512,640]{2,1,0:T(8,128)S(1)} fusion(bf16[1536,640]{1,0:T(8,128)(2,1)S(1)} %copy-done, s32[]{:T(128)S(6)} %select_n.29, bf16[1536,512]{1,0:T(8,128)(2,1)} %all-gather.4.cloned.1.call-done), kind=kOutput, calls=%fused_computation.19 | convolution fusion | flops 1006632960 | bytes 4849668 | tf_op jit(solution)/shard_map/dot_general | solution.py:65
  202.6 1.5 fusion.17
  204.1 1.5 fusion.20
  205.6 1.5 fusion.23
  207.1 2.8 %maximum_multiply_fusion = f32[4,512,640]{2,1,0:T(8,128)} fusion(f32[1,512,640]{2,1,0:T(8,128)S(1)} %fusion.23, f32[1,512,640]{2,1,0:T(8,128)S(1)} %fusion.20, f32[1,512,640]{2,1,0:T(8,128)S(1)} %fusion.17, f32[1,512,640]{2,1,0:T(8,128)S(1)} %fusion.14), kind=kLoop, calls=%fused_computation | loop fusion | flops 5242880 | bytes 10485760 | tf_op jit(solution)/shard_map/mul | solution.py:66
  (31 shorter events, 3.5 us)
Async XLA Ops:
  6.5 193.1 %copy-start = (bf16[1536,640]{1,0:T(8,128)(2,1)S(1)}, bf16[1536,640]{1,0:T(8,128)(2,1)}, u32[]{:S(2)}) copy-start(bf16[1536,640]{1,0:T(8,128)(2,1)} %param.13) | copy-start | bytes 5898244
  6.5 82.2 %all-gather.6.cloned.1.call-start = ((), (), s32[]{:S(2)}) async-start(), calls=%async_computation.2 | async-start | bytes 8912896 | tf_op jit(solution)/shard_map/all_gather | solution.py:39
  6.5 17.0 %collective-permute-start.3 = (bf16[512,512]{1,0:T(8,128)(2,1)}, bf16[512,512]{1,0:T(8,128)(2,1)S(1)}, u32[]{:S(2)}, u32[]{:S(2)}) collective-permute-start(bf16[512,512]{1,0:T(8,128)(2,1)} %param.8), channel_id=1, source_target_pairs={{0,0},{16,1},{32,2},{48,3},{4,4},{20,5},{36,6},{52,7},{8,8},{24,9}... | collective-permute-start | bytes 1572872 | tf_op jit(solution)/shard_map/ppermute | solution.py:23
  23.5 0.8 copy-start.2
  24.3 175.3 %all-gather.4.cloned.1.call-start = ((), (), s32[]{:S(2)}) async-start(), calls=%async_computation.1 | async-start | bytes 1671168 | tf_op jit(solution)/shard_map/all_gather | solution.py:58
  24.4 12.4 %collective-permute-start = (bf16[384,512]{1,0:T(8,128)(2,1)}, bf16[384,512]{1,0:T(8,128)(2,1)S(1)}, u32[]{:S(2)}, u32[]{:S(2)}) collective-permute-start(bf16[384,512]{1,0:T(8,128)(2,1)} %param.7), channel_id=1, source_target_pairs={{0,1},{1,0},{2,3},{3,2},{4,5},{5,4},{6,7},{7,6},{8,9},{9,8},{10,11... | collective-permute-start | bytes 1179656 | tf_op jit(solution)/shard_map/ppermute | solution.py:33
  24.5 12.3 %collective-permute-start.1 = (bf16[384,512]{1,0:T(8,128)(2,1)}, bf16[384,512]{1,0:T(8,128)(2,1)S(1)}, u32[]{:S(2)}, u32[]{:S(2)}) collective-permute-start(bf16[384,512]{1,0:T(8,128)(2,1)} %param.7), channel_id=1, source_target_pairs={{0,2},{1,3},{2,0},{3,1},{4,6},{5,7},{6,4},{7,5},{8,10},{9,11},{10,... | collective-permute-start | bytes 1179656 | tf_op jit(solution)/shard_map/ppermute | solution.py:33
  29.3 20.3 %collective-permute-start.2 = (bf16[384,512]{1,0:T(8,128)(2,1)}, bf16[384,512]{1,0:T(8,128)(2,1)S(1)}, u32[]{:S(2)}, u32[]{:S(2)}) collective-permute-start(bf16[384,512]{1,0:T(8,128)(2,1)} %param.7), channel_id=1, source_target_pairs={{0,3},{1,2},{2,1},{3,0},{4,7},{5,6},{6,5},{7,4},{8,11},{9,10},{10,... | collective-permute-start | bytes 1179656 | tf_op jit(solution)/shard_map/ppermute | solution.py:33
  135.7 1.0 copy-start.3
  135.7 14.0 %copy-start.5 = (s32[1,384]{1,0:T(1,128)S(1)}, s32[1,384]{1,0:T(1,128)}, u32[]{:S(2)}) copy-start(s32[1,384]{1,0:T(1,128)} %param.11) | copy-start | bytes 4612
  135.7 23.2 %copy-start.6 = (f32[512]{0:T(512)S(1)}, f32[512]{0:T(512)}, u32[]{:S(2)}) copy-start(f32[512]{0:T(512)} %param.10) | copy-start | bytes 6148
  136.7 23.2 %copy-start.4 = (s32[4]{0:T(128)S(1)}, s32[4]{0:T(128)}, u32[]{:S(2)}) copy-start(s32[4]{0:T(128)} %param.12) | copy-start | bytes 52
  136.8 4.0 %collective-permute-start.4 = (f32[384]{0:T(512)S(1)}, f32[384]{0:T(512)S(1)}, u32[]{:S(2)}, u32[]{:S(2)}) collective-permute-start(f32[384]{0:T(512)S(1)} %multiply_reduce_fusion), channel_id=1, source_target_pairs={{0,1},{1,0},{2,3},{3,2},{4,5},{5,4},{6,7},{7,6},{8,9},{9,8},{10,11... | collective-permute-start | bytes 4616 | tf_op jit(solution)/shard_map/ppermute | solution.py:49
  140.9 8.3 %collective-permute-start.5 = (f32[384]{0:T(512)S(1)}, f32[384]{0:T(512)S(1)}, u32[]{:S(2)}, u32[]{:S(2)}) collective-permute-start(f32[384]{0:T(512)S(1)} %add.70), channel_id=1, source_target_pairs={{0,2},{2,0},{1,3},{3,1},{4,6},{6,4},{5,7},{7,5},{8,10},{10,8},{9,1... | collective-permute-start | bytes 4616 | tf_op jit(solution)/shard_map/ppermute | solution.py:49
  149.2 3.3 %collective-permute-start.6 = (f32[384]{0:T(512)S(1)}, f32[384]{0:T(512)S(1)}, u32[]{:S(2)}, u32[]{:S(2)}) collective-permute-start(f32[384]{0:T(512)S(1)} %add.71), channel_id=1, source_target_pairs={{0,4},{4,0},{8,12},{12,8},{1,5},{5,1},{9,13},{13,9},{2,6},{6,2},{1... | collective-permute-start | bytes 4616 | tf_op jit(solution)/shard_map/ppermute | solution.py:49
  152.5 6.3 %collective-permute-start.7 = (f32[384]{0:T(512)S(1)}, f32[384]{0:T(512)S(1)}, u32[]{:S(2)}, u32[]{:S(2)}) collective-permute-start(f32[384]{0:T(512)S(1)} %add.72), channel_id=1, source_target_pairs={{0,8},{4,12},{8,0},{12,4},{1,9},{5,13},{9,1},{13,5},{2,10},{6,14},... | collective-permute-start | bytes 4616 | tf_op jit(solution)/shard_map/ppermute | solution.py:49
  199.6 3.0 %copy-start.1 = (bf16[1536,512]{1,0:T(8,128)(2,1)S(1)}, bf16[1536,512]{1,0:T(8,128)(2,1)}, u32[]{:S(2)}) copy-start(bf16[1536,512]{1,0:T(8,128)(2,1)} %all-gather.4.cloned.1.call-done) | copy-start | bytes 4718596
Sparse Core Ops, SparseCore 0:
  24.5 64.2 all-gather.5
  160.0 39.6 all-gather.3

commit v13 on v10

--- a/solution.py
+++ b/solution.py
@@ -36,7 +36,8 @@
         "iqh,rqhf->irf", slab.reshape(-1, quad, heads), blocks, preferred_element_type=jnp.float32
     )
     received = lax.all_to_all(partial.astype(jnp.bfloat16), "zhi", 1, 1, tiled=True)
-    summed = jnp.sum(received.astype(jnp.float32), axis=1)
+    kept = (jnp.arange(ring) == lax.axis_index("zhi"))[None, :, None]
+    summed = jnp.sum(jnp.where(kept, partial, received.astype(jnp.float32)), axis=1)
     hidden = residual.astype(jnp.float32) + summed
     squares = jnp.sum(hidden * hidden, axis=1)
     for axis, mask in (("xhi", 1), ("zlo", 1), ("zhi", 1), ("zhi", 2)):

time: 211 us -> 217 us (1.028)
  blocking collectives: 57.2 us -> 12.8 us
  waiting for transfers between devices: 94.6 us -> 131 us
  starting transfers between devices: 17.7 us -> 25.2 us
  matrix products: 15.2 us -> 18.7 us
  other arithmetic: 3.7 us -> 6.03 us
    all_to_all x1 -> x0, blocking collectives: 44.4 us -> none  [on_device(): lax.all_to_all(partial.astype(jnp.bfloat16), 'zhi', 1, 1, tiled=True)]
    all_to_all x0 -> x1, waiting for transfers between devices: none -> 37.3 us  [on_device(): lax.all_to_all(partial.astype(jnp.bfloat16), 'zhi', 1, 1, tiled=True)]
    all_to_all x0 -> x1, starting transfers between devices: none -> 6.72 us  [on_device(): lax.all_to_all(partial.astype(jnp.bfloat16), 'zhi', 1, 1, tiled=True)]
    reduce_sum x1, other arithmetic: 0.25 us -> 2.58 us  [on_device(): jnp.sum(jnp.where(kept, partial, received.astype(jnp.float32)), axis=1)]
    dot_general x1, matrix products: 6.83 us -> 9.07 us  [on_device(): jnp.einsum('iqh,rqhf->irf', slab.reshape(-1, quad, heads), blocks, prefer...]
  transfers between devices with their start and end apart: 8 -> 9, of which waited for: 8 -> 9; matrix products, arithmetic and copies ran while one was open for 1% -> 1% of each run, Pallas kernels for 0% -> 0%
where the time goes in v13:
time: 217 us; the launch traced here: 216 us
  waiting for transfers between devices  131 us (60%)
  starting transfers between devices  25.2 us (12%)
  matrix products  18.7 us (9%)
  between operations  18.7 us (9%)
  blocking collectives  12.8 us (6%)
  other arithmetic  6.03 us (3%)
  local copies, waits for them, and re-layouts  3.56 us (2%)
    all_to_all x1, waiting for transfers between devices, on_device(): lax.all_to_all(partial.astype(jnp.bfloat16), 'zhi', 1, 1, tiled=True)  37.3 us
    all_gather x1, waiting for transfers between devices, on_device(): story = lax.all_gather(binned, GROUP, axis=0, tiled=True)  32.9 us
    all_gather x1, waiting for transfers between devices, on_device(): lax.all_gather(ring_block(out_weight), GROUP, axis=0)  23.7 us
    ppermute x1, waiting for transfers between devices, on_device(): other = lax.ppermute(pair, 'zlo', [(0, 1), (1, 0)])  17.9 us
    all_gather x1, blocking collectives, on_device(): pair = lax.all_gather(attention, 'xhi', axis=1, tiled=True)  12.8 us
    ppermute x1, waiting for transfers between devices, ring_block(): return lax.ppermute(block, GROUP + TENSOR, route)  10.8 us
    dot_general x1, matrix products, on_device(): jnp.einsum('iqh,rqhf->irf', slab.reshape(-1, quad, heads), blocks, prefer...  9.07 us
    ppermute x4, waiting for transfers between devices, on_device(): lax.ppermute(squares, axis, [(i, i ^ mask) for i in range(size)])  8.78 us
  transfers between devices with their start and end apart: 9, of which 9 were waited for; matrix products, arithmetic and copies ran while one was open for 1% of the time, Pallas kernels for 0%

profile of v13, /device:TPU:1, one launch (start us, length us, event | category | flops | bytes accessed | tf_op | source)
XLA Modules:
  0.0 216.4 jit_solution(10181869282855615707)
XLA Ops:
  6.5 6.1 %collective-permute-start.1 = (bf16[512,512]{1,0:T(8,128)(2,1)}, bf16[512,512]{1,0:T(8,128)(2,1)S(1)}, u32[]{:S(2)}, u32[]{:S(2)}) collective-permute-start(bf16[512,512]{1,0:T(8,128)(2,1)} %param.8), channel_id=1, source_target_pairs={{0,0},{16,1},{32,2},{48,3},{4,4},{20,5},{36,6},{52,7},{8,8},{24,9}... | collective-permute-start | bytes 1572872 | tf_op jit(solution)/shard_map/ppermute | solution.py:23
  12.7 10.8 %collective-permute-done.1 = bf16[512,512]{1,0:T(8,128)(2,1)S(1)} collective-permute-done((bf16[512,512]{1,0:T(8,128)(2,1)}, bf16[512,512]{1,0:T(8,128)(2,1)S(1)}, u32[]{:S(2)}, u32[]{:S(2)}) %collective-permute-start.1) | collective-permute-done | bytes 524320 | tf_op jit(solution)/shard_map/ppermute | solution.py:23
  24.3 1.2 copy.10
  25.6 12.8 %all_gather.12 = bf16[384,1024]{0,1:T(8,128)(2,1)S(1)} all-gather(bf16[384,512]{0,1:T(8,128)(2,1)S(1)} %copy.10), channel_id=1, replica_groups=mesh['xlo'=2,'y'=4,'core'=2,'zhi'=4,'zlo'=2,'xhi'=2] {'xhi'}, dimensions={1}, use_global_device_ids=true | all-gather | bytes 1179648 | tf_op jit(solution)/shard_map/all_gather | solution.py:30
  38.3 4.4 %collective-permute-start = (bf16[384,1024]{0,1:T(8,128)(2,1)S(1)}, bf16[384,1024]{0,1:T(8,128)(2,1)S(1)}, u32[]{:S(2)}, u32[]{:S(2)}) collective-permute-start(bf16[384,1024]{0,1:T(8,128)(2,1)S(1)} %all_gather.12), channel_id=1, source_target_pairs={{0,2},{2,0},{1,3},{3,1},{4,6},{6,4},{5,7},{7,5},{8,10},{10,8},{9,1... | collective-permute-start | bytes 2359304 | tf_op jit(solution)/shard_map/ppermute | solution.py:31
  42.7 17.9 %collective-permute-done = bf16[384,1024]{0,1:T(8,128)(2,1)S(1)} collective-permute-done((bf16[384,1024]{0,1:T(8,128)(2,1)S(1)}, bf16[384,1024]{0,1:T(8,128)(2,1)S(1)}, u32[]{:S(2)}, u32[]{:S(2)}) %collective-permute-start) | collective-permute-done | bytes 786464 | tf_op jit(solution)/shard_map/ppermute | solution.py:31
  60.9 23.7 %all-gather.6.cloned.1.call-done = bf16[8192,512]{1,0:T(8,128)(2,1)} async-done(((bf16[512,512]{1,0:T(8,128)(2,1)}), bf16[8192,512]{1,0:T(8,128)(2,1)}) %all-gather.6.cloned.1.call-update) | async-done | bytes 8388624 | tf_op jit(solution)/shard_map/all_gather | solution.py:34
  84.6 9.1 %bitcast_convert_fusion = (bf16[384,4,512]{2,0,1:T(8,128)(2,1)}, f32[384,4,512,1]{2,0,3,1:T(8,128)}) fusion(bf16[384,4,512,1]{0,2,1,3:T(8,128)(2,1)S(1)} %bitcast.32, bf16[4,4,512,512]{3,2,1,0:T(8,128)(2,1)} %bitcast.33), kind=kOutput, calls=%fused_computation.2 | convolution fusion | flops 3222011904 | bytes 14680064 | tf_op jit(solution)/shard_map/iqh,rqhf->irf/dot_general | solution.py:35
  93.7 6.7 %all-to-all-start = ((bf16[384,4,512]{2,0,1:T(8,128)(2,1)}), bf16[384,4,512]{2,0,1:T(8,128)(2,1)S(1)}, u32[]{:S(2)}, u32[]{:S(2)}) async-start(bf16[384,4,512]{2,0,1:T(8,128)(2,1)} %get-tuple-element.11), calls=%async_computation | async-start | bytes 3145728 | tf_op jit(solution)/shard_map/all_to_all | solution.py:38
  100.4 37.3 %all-to-all-done = bf16[384,4,512]{2,0,1:T(8,128)(2,1)S(1)} async-done(((bf16[384,4,512]{2,0,1:T(8,128)(2,1)}), bf16[384,4,512]{2,0,1:T(8,128)(2,1)S(1)}, u32[]{:S(2)}, u32[]{:S(2)}) %all-to-all-start) | async-done | bytes 1572896 | tf_op jit(solution)/shard_map/all_to_all | solution.py:38
  137.7 2.6 %fusion = f32[384,512]{1,0:T(8,128)S(1)} fusion(f32[384,4,512,1]{2,0,3,1:T(8,128)} %get-tuple-element.12, bf16[384,4,512]{2,0,1:T(8,128)(2,1)S(1)} %all-to-all-done, pred[4]{0:T(512)(128)(4,1)S(1)} %iota_compare_fusion.2), kind=kLoop, calls=%fused_computation.3 | loop fusion | flops 2162688 | bytes 5505028 | tf_op jit(solution)/shard_map/reduce_sum | solution.py:40
  141.4 2.8 %collective-permute-start.2 = (f32[384]{0:T(512)S(1)}, f32[384]{0:T(512)S(1)}, u32[]{:S(2)}, u32[]{:S(2)}) collective-permute-start(f32[384]{0:T(512)S(1)} %multiply_reduce_fusion), channel_id=1, source_target_pairs={{0,1},{1,0},{2,3},{3,2},{4,5},{5,4},{6,7},{7,6},{8,9},{9,8},{10,11... | collective-permute-start | bytes 4616 | tf_op jit(solution)/shard_map/ppermute | solution.py:45
  144.2 1.2 collective-permute-done.2
  145.4 2.7 %collective-permute-done.3 = f32[384]{0:T(512)S(1)} collective-permute-done((f32[384]{0:T(512)S(1)}, f32[384]{0:T(512)S(1)}, u32[]{:S(2)}, u32[]{:S(2)}) %collective-permute-start.3) | collective-permute-done | bytes 1568 | tf_op jit(solution)/shard_map/ppermute | solution.py:45
  148.2 2.8 %collective-permute-start.4 = (f32[384]{0:T(512)S(1)}, f32[384]{0:T(512)S(1)}, u32[]{:S(2)}, u32[]{:S(2)}) collective-permute-start(f32[384]{0:T(512)S(1)} %add.50), channel_id=1, source_target_pairs={{0,4},{4,0},{8,12},{12,8},{1,5},{5,1},{9,13},{13,9},{2,6},{6,2},{1... | collective-permute-start | bytes 4616 | tf_op jit(solution)/shard_map/ppermute | solution.py:45
  152.0 2.4 %collective-permute-start.5 = (f32[384]{0:T(512)S(1)}, f32[384]{0:T(512)S(1)}, u32[]{:S(2)}, u32[]{:S(2)}) collective-permute-start(f32[384]{0:T(512)S(1)} %add.51), channel_id=1, source_target_pairs={{0,8},{4,12},{8,0},{12,4},{1,9},{5,13},{9,1},{13,5},{2,10},{6,14},... | collective-permute-start | bytes 4616 | tf_op jit(solution)/shard_map/ppermute | solution.py:45
  154.4 3.9 %collective-permute-done.5 = f32[384]{0:T(512)S(1)} collective-permute-done((f32[384]{0:T(512)S(1)}, f32[384]{0:T(512)S(1)}, u32[]{:S(2)}, u32[]{:S(2)}) %collective-permute-start.5) | collective-permute-done | bytes 1568 | tf_op jit(solution)/shard_map/ppermute | solution.py:45
  158.3 2.2 %fusion.21 = bf16[96,512]{1,0:T(8,128)(2,1)} fusion(f32[384,512]{1,0:T(8,128)} %copy-done.2, bf16[384,512]{1,0:T(8,128)(2,1)} %param.9, f32[512]{0:T(512)S(1)} %copy-done.7, f32[384]{0:T(512)S(1)} %add_rsqrt_fusion, f32[96]{0:T(128)S(1)} %convert_reduce_fusion, s32[384]{0:T(512)S(1)} %reduce), kind=kOutput, calls=%fused_computation.18 | convolution fusion | flops 38866944 | bytes 1283456 | tf_op jit(solution)/shard_map/dot_general | solution.py:50
  166.4 32.9 %all-gather.4.cloned.1.call-done = bf16[1536,512]{1,0:T(8,128)(2,1)} async-done(((bf16[96,512]{1,0:T(8,128)(2,1)}), bf16[1536,512]{1,0:T(8,128)(2,1)}) %all-gather.4.cloned.1.call-update) | async-done | bytes 1572880 | tf_op jit(solution)/shard_map/all_gather | solution.py:54
  199.3 3.0 %fusion.12 = f32[1,512,640]{2,1,0:T(8,128)S(1)} fusion(bf16[1536,640]{1,0:T(8,128)(2,1)S(1)} %copy-done, s32[]{:T(128)S(6)} %select_n.33, bf16[1536,512]{1,0:T(8,128)(2,1)} %all-gather.4.cloned.1.call-done), kind=kOutput, calls=%fused_computation.14 | convolution fusion | flops 1006632960 | bytes 4849668 | tf_op jit(solution)/shard_map/dot_general | solution.py:61
  202.3 1.5 fusion.15
  203.8 1.5 fusion.9
  205.3 1.5 fusion.18
  206.7 2.8 %maximum_multiply_fusion = f32[4,512,640]{2,1,0:T(8,128)} fusion(f32[1,512,640]{2,1,0:T(8,128)S(1)} %fusion.18, f32[1,512,640]{2,1,0:T(8,128)S(1)} %fusion.15, f32[1,512,640]{2,1,0:T(8,128)S(1)} %fusion.12, f32[1,512,640]{2,1,0:T(8,128)S(1)} %fusion.9), kind=kLoop, calls=%fused_computation | loop fusion | flops 5242880 | bytes 10485760 | tf_op jit(solution)/shard_map/mul | solution.py:62
  (33 shorter events, 4.0 us)
Async XLA Ops:
  6.5 192.8 %copy-start = (bf16[1536,640]{1,0:T(8,128)(2,1)S(1)}, bf16[1536,640]{1,0:T(8,128)(2,1)}, u32[]{:S(2)}) copy-start(bf16[1536,640]{1,0:T(8,128)(2,1)} %param.13) | copy-start | bytes 5898244
  6.5 78.1 %all-gather.6.cloned.1.call-start = ((), (), s32[]{:S(2)}) async-start(), calls=%async_computation.2 | async-start | bytes 8912896 | tf_op jit(solution)/shard_map/all_gather | solution.py:34
  6.5 17.0 %collective-permute-start.1 = (bf16[512,512]{1,0:T(8,128)(2,1)}, bf16[512,512]{1,0:T(8,128)(2,1)S(1)}, u32[]{:S(2)}, u32[]{:S(2)}) collective-permute-start(bf16[512,512]{1,0:T(8,128)(2,1)} %param.8), channel_id=1, source_target_pairs={{0,0},{16,1},{32,2},{48,3},{4,4},{20,5},{36,6},{52,7},{8,8},{24,9}... | collective-permute-start | bytes 1572872 | tf_op jit(solution)/shard_map/ppermute | solution.py:23
  23.5 0.8 copy-start.3
  38.3 22.3 %collective-permute-start = (bf16[384,1024]{0,1:T(8,128)(2,1)S(1)}, bf16[384,1024]{0,1:T(8,128)(2,1)S(1)}, u32[]{:S(2)}, u32[]{:S(2)}) collective-permute-start(bf16[384,1024]{0,1:T(8,128)(2,1)S(1)} %all_gather.12), channel_id=1, source_target_pairs={{0,2},{2,0},{1,3},{3,1},{4,6},{6,4},{5,7},{7,5},{8,10},{10,8},{9,1... | collective-permute-start | bytes 2359304 | tf_op jit(solution)/shard_map/ppermute | solution.py:31
  93.7 44.1 %all-to-all-start = ((bf16[384,4,512]{2,0,1:T(8,128)(2,1)}), bf16[384,4,512]{2,0,1:T(8,128)(2,1)S(1)}, u32[]{:S(2)}, u32[]{:S(2)}) async-start(bf16[384,4,512]{2,0,1:T(8,128)(2,1)} %get-tuple-element.11), calls=%async_computation | async-start | bytes 3145728 | tf_op jit(solution)/shard_map/all_to_all | solution.py:38
  100.4 98.9 %all-gather.4.cloned.1.call-start = ((), (), s32[]{:S(2)}) async-start(), calls=%async_computation.1 | async-start | bytes 1671168 | tf_op jit(solution)/shard_map/all_gather | solution.py:54
  137.7 3.5 %copy-start.4 = (bf16[384,512]{1,0:T(8,128)(2,1)S(1)}, bf16[384,512]{1,0:T(8,128)(2,1)}, u32[]{:S(2)}) copy-start(bf16[384,512]{1,0:T(8,128)(2,1)} %param.9) | copy-start | bytes 1179652
  137.7 13.2 %copy-start.6 = (s32[1,384]{1,0:T(1,128)S(1)}, s32[1,384]{1,0:T(1,128)}, u32[]{:S(2)}) copy-start(s32[1,384]{1,0:T(1,128)} %param.11) | copy-start | bytes 4612
  137.7 20.6 %copy-start.7 = (f32[512]{0:T(512)S(1)}, f32[512]{0:T(512)}, u32[]{:S(2)}) copy-start(f32[512]{0:T(512)} %param.10) | copy-start | bytes 6148
  140.3 0.9 copy-start.2
  141.2 19.3 %copy-start.5 = (s32[4]{0:T(128)S(1)}, s32[4]{0:T(128)}, u32[]{:S(2)}) copy-start(s32[4]{0:T(128)} %param.12) | copy-start | bytes 52
  141.4 4.0 %collective-permute-start.2 = (f32[384]{0:T(512)S(1)}, f32[384]{0:T(512)S(1)}, u32[]{:S(2)}, u32[]{:S(2)}) collective-permute-start(f32[384]{0:T(512)S(1)} %multiply_reduce_fusion), channel_id=1, source_target_pairs={{0,1},{1,0},{2,3},{3,2},{4,5},{5,4},{6,7},{7,6},{8,9},{9,8},{10,11... | collective-permute-start | bytes 4616 | tf_op jit(solution)/shard_map/ppermute | solution.py:45
  145.4 2.7 %collective-permute-start.3 = (f32[384]{0:T(512)S(1)}, f32[384]{0:T(512)S(1)}, u32[]{:S(2)}, u32[]{:S(2)}) collective-permute-start(f32[384]{0:T(512)S(1)} %add.49), channel_id=1, source_target_pairs={{0,2},{2,0},{1,3},{3,1},{4,6},{6,4},{5,7},{7,5},{8,10},{10,8},{9,1... | collective-permute-start | bytes 4616 | tf_op jit(solution)/shard_map/ppermute | solution.py:45
  148.2 3.8 %collective-permute-start.4 = (f32[384]{0:T(512)S(1)}, f32[384]{0:T(512)S(1)}, u32[]{:S(2)}, u32[]{:S(2)}) collective-permute-start(f32[384]{0:T(512)S(1)} %add.50), channel_id=1, source_target_pairs={{0,4},{4,0},{8,12},{12,8},{1,5},{5,1},{9,13},{13,9},{2,6},{6,2},{1... | collective-permute-start | bytes 4616 | tf_op jit(solution)/shard_map/ppermute | solution.py:45
  152.0 6.3 %collective-permute-start.5 = (f32[384]{0:T(512)S(1)}, f32[384]{0:T(512)S(1)}, u32[]{:S(2)}, u32[]{:S(2)}) collective-permute-start(f32[384]{0:T(512)S(1)} %add.51), channel_id=1, source_target_pairs={{0,8},{4,12},{8,0},{12,4},{1,9},{5,13},{9,1},{13,5},{2,10},{6,14},... | collective-permute-start | bytes 4616 | tf_op jit(solution)/shard_map/ppermute | solution.py:45
  199.3 3.0 %copy-start.1 = (bf16[1536,512]{1,0:T(8,128)(2,1)S(1)}, bf16[1536,512]{1,0:T(8,128)(2,1)}, u32[]{:S(2)}) copy-start(bf16[1536,512]{1,0:T(8,128)(2,1)} %all-gather.4.cloned.1.call-done) | copy-start | bytes 4718596
Sparse Core Ops, SparseCore 0:
  24.5 60.0 all-gather.5
  160.6 38.6 all-gather.3

commit v14 on v10

--- a/solution.py
+++ b/solution.py
@@ -39,9 +39,10 @@
     summed = jnp.sum(received.astype(jnp.float32), axis=1)
     hidden = residual.astype(jnp.float32) + summed
     squares = jnp.sum(hidden * hidden, axis=1)
-    for axis, mask in (("xhi", 1), ("zlo", 1), ("zhi", 1), ("zhi", 2)):
+    for axis in (("zlo", "xhi"), "zhi"):
         size = lax.axis_size(axis)
-        squares = squares + lax.ppermute(squares, axis, [(i, i ^ mask) for i in range(size)])
+        others = [lax.ppermute(squares, axis, [(i, i ^ m) for i in range(size)]) for m in range(1, size)]
+        squares = squares + sum(others)
     normed = (hidden * lax.rsqrt(squares[:, None] / D + 1e-05) * gain[None, :]).astype(jnp.bfloat16)
     member = jnp.arange(R_DEV, dtype=jnp.int32)[:, None] == token_tr[0][None, :]
     counts = jnp.sum(member.astype(jnp.float32), axis=1, keepdims=True)

time: 211 us -> 209 us (level)
  waiting for transfers between devices: 94.6 us -> 90 us
  starting transfers between devices: 17.7 us -> 20.7 us
    ppermute x4 -> x6, starting transfers between devices: 7.15 us -> 10.1 us  [on_device(): lax.ppermute(squares, axis, [(i, i ^ m) for i in range(size)])]
    ppermute x4 -> x6, waiting for transfers between devices: 9.14 us -> 6.21 us  [on_device(): lax.ppermute(squares, axis, [(i, i ^ m) for i in range(size)])]
  transfers between devices with their start and end apart: 8 -> 10, of which waited for: 8 -> 7; matrix products, arithmetic and copies ran while one was open for 1% -> 1% of each run, Pallas kernels for 0% -> 0%
where the time goes in v14:
time: 209 us
  waiting for transfers between devices  90 us (43%)
  blocking collectives  57.2 us (27%)
  starting transfers between devices  20.7 us (10%)
  between operations  18.7 us (9%)
  matrix products  15.2 us (7%)
  other arithmetic  3.69 us (2%)
  local copies, waits for them, and re-layouts  3.42 us (2%)
    all_to_all x1, blocking collectives, on_device(): lax.all_to_all(partial.astype(jnp.bfloat16), 'zhi', 1, 1, tiled=True)  44.4 us
    all_gather x1, waiting for transfers between devices, on_device(): story = lax.all_gather(binned, GROUP, axis=0, tiled=True)  31.4 us
    all_gather x1, waiting for transfers between devices, on_device(): lax.all_gather(ring_block(out_weight), GROUP, axis=0)  23.6 us
    ppermute x1, waiting for transfers between devices, on_device(): other = lax.ppermute(pair, 'zlo', [(0, 1), (1, 0)])  17.9 us
    all_gather x1, blocking collectives, on_device(): pair = lax.all_gather(attention, 'xhi', axis=1, tiled=True)  12.8 us
    ppermute x1, waiting for transfers between devices, ring_block(): return lax.ppermute(block, GROUP + TENSOR, route)  10.8 us
    ppermute x6, starting transfers between devices, on_device(): lax.ppermute(squares, axis, [(i, i ^ m) for i in range(size)])  10.1 us
    dot_general x4, matrix products, on_device(): lax.dot_general(lagged, responses, contract, preferred_element_type=jnp.f...  7.41 us
  transfers between devices with their start and end apart: 10, of which 7 were waited for; matrix products, arithmetic and copies ran while one was open for 1% of the time, Pallas kernels for 0%

profile of v14, /device:TPU:1, one launch (start us, length us, event | category | flops | bytes accessed | tf_op | source)
XLA Modules:
  0.0 208.9 jit_solution(11410746061269497016)
XLA Ops:
  6.5 6.1 %collective-permute-start.1 = (bf16[512,512]{1,0:T(8,128)(2,1)}, bf16[512,512]{1,0:T(8,128)(2,1)S(1)}, u32[]{:S(2)}, u32[]{:S(2)}) collective-permute-start(bf16[512,512]{1,0:T(8,128)(2,1)} %param.8), channel_id=1, source_target_pairs={{0,0},{16,1},{32,2},{48,3},{4,4},{20,5},{36,6},{52,7},{8,8},{24,9}... | collective-permute-start | bytes 1572872 | tf_op jit(solution)/shard_map/ppermute | solution.py:23
  12.7 10.8 %collective-permute-done.1 = bf16[512,512]{1,0:T(8,128)(2,1)S(1)} collective-permute-done((bf16[512,512]{1,0:T(8,128)(2,1)}, bf16[512,512]{1,0:T(8,128)(2,1)S(1)}, u32[]{:S(2)}, u32[]{:S(2)}) %collective-permute-start.1) | collective-permute-done | bytes 524320 | tf_op jit(solution)/shard_map/ppermute | solution.py:23
  24.4 1.2 copy.10
  25.6 12.8 %all_gather.12 = bf16[384,1024]{0,1:T(8,128)(2,1)S(1)} all-gather(bf16[384,512]{0,1:T(8,128)(2,1)S(1)} %copy.10), channel_id=1, replica_groups=mesh['xlo'=2,'y'=4,'core'=2,'zhi'=4,'zlo'=2,'xhi'=2] {'xhi'}, dimensions={1}, use_global_device_ids=true | all-gather | bytes 1179648 | tf_op jit(solution)/shard_map/all_gather | solution.py:30
  38.4 4.4 %collective-permute-start = (bf16[384,1024]{0,1:T(8,128)(2,1)S(1)}, bf16[384,1024]{0,1:T(8,128)(2,1)S(1)}, u32[]{:S(2)}, u32[]{:S(2)}) collective-permute-start(bf16[384,1024]{0,1:T(8,128)(2,1)S(1)} %all_gather.12), channel_id=1, source_target_pairs={{0,2},{2,0},{1,3},{3,1},{4,6},{6,4},{5,7},{7,5},{8,10},{10,8},{9,1... | collective-permute-start | bytes 2359304 | tf_op jit(solution)/shard_map/ppermute | solution.py:31
  42.8 17.9 %collective-permute-done = bf16[384,1024]{0,1:T(8,128)(2,1)S(1)} collective-permute-done((bf16[384,1024]{0,1:T(8,128)(2,1)S(1)}, bf16[384,1024]{0,1:T(8,128)(2,1)S(1)}, u32[]{:S(2)}, u32[]{:S(2)}) %collective-permute-start) | collective-permute-done | bytes 786464 | tf_op jit(solution)/shard_map/ppermute | solution.py:31
  61.0 23.6 %all-gather.6.cloned.1.call-done = bf16[8192,512]{1,0:T(8,128)(2,1)} async-done(((bf16[512,512]{1,0:T(8,128)(2,1)}), bf16[8192,512]{1,0:T(8,128)(2,1)}) %all-gather.6.cloned.1.call-update) | async-done | bytes 8388624 | tf_op jit(solution)/shard_map/all_gather | solution.py:34
  84.6 6.8 %bitcast_convert_fusion = bf16[384,4,512]{2,0,1:T(8,128)(2,1)S(1)} fusion(bf16[384,4,512,1]{0,2,1,3:T(8,128)(2,1)S(1)} %bitcast.29, bf16[4,4,512,512]{3,2,1,0:T(8,128)(2,1)} %bitcast.30), kind=kOutput, calls=%fused_computation.1 | convolution fusion | flops 3222011904 | bytes 11534336 | tf_op jit(solution)/shard_map/iqh,rqhf->irf/dot_general | solution.py:35
  91.4 44.4 %all_to_all.5 = bf16[384,4,512]{2,0,1:T(8,128)(2,1)S(1)} all-to-all(bf16[384,4,512]{2,0,1:T(8,128)(2,1)S(1)} %bitcast_convert_fusion), channel_id=1, replica_groups=mesh['xlo'=2,'y'=4,'core'=2,'zhi'=4,'zlo'=2,'xhi'=2] {'zhi'}, dimensions={1} | all-to-all | bytes 3145728 | tf_op jit(solution)/shard_map/all_to_all | solution.py:38
  137.1 2.8 %collective-permute-start.2 = (f32[384]{0:T(512)S(1)}, f32[384]{0:T(512)S(1)}, u32[]{:S(2)}, u32[]{:S(2)}) collective-permute-start(f32[384]{0:T(512)S(1)} %multiply_reduce_fusion), channel_id=1, source_target_pairs={{0,1},{1,0},{2,3},{3,2},{4,5},{5,4},{6,7},{7,6},{8,9},{9,8},{10,11... | collective-permute-start | bytes 4616 | tf_op jit(solution)/shard_map/ppermute | solution.py:44
  139.9 1.5 collective-permute-start.4
  141.3 1.0 collective-permute-done.3
  142.3 2.4 %collective-permute-done.4 = f32[384]{0:T(512)S(1)} collective-permute-done((f32[384]{0:T(512)S(1)}, f32[384]{0:T(512)S(1)}, u32[]{:S(2)}, u32[]{:S(2)}) %collective-permute-start.4) | collective-permute-done | bytes 1568 | tf_op jit(solution)/shard_map/ppermute | solution.py:44
  144.7 2.5 %collective-permute-start.5 = (f32[384]{0:T(512)S(1)}, f32[384]{0:T(512)S(1)}, u32[]{:S(2)}, u32[]{:S(2)}) collective-permute-start(f32[384]{0:T(512)S(1)} %add_add_fusion), channel_id=1, source_target_pairs={{0,4},{4,0},{8,12},{12,8},{1,5},{5,1},{9,13},{13,9},{2,6},{6,2},{1... | collective-permute-start | bytes 4616 | tf_op jit(solution)/shard_map/ppermute | solution.py:44
  147.2 0.8 collective-permute-start.6
  148.0 2.5 %collective-permute-start.7 = (f32[384]{0:T(512)S(1)}, f32[384]{0:T(512)S(1)}, u32[]{:S(2)}, u32[]{:S(2)}) collective-permute-start(f32[384]{0:T(512)S(1)} %add_add_fusion), channel_id=1, source_target_pairs={{0,12},{4,8},{8,4},{12,0},{1,13},{5,9},{9,5},{13,1},{2,14},{6,10},... | collective-permute-start | bytes 4616 | tf_op jit(solution)/shard_map/ppermute | solution.py:44
  150.7 2.8 %collective-permute-done.6 = f32[384]{0:T(512)S(1)} collective-permute-done((f32[384]{0:T(512)S(1)}, f32[384]{0:T(512)S(1)}, u32[]{:S(2)}, u32[]{:S(2)}) %collective-permute-start.6) | collective-permute-done | bytes 1568 | tf_op jit(solution)/shard_map/ppermute | solution.py:44
  153.5 1.0 fusion.20
  160.4 31.4 %all-gather.4.cloned.1.call-done = bf16[1536,512]{1,0:T(8,128)(2,1)} async-done(((bf16[96,512]{1,0:T(8,128)(2,1)}), bf16[1536,512]{1,0:T(8,128)(2,1)}) %all-gather.4.cloned.1.call-update) | async-done | bytes 1572880 | tf_op jit(solution)/shard_map/all_gather | solution.py:54
  191.8 3.0 %fusion.11 = f32[1,512,640]{2,1,0:T(8,128)S(1)} fusion(bf16[1536,640]{1,0:T(8,128)(2,1)S(1)} %copy-done, s32[]{:T(128)S(6)} %select_n.28, bf16[1536,512]{1,0:T(8,128)(2,1)} %all-gather.4.cloned.1.call-done), kind=kOutput, calls=%fused_computation.13 | convolution fusion | flops 1006632960 | bytes 4849668 | tf_op jit(solution)/shard_map/dot_general | solution.py:61
  194.8 1.5 fusion.14
  196.2 1.5 fusion.8
  197.7 1.5 fusion.17
  199.2 2.8 %maximum_multiply_fusion = f32[4,512,640]{2,1,0:T(8,128)} fusion(f32[1,512,640]{2,1,0:T(8,128)S(1)} %fusion.17, f32[1,512,640]{2,1,0:T(8,128)S(1)} %fusion.14, f32[1,512,640]{2,1,0:T(8,128)S(1)} %fusion.11, f32[1,512,640]{2,1,0:T(8,128)S(1)} %fusion.8), kind=kLoop, calls=%fused_computation | loop fusion | flops 5242880 | bytes 10485760 | tf_op jit(solution)/shard_map/mul | solution.py:62
  (31 shorter events, 3.2 us)
Async XLA Ops:
  6.5 185.2 %copy-start = (bf16[1536,640]{1,0:T(8,128)(2,1)S(1)}, bf16[1536,640]{1,0:T(8,128)(2,1)}, u32[]{:S(2)}) copy-start(bf16[1536,640]{1,0:T(8,128)(2,1)} %param.13) | copy-start | bytes 5898244
  6.5 78.1 %all-gather.6.cloned.1.call-start = ((), (), s32[]{:S(2)}) async-start(), calls=%async_computation.2 | async-start | bytes 8912896 | tf_op jit(solution)/shard_map/all_gather | solution.py:34
  6.5 17.0 %collective-permute-start.1 = (bf16[512,512]{1,0:T(8,128)(2,1)}, bf16[512,512]{1,0:T(8,128)(2,1)S(1)}, u32[]{:S(2)}, u32[]{:S(2)}) collective-permute-start(bf16[512,512]{1,0:T(8,128)(2,1)} %param.8), channel_id=1, source_target_pairs={{0,0},{16,1},{32,2},{48,3},{4,4},{20,5},{36,6},{52,7},{8,8},{24,9}... | collective-permute-start | bytes 1572872 | tf_op jit(solution)/shard_map/ppermute | solution.py:23
  23.5 0.8 copy-start.2
  24.3 167.4 %all-gather.4.cloned.1.call-start = ((), (), s32[]{:S(2)}) async-start(), calls=%async_computation.1 | async-start | bytes 1671168 | tf_op jit(solution)/shard_map/all_gather | solution.py:54
  38.4 22.3 %collective-permute-start = (bf16[384,1024]{0,1:T(8,128)(2,1)S(1)}, bf16[384,1024]{0,1:T(8,128)(2,1)S(1)}, u32[]{:S(2)}, u32[]{:S(2)}) collective-permute-start(bf16[384,1024]{0,1:T(8,128)(2,1)S(1)} %all_gather.12), channel_id=1, source_target_pairs={{0,2},{2,0},{1,3},{3,1},{4,6},{6,4},{5,7},{7,5},{8,10},{10,8},{9,1... | collective-permute-start | bytes 2359304 | tf_op jit(solution)/shard_map/ppermute | solution.py:31
  135.9 1.0 copy-start.3
  135.9 5.4 %copy-start.5 = (s32[1,384]{1,0:T(1,128)S(1)}, s32[1,384]{1,0:T(1,128)}, u32[]{:S(2)}) copy-start(s32[1,384]{1,0:T(1,128)} %param.11) | copy-start | bytes 4612
  135.9 17.6 %copy-start.6 = (f32[512]{0:T(512)S(1)}, f32[512]{0:T(512)}, u32[]{:S(2)}) copy-start(f32[512]{0:T(512)} %param.10) | copy-start | bytes 6148
  136.9 17.6 %copy-start.4 = (s32[4]{0:T(128)S(1)}, s32[4]{0:T(128)}, u32[]{:S(2)}) copy-start(s32[4]{0:T(128)} %param.12) | copy-start | bytes 52
  137.1 4.3 %collective-permute-start.2 = (f32[384]{0:T(512)S(1)}, f32[384]{0:T(512)S(1)}, u32[]{:S(2)}, u32[]{:S(2)}) collective-permute-start(f32[384]{0:T(512)S(1)} %multiply_reduce_fusion), channel_id=1, source_target_pairs={{0,1},{1,0},{2,3},{3,2},{4,5},{5,4},{6,7},{7,6},{8,9},{9,8},{10,11... | collective-permute-start | bytes 4616 | tf_op jit(solution)/shard_map/ppermute | solution.py:44
  139.8 2.4 %collective-permute-start.3 = (f32[384]{0:T(512)S(1)}, f32[384]{0:T(512)S(1)}, u32[]{:S(2)}, u32[]{:S(2)}) collective-permute-start(f32[384]{0:T(512)S(1)} %multiply_reduce_fusion), channel_id=1, source_target_pairs={{0,2},{1,3},{2,0},{3,1},{4,6},{5,7},{6,4},{7,5},{8,10},{9,11},{10,... | collective-permute-start | bytes 4616 | tf_op jit(solution)/shard_map/ppermute | solution.py:44
  139.9 4.8 %collective-permute-start.4 = (f32[384]{0:T(512)S(1)}, f32[384]{0:T(512)S(1)}, u32[]{:S(2)}, u32[]{:S(2)}) collective-permute-start(f32[384]{0:T(512)S(1)} %multiply_reduce_fusion), channel_id=1, source_target_pairs={{0,3},{1,2},{2,1},{3,0},{4,7},{5,6},{6,5},{7,4},{8,11},{9,10},{10,... | collective-permute-start | bytes 4616 | tf_op jit(solution)/shard_map/ppermute | solution.py:44
  144.7 6.0 %collective-permute-start.5 = (f32[384]{0:T(512)S(1)}, f32[384]{0:T(512)S(1)}, u32[]{:S(2)}, u32[]{:S(2)}) collective-permute-start(f32[384]{0:T(512)S(1)} %add_add_fusion), channel_id=1, source_target_pairs={{0,4},{4,0},{8,12},{12,8},{1,5},{5,1},{9,13},{13,9},{2,6},{6,2},{1... | collective-permute-start | bytes 4616 | tf_op jit(solution)/shard_map/ppermute | solution.py:44
  147.2 6.3 %collective-permute-start.6 = (f32[384]{0:T(512)S(1)}, f32[384]{0:T(512)S(1)}, u32[]{:S(2)}, u32[]{:S(2)}) collective-permute-start(f32[384]{0:T(512)S(1)} %add_add_fusion), channel_id=1, source_target_pairs={{0,8},{4,12},{8,0},{12,4},{1,9},{5,13},{9,1},{13,5},{2,10},{6,14},... | collective-permute-start | bytes 4616 | tf_op jit(solution)/shard_map/ppermute | solution.py:44
  148.0 5.5 %collective-permute-start.7 = (f32[384]{0:T(512)S(1)}, f32[384]{0:T(512)S(1)}, u32[]{:S(2)}, u32[]{:S(2)}) collective-permute-start(f32[384]{0:T(512)S(1)} %add_add_fusion), channel_id=1, source_target_pairs={{0,12},{4,8},{8,4},{12,0},{1,13},{5,9},{9,5},{13,1},{2,14},{6,10},... | collective-permute-start | bytes 4616 | tf_op jit(solution)/shard_map/ppermute | solution.py:44
  191.8 3.0 %copy-start.1 = (bf16[1536,512]{1,0:T(8,128)(2,1)S(1)}, bf16[1536,512]{1,0:T(8,128)(2,1)}, u32[]{:S(2)}) copy-start(bf16[1536,512]{1,0:T(8,128)(2,1)} %all-gather.4.cloned.1.call-done) | copy-start | bytes 4718596
Sparse Core Ops, SparseCore 0:
  24.5 60.0 all-gather.5
  154.6 37.0 all-gather.3

commit v15 on v14

--- a/solution.py
+++ b/solution.py
@@ -31,12 +31,16 @@
     other = lax.ppermute(pair, "zlo", [(0, 1), (1, 0)])
     low = lax.axis_index("zlo") == 0
     slab = jnp.concatenate([jnp.where(low, pair, other), jnp.where(low, other, pair)], axis=1)
-    blocks = lax.all_gather(ring_block(out_weight), GROUP, axis=0).reshape(ring, quad, heads, -1)
-    partial = jnp.einsum(
-        "iqh,rqhf->irf", slab.reshape(-1, quad, heads), blocks, preferred_element_type=jnp.float32
-    )
-    received = lax.all_to_all(partial.astype(jnp.bfloat16), "zhi", 1, 1, tiled=True)
-    summed = jnp.sum(received.astype(jnp.float32), axis=1)
+    fetched = ring_block(out_weight)
+    lhs = slab.reshape(-1, quad, heads)
+    cut = fetched.shape[1] // 2
+    sums = []
+    for cols in (slice(0, cut), slice(cut, None)):
+        blocks = lax.all_gather(fetched[:, cols], GROUP, axis=0).reshape(ring, quad, heads, -1)
+        partial = jnp.einsum("iqh,rqhf->irf", lhs, blocks, preferred_element_type=jnp.float32)
+        received = lax.all_to_all(partial.astype(jnp.bfloat16), "zhi", 1, 1, tiled=True)
+        sums.append(jnp.sum(received.astype(jnp.float32), axis=1))
+    summed = jnp.concatenate(sums, axis=1)
     hidden = residual.astype(jnp.float32) + summed
     squares = jnp.sum(hidden * hidden, axis=1)
     for axis in (("zlo", "xhi"), "zhi"):

time: 209 us -> 218 us (1.043)
  blocking collectives: 57.2 us -> 12.8 us
  waiting for transfers between devices: 90 us -> 125 us
  starting transfers between devices: 20.7 us -> 35 us
  matrix products: 15.2 us -> 19.7 us
    all_to_all x1 -> x0, blocking collectives: 44.4 us -> none  [on_device(): lax.all_to_all(partial.astype(jnp.bfloat16), 'zhi', 1, 1, tiled=True)]
    all_to_all x0 -> x2, waiting for transfers between devices: none -> 19.3 us  [on_device(): lax.all_to_all(partial.astype(jnp.bfloat16), 'zhi', 1, 1, tiled=True)]
    all_gather x1 -> x2, waiting for transfers between devices: 23.6 us -> 39.2 us  [on_device(): lax.all_gather(fetched[:, cols], GROUP, axis=0)]
    all_to_all x0 -> x2, starting transfers between devices: none -> 13.5 us  [on_device(): lax.all_to_all(partial.astype(jnp.bfloat16), 'zhi', 1, 1, tiled=True)]
    dot_general x1 -> x2, matrix products: 6.83 us -> 10.3 us  [on_device(): jnp.einsum('iqh,rqhf->irf', lhs, blocks, preferred_element_type=jnp.float32)]
    unnamed x15 -> x17, local copies, waits for them, and re-layouts: 2.75 us -> 0.25 us
  transfers between devices with their start and end apart: 10 -> 13, of which waited for: 7 -> 9; matrix products, arithmetic and copies ran while one was open for 1% -> 6% of each run, Pallas kernels for 0% -> 0%
where the time goes in v15:
time: 218 us
  waiting for transfers between devices  125 us (57%)
  starting transfers between devices  35 us (16%)
  matrix products  19.7 us (9%)
  between operations  18.3 us (8%)
  blocking collectives  12.8 us (6%)
  other arithmetic  5.51 us (3%)
    all_gather x2, waiting for transfers between devices, on_device(): lax.all_gather(fetched[:, cols], GROUP, axis=0)  39.2 us
    all_gather x1, waiting for transfers between devices, on_device(): story = lax.all_gather(binned, GROUP, axis=0, tiled=True)  30.9 us
    all_to_all x2, waiting for transfers between devices, on_device(): lax.all_to_all(partial.astype(jnp.bfloat16), 'zhi', 1, 1, tiled=True)  19.3 us
    ppermute x1, waiting for transfers between devices, on_device(): other = lax.ppermute(pair, 'zlo', [(0, 1), (1, 0)])  17.8 us
    all_to_all x2, starting transfers between devices, on_device(): lax.all_to_all(partial.astype(jnp.bfloat16), 'zhi', 1, 1, tiled=True)  13.5 us
    all_gather x1, blocking collectives, on_device(): pair = lax.all_gather(attention, 'xhi', axis=1, tiled=True)  12.8 us
    ppermute x6, starting transfers between devices, on_device(): lax.ppermute(squares, axis, [(i, i ^ m) for i in range(size)])  11 us
    ppermute x1, waiting for transfers between devices, ring_block(): return lax.ppermute(block, GROUP + TENSOR, route)  10.8 us
  transfers between devices with their start and end apart: 13, of which 9 were waited for; matrix products, arithmetic and copies ran while one was open for 6% of the time, Pallas kernels for 0%

profile of v15, /device:TPU:1, one launch (start us, length us, event | category | flops | bytes accessed | tf_op | source)
XLA Modules:
  0.0 217.8 jit_solution(15560599421532324912)
XLA Ops:
  6.5 6.1 %collective-permute-start.1 = (bf16[512,512]{1,0:T(8,128)(2,1)}, bf16[512,512]{1,0:T(8,128)(2,1)S(1)}, u32[]{:S(2)}, u32[]{:S(2)}) collective-permute-start(bf16[512,512]{1,0:T(8,128)(2,1)} %param.8), channel_id=1, source_target_pairs={{0,0},{16,1},{32,2},{48,3},{4,4},{20,5},{36,6},{52,7},{8,8},{24,9}... | collective-permute-start | bytes 1572872 | tf_op jit(solution)/shard_map/ppermute | solution.py:23
  12.7 10.8 %collective-permute-done.1 = bf16[512,512]{1,0:T(8,128)(2,1)S(1)} collective-permute-done((bf16[512,512]{1,0:T(8,128)(2,1)}, bf16[512,512]{1,0:T(8,128)(2,1)S(1)}, u32[]{:S(2)}, u32[]{:S(2)}) %collective-permute-start.1) | collective-permute-done | bytes 524320 | tf_op jit(solution)/shard_map/ppermute | solution.py:23
  25.4 12.8 %all_gather.18 = bf16[384,1024]{0,1:T(8,128)(2,1)S(1)} all-gather(bf16[384,512]{0,1:T(8,128)(2,1)S(1)} %copy.11), channel_id=1, replica_groups=mesh['xlo'=2,'y'=4,'core'=2,'zhi'=4,'zlo'=2,'xhi'=2] {'xhi'}, dimensions={1}, use_global_device_ids=true | all-gather | bytes 1179648 | tf_op jit(solution)/shard_map/all_gather | solution.py:30
  38.2 4.4 %collective-permute-start = (bf16[384,1024]{0,1:T(8,128)(2,1)S(1)}, bf16[384,1024]{0,1:T(8,128)(2,1)S(1)}, u32[]{:S(2)}, u32[]{:S(2)}) collective-permute-start(bf16[384,1024]{0,1:T(8,128)(2,1)S(1)} %all_gather.18), channel_id=1, source_target_pairs={{0,2},{2,0},{1,3},{3,1},{4,6},{6,4},{5,7},{7,5},{8,10},{10,8},{9,1... | collective-permute-start | bytes 2359304 | tf_op jit(solution)/shard_map/ppermute | solution.py:31
  42.6 17.8 %collective-permute-done = bf16[384,1024]{0,1:T(8,128)(2,1)S(1)} collective-permute-done((bf16[384,1024]{0,1:T(8,128)(2,1)S(1)}, bf16[384,1024]{0,1:T(8,128)(2,1)S(1)}, u32[]{:S(2)}, u32[]{:S(2)}) %collective-permute-start) | collective-permute-done | bytes 786464 | tf_op jit(solution)/shard_map/ppermute | solution.py:31
  60.7 9.1 %all-gather.10.cloned.1.call-done = bf16[8192,256]{1,0:T(8,128)(2,1)} async-done(((bf16[512,256]{1,0:T(8,128)(2,1)}), bf16[8192,256]{1,0:T(8,128)(2,1)}) %all-gather.10.cloned.1.call-update) | async-done | bytes 4194320 | tf_op jit(solution)/shard_map/all_gather | solution.py:39
  69.8 5.0 %bitcast_convert_fusion = bf16[384,4,256]{2,0,1:T(8,128)(2,1)} fusion(bf16[384,4,512,1]{0,2,1,3:T(8,128)(2,1)S(1)} %bitcast.36, bf16[4,4,512,256]{3,2,1,0:T(8,128)(2,1)} %bitcast.38), kind=kOutput, calls=%fused_computation.2 | convolution fusion | flops 1611005952 | bytes 6553600 | tf_op jit(solution)/shard_map/iqh,rqhf->irf/dot_general | solution.py:40
  74.8 6.7 %all-to-all-start.1 = ((bf16[384,4,256]{2,0,1:T(8,128)(2,1)}), bf16[384,4,256]{2,0,1:T(8,128)(2,1)S(1)}, u32[]{:S(2)}, u32[]{:S(2)}) async-start(bf16[384,4,256]{2,0,1:T(8,128)(2,1)} %bitcast_convert_fusion), calls=%async_computation.1 | async-start | bytes 1572864 | tf_op jit(solution)/shard_map/all_to_all | solution.py:41
  81.5 30.1 %all-gather.8.cloned.1.call-done = bf16[8192,256]{1,0:T(8,128)(2,1)} async-done(((bf16[512,256]{1,0:T(8,128)(2,1)}), bf16[8192,256]{1,0:T(8,128)(2,1)}) %all-gather.8.cloned.1.call-update) | async-done | bytes 4194320 | tf_op jit(solution)/shard_map/all_gather | solution.py:39
  111.6 5.4 %bitcast_convert_fusion.1 = bf16[384,4,256]{2,0,1:T(8,128)(2,1)} fusion(bf16[384,4,512,1]{0,2,1,3:T(8,128)(2,1)} %bitcast.37, bf16[4,4,512,256]{3,2,1,0:T(8,128)(2,1)} %bitcast.39), kind=kOutput, calls=%fused_computation.3 | convolution fusion | flops 1611005952 | bytes 6553600 | tf_op jit(solution)/shard_map/iqh,rqhf->irf/dot_general | solution.py:40
  117.0 6.7 %all-to-all-start = ((bf16[384,4,256]{2,0,1:T(8,128)(2,1)}), bf16[384,4,256]{2,0,1:T(8,128)(2,1)S(1)}, u32[]{:S(2)}, u32[]{:S(2)}) async-start(bf16[384,4,256]{2,0,1:T(8,128)(2,1)} %bitcast_convert_fusion.1), calls=%async_computation | async-start | bytes 1572864 | tf_op jit(solution)/shard_map/all_to_all | solution.py:41
  124.6 19.3 %all-to-all-done = bf16[384,4,256]{2,0,1:T(8,128)(2,1)S(1)} async-done(((bf16[384,4,256]{2,0,1:T(8,128)(2,1)}), bf16[384,4,256]{2,0,1:T(8,128)(2,1)S(1)}, u32[]{:S(2)}, u32[]{:S(2)}) %all-to-all-start) | async-done | bytes 786464 | tf_op jit(solution)/shard_map/all_to_all | solution.py:41
  145.3 2.5 %collective-permute-start.2 = (f32[384]{0:T(512)S(1)}, f32[384]{0:T(512)S(1)}, u32[]{:S(2)}, u32[]{:S(2)}) collective-permute-start(f32[384]{0:T(512)S(1)} %multiply_reduce_fusion), channel_id=1, source_target_pairs={{0,1},{1,0},{2,3},{3,2},{4,5},{5,4},{6,7},{7,6},{8,9},{9,8},{10,11... | collective-permute-start | bytes 4616 | tf_op jit(solution)/shard_map/ppermute | solution.py:48
  147.8 1.7 collective-permute-start.4
  150.6 2.1 collective-permute-done.4
  152.7 3.3 %collective-permute-start.5 = (f32[384]{0:T(512)S(1)}, f32[384]{0:T(512)S(1)}, u32[]{:S(2)}, u32[]{:S(2)}) collective-permute-start(f32[384]{0:T(512)S(1)} %add_add_fusion), channel_id=1, source_target_pairs={{0,4},{4,0},{8,12},{12,8},{1,5},{5,1},{9,13},{13,9},{2,6},{6,2},{1... | collective-permute-start | bytes 4616 | tf_op jit(solution)/shard_map/ppermute | solution.py:48
  156.7 2.7 %collective-permute-start.7 = (f32[384]{0:T(512)S(1)}, f32[384]{0:T(512)S(1)}, u32[]{:S(2)}, u32[]{:S(2)}) collective-permute-start(f32[384]{0:T(512)S(1)} %add_add_fusion), channel_id=1, source_target_pairs={{0,12},{4,8},{8,4},{12,0},{1,13},{5,9},{9,5},{13,1},{2,14},{6,10},... | collective-permute-start | bytes 4616 | tf_op jit(solution)/shard_map/ppermute | solution.py:48
  159.5 2.8 %collective-permute-done.6 = f32[384]{0:T(512)S(1)} collective-permute-done((f32[384]{0:T(512)S(1)}, f32[384]{0:T(512)S(1)}, u32[]{:S(2)}, u32[]{:S(2)}) %collective-permute-start.6) | collective-permute-done | bytes 1568 | tf_op jit(solution)/shard_map/ppermute | solution.py:48
  162.4 1.9 fusion.20
  170.1 30.9 %all-gather.6.cloned.1.call-done = bf16[1536,512]{1,0:T(8,128)(2,1)} async-done(((bf16[96,512]{1,0:T(8,128)(2,1)}), bf16[1536,512]{1,0:T(8,128)(2,1)}) %all-gather.6.cloned.1.call-update) | async-done | bytes 1572880 | tf_op jit(solution)/shard_map/all_gather | solution.py:58
  201.0 3.0 %fusion.11 = f32[1,512,640]{2,1,0:T(8,128)S(1)} fusion(bf16[1536,640]{1,0:T(8,128)(2,1)S(1)} %copy-done, s32[]{:T(128)S(6)} %select_n.28, bf16[1536,512]{1,0:T(8,128)(2,1)} %all-gather.6.cloned.1.call-done), kind=kOutput, calls=%fused_computation.15 | convolution fusion | flops 1006632960 | bytes 4849668 | tf_op jit(solution)/shard_map/dot_general | solution.py:65
  205.5 1.5 fusion.8
  207.0 1.5 fusion.17
  208.5 2.8 %maximum_multiply_fusion = f32[4,512,640]{2,1,0:T(8,128)} fusion(f32[1,512,640]{2,1,0:T(8,128)S(1)} %fusion.17, f32[1,512,640]{2,1,0:T(8,128)S(1)} %fusion.14, f32[1,512,640]{2,1,0:T(8,128)S(1)} %fusion.11, f32[1,512,640]{2,1,0:T(8,128)S(1)} %fusion.8), kind=kLoop, calls=%fused_computation | loop fusion | flops 5242880 | bytes 10485760 | tf_op jit(solution)/shard_map/mul | solution.py:66
  (42 shorter events, 8.4 us)
Async XLA Ops:
  6.5 194.5 %copy-start = (bf16[1536,640]{1,0:T(8,128)(2,1)S(1)}, bf16[1536,640]{1,0:T(8,128)(2,1)}, u32[]{:S(2)}) copy-start(bf16[1536,640]{1,0:T(8,128)(2,1)} %param.13) | copy-start | bytes 5898244
  6.5 18.6 %copy-start.4 = (bf16[384,512]{1,0:T(8,128)(2,1)S(1)}, bf16[384,512]{1,0:T(8,128)(2,1)}, u32[]{:S(2)}) copy-start(bf16[384,512]{1,0:T(8,128)(2,1)} %param.7) | copy-start | bytes 1179652
  6.5 63.3 %all-gather.10.cloned.1.call-start = ((), (), s32[]{:S(2)}) async-start(), calls=%async_computation.4 | async-start | bytes 4456448 | tf_op jit(solution)/shard_map/all_gather | solution.py:39
  6.5 17.0 %collective-permute-start.1 = (bf16[512,512]{1,0:T(8,128)(2,1)}, bf16[512,512]{1,0:T(8,128)(2,1)S(1)}, u32[]{:S(2)}, u32[]{:S(2)}) collective-permute-start(bf16[512,512]{1,0:T(8,128)(2,1)} %param.8), channel_id=1, source_target_pairs={{0,0},{16,1},{32,2},{48,3},{4,4},{20,5},{36,6},{52,7},{8,8},{24,9}... | collective-permute-start | bytes 1572872 | tf_op jit(solution)/shard_map/ppermute | solution.py:23
  24.4 87.2 %all-gather.8.cloned.1.call-start = ((), (), s32[]{:S(2)}) async-start(), calls=%async_computation.3 | async-start | bytes 4456448 | tf_op jit(solution)/shard_map/all_gather | solution.py:39
  38.2 22.2 %collective-permute-start = (bf16[384,1024]{0,1:T(8,128)(2,1)S(1)}, bf16[384,1024]{0,1:T(8,128)(2,1)S(1)}, u32[]{:S(2)}, u32[]{:S(2)}) collective-permute-start(bf16[384,1024]{0,1:T(8,128)(2,1)S(1)} %all_gather.18), channel_id=1, source_target_pairs={{0,2},{2,0},{1,3},{3,1},{4,6},{6,4},{5,7},{7,5},{8,10},{10,8},{9,1... | collective-permute-start | bytes 2359304 | tf_op jit(solution)/shard_map/ppermute | solution.py:31
  60.7 14.1 %copy-start.2 = (bf16[384,2048]{0,1:T(8,128)(2,1)}, bf16[384,2048]{0,1:T(8,128)(2,1)S(1)}, u32[]{:S(2)}) copy-start(bf16[384,2048]{0,1:T(8,128)(2,1)S(1)} %pad_maximum_fusion) | copy-start | bytes 4718596
  74.8 42.2 %all-to-all-start.1 = ((bf16[384,4,256]{2,0,1:T(8,128)(2,1)}), bf16[384,4,256]{2,0,1:T(8,128)(2,1)S(1)}, u32[]{:S(2)}, u32[]{:S(2)}) async-start(bf16[384,4,256]{2,0,1:T(8,128)(2,1)} %bitcast_convert_fusion), calls=%async_computation.1 | async-start | bytes 1572864 | tf_op jit(solution)/shard_map/all_to_all | solution.py:41
  117.0 26.9 %all-to-all-start = ((bf16[384,4,256]{2,0,1:T(8,128)(2,1)}), bf16[384,4,256]{2,0,1:T(8,128)(2,1)S(1)}, u32[]{:S(2)}, u32[]{:S(2)}) async-start(bf16[384,4,256]{2,0,1:T(8,128)(2,1)} %bitcast_convert_fusion.1), calls=%async_computation | async-start | bytes 1572864 | tf_op jit(solution)/shard_map/all_to_all | solution.py:41
  123.7 25.9 %copy-start.6 = (s32[1,384]{1,0:T(1,128)S(1)}, s32[1,384]{1,0:T(1,128)}, u32[]{:S(2)}) copy-start(s32[1,384]{1,0:T(1,128)} %param.11) | copy-start | bytes 4612
  123.7 38.7 %copy-start.7 = (f32[512]{0:T(512)S(1)}, f32[512]{0:T(512)}, u32[]{:S(2)}) copy-start(f32[512]{0:T(512)} %param.10) | copy-start | bytes 6148
  123.7 77.3 %all-gather.6.cloned.1.call-start = ((), (), s32[]{:S(2)}) async-start(), calls=%async_computation.2 | async-start | bytes 1671168 | tf_op jit(solution)/shard_map/all_gather | solution.py:58
  124.6 37.8 %copy-start.3 = (f32[384,256]{1,0:T(8,128)S(1)}, f32[384,256]{1,0:T(8,128)}, u32[]{:S(2)}) copy-start(f32[384,256]{1,0:T(8,128)} %convert_reduce_fusion) | copy-start | bytes 1179652
  144.0 20.4 %copy-start.5 = (s32[4]{0:T(128)S(1)}, s32[4]{0:T(128)}, u32[]{:S(2)}) copy-start(s32[4]{0:T(128)} %param.12) | copy-start | bytes 52
  145.3 4.3 %collective-permute-start.2 = (f32[384]{0:T(512)S(1)}, f32[384]{0:T(512)S(1)}, u32[]{:S(2)}, u32[]{:S(2)}) collective-permute-start(f32[384]{0:T(512)S(1)} %multiply_reduce_fusion), channel_id=1, source_target_pairs={{0,1},{1,0},{2,3},{3,2},{4,5},{5,4},{6,7},{7,6},{8,9},{9,8},{10,11... | collective-permute-start | bytes 4616 | tf_op jit(solution)/shard_map/ppermute | solution.py:48
  147.8 2.7 %collective-permute-start.3 = (f32[384]{0:T(512)S(1)}, f32[384]{0:T(512)S(1)}, u32[]{:S(2)}, u32[]{:S(2)}) collective-permute-start(f32[384]{0:T(512)S(1)} %multiply_reduce_fusion), channel_id=1, source_target_pairs={{0,2},{1,3},{2,0},{3,1},{4,6},{5,7},{6,4},{7,5},{8,10},{9,11},{10,... | collective-permute-start | bytes 4616 | tf_op jit(solution)/shard_map/ppermute | solution.py:48
  147.8 4.8 %collective-permute-start.4 = (f32[384]{0:T(512)S(1)}, f32[384]{0:T(512)S(1)}, u32[]{:S(2)}, u32[]{:S(2)}) collective-permute-start(f32[384]{0:T(512)S(1)} %multiply_reduce_fusion), channel_id=1, source_target_pairs={{0,3},{1,2},{2,1},{3,0},{4,7},{5,6},{6,5},{7,4},{8,11},{9,10},{10,... | collective-permute-start | bytes 4616 | tf_op jit(solution)/shard_map/ppermute | solution.py:48
  152.7 6.8 %collective-permute-start.5 = (f32[384]{0:T(512)S(1)}, f32[384]{0:T(512)S(1)}, u32[]{:S(2)}, u32[]{:S(2)}) collective-permute-start(f32[384]{0:T(512)S(1)} %add_add_fusion), channel_id=1, source_target_pairs={{0,4},{4,0},{8,12},{12,8},{1,5},{5,1},{9,13},{13,9},{2,6},{6,2},{1... | collective-permute-start | bytes 4616 | tf_op jit(solution)/shard_map/ppermute | solution.py:48
  156.0 6.3 %collective-permute-start.6 = (f32[384]{0:T(512)S(1)}, f32[384]{0:T(512)S(1)}, u32[]{:S(2)}, u32[]{:S(2)}) collective-permute-start(f32[384]{0:T(512)S(1)} %add_add_fusion), channel_id=1, source_target_pairs={{0,8},{4,12},{8,0},{12,4},{1,9},{5,13},{9,1},{13,5},{2,10},{6,14},... | collective-permute-start | bytes 4616 | tf_op jit(solution)/shard_map/ppermute | solution.py:48
  156.7 5.7 %collective-permute-start.7 = (f32[384]{0:T(512)S(1)}, f32[384]{0:T(512)S(1)}, u32[]{:S(2)}, u32[]{:S(2)}) collective-permute-start(f32[384]{0:T(512)S(1)} %add_add_fusion), channel_id=1, source_target_pairs={{0,12},{4,8},{8,4},{12,0},{1,13},{5,9},{9,5},{13,1},{2,14},{6,10},... | collective-permute-start | bytes 4616 | tf_op jit(solution)/shard_map/ppermute | solution.py:48
  201.0 3.0 %copy-start.1 = (bf16[1536,512]{1,0:T(8,128)(2,1)S(1)}, bf16[1536,512]{1,0:T(8,128)(2,1)}, u32[]{:S(2)}) copy-start(bf16[1536,512]{1,0:T(8,128)(2,1)} %all-gather.6.cloned.1.call-done) | copy-start | bytes 4718596
Sparse Core Ops, SparseCore 0:
  24.5 45.2 all-gather.9
  71.7 39.8 all-gather.7
  164.5 36.4 all-gather.5

commit v16 on v14

--- a/solution.py
+++ b/solution.py
@@ -13,33 +13,35 @@
 def ring_block(block):
     groups = lax.axis_size(GROUP)
     tensors = lax.axis_size(TENSOR)
-    quad = lax.axis_size(("zlo", "xhi"))
+    zlos, xs = lax.axis_size("zlo"), lax.axis_size("xhi")
     route = []
     for g in range(groups):
         for t in range(tensors):
-            ring, q = t // quad, t % quad
-            source = (quad * (g // quad) + q) * tensors + quad * ring + g % quad
-            route.append((source, g * tensors + t))
+            zhi, zlo, x = t // (zlos * xs), (t // xs) % zlos, t % xs
+            r, q = g // (2 * xs), g % (2 * xs)
+            feats = zhi * zlos * xs + r * xs + x
+            heads = (q // xs) * zlos * xs + zlo * xs + q % xs
+            route.append((feats * tensors + heads, g * tensors + t))
     return lax.ppermute(block, GROUP + TENSOR, route)
 
 
 def on_device(attention, out_weight, residual, gain, token_tr, lag_offsets, responses):
-    quad = lax.axis_size(("zlo", "xhi"))
-    ring = lax.axis_size("zhi")
+    quad = lax.axis_size(("zhi", "xhi"))
+    ring = lax.axis_size("zlo")
     heads = attention.shape[1]
     pair = lax.all_gather(attention, "xhi", axis=1, tiled=True)
-    other = lax.ppermute(pair, "zlo", [(0, 1), (1, 0)])
-    low = lax.axis_index("zlo") == 0
+    other = lax.ppermute(pair, "zhi", [(0, 1), (1, 0)])
+    low = lax.axis_index("zhi") == 0
     slab = jnp.concatenate([jnp.where(low, pair, other), jnp.where(low, other, pair)], axis=1)
     blocks = lax.all_gather(ring_block(out_weight), GROUP, axis=0).reshape(ring, quad, heads, -1)
     partial = jnp.einsum(
         "iqh,rqhf->irf", slab.reshape(-1, quad, heads), blocks, preferred_element_type=jnp.float32
     )
-    received = lax.all_to_all(partial.astype(jnp.bfloat16), "zhi", 1, 1, tiled=True)
+    received = lax.all_to_all(partial.astype(jnp.bfloat16), "zlo", 1, 1, tiled=True)
     summed = jnp.sum(received.astype(jnp.float32), axis=1)
     hidden = residual.astype(jnp.float32) + summed
     squares = jnp.sum(hidden * hidden, axis=1)
-    for axis in (("zlo", "xhi"), "zhi"):
+    for axis in (("zhi", "xhi"), "zlo"):
         size = lax.axis_size(axis)
         others = [lax.ppermute(squares, axis, [(i, i ^ m) for i in range(size)]) for m in range(1, size)]
         squares = squares + sum(others)
@@ -64,7 +66,7 @@
 
 
 def solution(mesh):
-    parts = Mesh(mesh.devices.reshape(2, 4, 2, 4, 2, 2), GROUP + TENSOR)
+    parts = Mesh(mesh.devices.reshape(2, 4, 2, 2, 4, 2), GROUP + TENSOR)
     return jax.shard_map(
         on_device,
         mesh=parts,

time: 209 us -> 224 us (1.072)
  starting transfers between devices: 20.7 us -> 31.8 us
  waiting for transfers between devices: 90 us -> 93.8 us
    ppermute x1, starting transfers between devices: 4.39 us -> 14 us  [on_device(): other = lax.ppermute(pair, 'zhi', [(0, 1), (1, 0)])]
    all_gather x1, waiting for transfers between devices: 23.6 us -> 30.2 us  [on_device(): lax.all_gather(ring_block(out_weight), GROUP, axis=0)]
    ppermute x1, waiting for transfers between devices: 10.8 us -> 7.06 us  [ring_block(): return lax.ppermute(block, GROUP + TENSOR, route)]
    all_to_all x1, blocking collectives: 44.4 us -> 40.8 us  [on_device(): lax.all_to_all(partial.astype(jnp.bfloat16), 'zlo', 1, 1, tiled=True)]
    ppermute x6, waiting for transfers between devices: 6.21 us -> 9.3 us  [on_device(): lax.ppermute(squares, axis, [(i, i ^ m) for i in range(size)])]
    all_gather x1, blocking collectives: 12.8 us -> 15.9 us  [on_device(): pair = lax.all_gather(attention, 'xhi', axis=1, tiled=True)]
where the time goes in v16:
time: 224 us; the launch traced here: 223 us
  waiting for transfers between devices  93.8 us (42%)
  blocking collectives  56.7 us (25%)
  starting transfers between devices  31.8 us (14%)
  between operations  18.7 us (8%)
  matrix products  15.2 us (7%)
  other arithmetic  3.69 us (2%)
  local copies, waits for them, and re-layouts  3.42 us (2%)
    all_to_all x1, blocking collectives, on_device(): lax.all_to_all(partial.astype(jnp.bfloat16), 'zlo', 1, 1, tiled=True)  40.8 us
    all_gather x1, waiting for transfers between devices, on_device(): lax.all_gather(ring_block(out_weight), GROUP, axis=0)  30.2 us
    all_gather x1, waiting for transfers between devices, on_device(): story = lax.all_gather(binned, GROUP, axis=0, tiled=True)  29.9 us
    ppermute x1, waiting for transfers between devices, on_device(): other = lax.ppermute(pair, 'zhi', [(0, 1), (1, 0)])  17.3 us
    all_gather x1, blocking collectives, on_device(): pair = lax.all_gather(attention, 'xhi', axis=1, tiled=True)  15.9 us
    ppermute x1, starting transfers between devices, on_device(): other = lax.ppermute(pair, 'zhi', [(0, 1), (1, 0)])  14 us
    ppermute x6, starting transfers between devices, on_device(): lax.ppermute(squares, axis, [(i, i ^ m) for i in range(size)])  11.7 us
    ppermute x6, waiting for transfers between devices, on_device(): lax.ppermute(squares, axis, [(i, i ^ m) for i in range(size)])  9.3 us
  transfers between devices with their start and end apart: 10, of which 7 were waited for; matrix products, arithmetic and copies ran while one was open for 1% of the time, Pallas kernels for 0%

profile of v16, /device:TPU:1, one launch (start us, length us, event | category | flops | bytes accessed | tf_op | source)
XLA Modules:
  0.0 223.3 jit_solution(10234745733768675326)
XLA Ops:
  6.5 6.1 %collective-permute-start.1 = (bf16[512,512]{1,0:T(8,128)(2,1)}, bf16[512,512]{1,0:T(8,128)(2,1)S(1)}, u32[]{:S(2)}, u32[]{:S(2)}) collective-permute-start(bf16[512,512]{1,0:T(8,128)(2,1)} %param.8), channel_id=1, source_target_pairs={{0,0},{16,1},{2,2},{18,3},{4,4},{20,5},{6,6},{22,7},{128,8},{144,9... | collective-permute-start | bytes 1572872 | tf_op jit(solution)/shard_map/ppermute | solution.py:25
  12.7 7.1 %collective-permute-done.1 = bf16[512,512]{1,0:T(8,128)(2,1)S(1)} collective-permute-done((bf16[512,512]{1,0:T(8,128)(2,1)}, bf16[512,512]{1,0:T(8,128)(2,1)S(1)}, u32[]{:S(2)}, u32[]{:S(2)}) %collective-permute-start.1) | collective-permute-done | bytes 524320 | tf_op jit(solution)/shard_map/ppermute | solution.py:25
  20.6 1.2 copy.10
  21.8 15.9 %all_gather.12 = bf16[384,1024]{0,1:T(8,128)(2,1)S(1)} all-gather(bf16[384,512]{0,1:T(8,128)(2,1)S(1)} %copy.10), channel_id=1, replica_groups=mesh['xlo'=2,'y'=4,'core'=2,'zhi'=2,'zlo'=4,'xhi'=2] {'xhi'}, dimensions={1}, use_global_device_ids=true | all-gather | bytes 1179648 | tf_op jit(solution)/shard_map/all_gather | solution.py:32
  37.7 14.0 %collective-permute-start = (bf16[384,1024]{0,1:T(8,128)(2,1)S(1)}, bf16[384,1024]{0,1:T(8,128)(2,1)S(1)}, u32[]{:S(2)}, u32[]{:S(2)}) collective-permute-start(bf16[384,1024]{0,1:T(8,128)(2,1)S(1)} %all_gather.12), channel_id=1, source_target_pairs={{0,8},{8,0},{1,9},{9,1},{2,10},{10,2},{3,11},{11,3},{4,12},{12,4},... | collective-permute-start | bytes 2359304 | tf_op jit(solution)/shard_map/ppermute | solution.py:33
  51.6 17.3 %collective-permute-done = bf16[384,1024]{0,1:T(8,128)(2,1)S(1)} collective-permute-done((bf16[384,1024]{0,1:T(8,128)(2,1)S(1)}, bf16[384,1024]{0,1:T(8,128)(2,1)S(1)}, u32[]{:S(2)}, u32[]{:S(2)}) %collective-permute-start) | collective-permute-done | bytes 786464 | tf_op jit(solution)/shard_map/ppermute | solution.py:33
  69.2 30.2 %all-gather.6.cloned.1.call-done = bf16[8192,512]{1,0:T(8,128)(2,1)} async-done(((bf16[512,512]{1,0:T(8,128)(2,1)}), bf16[8192,512]{1,0:T(8,128)(2,1)}) %all-gather.6.cloned.1.call-update) | async-done | bytes 8388624 | tf_op jit(solution)/shard_map/all_gather | solution.py:36
  99.5 6.8 %bitcast_convert_fusion = bf16[384,4,512]{2,0,1:T(8,128)(2,1)S(1)} fusion(bf16[384,4,512,1]{0,2,1,3:T(8,128)(2,1)S(1)} %bitcast.29, bf16[4,4,512,512]{3,2,1,0:T(8,128)(2,1)} %bitcast.30), kind=kOutput, calls=%fused_computation.1 | convolution fusion | flops 3222011904 | bytes 11534336 | tf_op jit(solution)/shard_map/iqh,rqhf->irf/dot_general | solution.py:37
  106.3 40.8 %all_to_all.5 = bf16[384,4,512]{2,0,1:T(8,128)(2,1)S(1)} all-to-all(bf16[384,4,512]{2,0,1:T(8,128)(2,1)S(1)} %bitcast_convert_fusion), channel_id=1, replica_groups=mesh['xlo'=2,'y'=4,'core'=2,'zhi'=2,'zlo'=4,'xhi'=2] {'zlo'}, dimensions={1} | all-to-all | bytes 3145728 | tf_op jit(solution)/shard_map/all_to_all | solution.py:40
  148.4 2.8 %collective-permute-start.2 = (f32[384]{0:T(512)S(1)}, f32[384]{0:T(512)S(1)}, u32[]{:S(2)}, u32[]{:S(2)}) collective-permute-start(f32[384]{0:T(512)S(1)} %multiply_reduce_fusion), channel_id=1, source_target_pairs={{0,1},{1,0},{8,9},{9,8},{2,3},{3,2},{10,11},{11,10},{4,5},{5,4},{1... | collective-permute-start | bytes 4616 | tf_op jit(solution)/shard_map/ppermute | solution.py:46
  151.1 3.8 %collective-permute-start.3 = (f32[384]{0:T(512)S(1)}, f32[384]{0:T(512)S(1)}, u32[]{:S(2)}, u32[]{:S(2)}) collective-permute-start(f32[384]{0:T(512)S(1)} %multiply_reduce_fusion), channel_id=1, source_target_pairs={{0,8},{1,9},{8,0},{9,1},{2,10},{3,11},{10,2},{11,3},{4,12},{5,13},... | collective-permute-start | bytes 4616 | tf_op jit(solution)/shard_map/ppermute | solution.py:46
  155.0 1.5 collective-permute-start.4
  156.5 1.0 collective-permute-done.3
  157.5 6.3 %collective-permute-done.4 = f32[384]{0:T(512)S(1)} collective-permute-done((f32[384]{0:T(512)S(1)}, f32[384]{0:T(512)S(1)}, u32[]{:S(2)}, u32[]{:S(2)}) %collective-permute-start.4) | collective-permute-done | bytes 1568 | tf_op jit(solution)/shard_map/ppermute | solution.py:46
  163.7 1.5 collective-permute-start.6
  165.3 2.0 collective-permute-start.7
  167.4 2.1 collective-permute-done.7
  169.5 1.0 fusion.20
  176.3 29.9 %all-gather.4.cloned.1.call-done = bf16[1536,512]{1,0:T(8,128)(2,1)} async-done(((bf16[96,512]{1,0:T(8,128)(2,1)}), bf16[1536,512]{1,0:T(8,128)(2,1)}) %all-gather.4.cloned.1.call-update) | async-done | bytes 1572880 | tf_op jit(solution)/shard_map/all_gather | solution.py:56
  206.2 3.0 %fusion.11 = f32[1,512,640]{2,1,0:T(8,128)S(1)} fusion(bf16[1536,640]{1,0:T(8,128)(2,1)S(1)} %copy-done, s32[]{:T(128)S(6)} %select_n.28, bf16[1536,512]{1,0:T(8,128)(2,1)} %all-gather.4.cloned.1.call-done), kind=kOutput, calls=%fused_computation.13 | convolution fusion | flops 1006632960 | bytes 4849668 | tf_op jit(solution)/shard_map/dot_general | solution.py:63
  209.2 1.5 fusion.14
  210.7 1.5 fusion.8
  212.2 1.5 fusion.17
  213.7 2.8 %maximum_multiply_fusion = f32[4,512,640]{2,1,0:T(8,128)} fusion(f32[1,512,640]{2,1,0:T(8,128)S(1)} %fusion.17, f32[1,512,640]{2,1,0:T(8,128)S(1)} %fusion.14, f32[1,512,640]{2,1,0:T(8,128)S(1)} %fusion.11, f32[1,512,640]{2,1,0:T(8,128)S(1)} %fusion.8), kind=kLoop, calls=%fused_computation | loop fusion | flops 5242880 | bytes 10485760 | tf_op jit(solution)/shard_map/mul | solution.py:64
  (31 shorter events, 3.2 us)
Async XLA Ops:
  6.5 199.7 %copy-start = (bf16[1536,640]{1,0:T(8,128)(2,1)S(1)}, bf16[1536,640]{1,0:T(8,128)(2,1)}, u32[]{:S(2)}) copy-start(bf16[1536,640]{1,0:T(8,128)(2,1)} %param.13) | copy-start | bytes 5898244
  6.5 93.0 %all-gather.6.cloned.1.call-start = ((), (), s32[]{:S(2)}) async-start(), calls=%async_computation.2 | async-start | bytes 8912896 | tf_op jit(solution)/shard_map/all_gather | solution.py:36
  6.5 13.2 %collective-permute-start.1 = (bf16[512,512]{1,0:T(8,128)(2,1)}, bf16[512,512]{1,0:T(8,128)(2,1)S(1)}, u32[]{:S(2)}, u32[]{:S(2)}) collective-permute-start(bf16[512,512]{1,0:T(8,128)(2,1)} %param.8), channel_id=1, source_target_pairs={{0,0},{16,1},{2,2},{18,3},{4,4},{20,5},{6,6},{22,7},{128,8},{144,9... | collective-permute-start | bytes 1572872 | tf_op jit(solution)/shard_map/ppermute | solution.py:25
  19.8 0.8 copy-start.2
  20.6 185.6 %all-gather.4.cloned.1.call-start = ((), (), s32[]{:S(2)}) async-start(), calls=%async_computation.1 | async-start | bytes 1671168 | tf_op jit(solution)/shard_map/all_gather | solution.py:56
  37.7 31.2 %collective-permute-start = (bf16[384,1024]{0,1:T(8,128)(2,1)S(1)}, bf16[384,1024]{0,1:T(8,128)(2,1)S(1)}, u32[]{:S(2)}, u32[]{:S(2)}) collective-permute-start(bf16[384,1024]{0,1:T(8,128)(2,1)S(1)} %all_gather.12), channel_id=1, source_target_pairs={{0,8},{8,0},{1,9},{9,1},{2,10},{10,2},{3,11},{11,3},{4,12},{12,4},... | collective-permute-start | bytes 2359304 | tf_op jit(solution)/shard_map/ppermute | solution.py:33
  147.2 1.0 copy-start.3
  147.2 9.3 %copy-start.5 = (s32[1,384]{1,0:T(1,128)S(1)}, s32[1,384]{1,0:T(1,128)}, u32[]{:S(2)}) copy-start(s32[1,384]{1,0:T(1,128)} %param.11) | copy-start | bytes 4612
  147.2 22.3 %copy-start.6 = (f32[512]{0:T(512)S(1)}, f32[512]{0:T(512)}, u32[]{:S(2)}) copy-start(f32[512]{0:T(512)} %param.10) | copy-start | bytes 6148
  148.2 22.3 %copy-start.4 = (s32[4]{0:T(128)S(1)}, s32[4]{0:T(128)}, u32[]{:S(2)}) copy-start(s32[4]{0:T(128)} %param.12) | copy-start | bytes 52
  148.4 8.2 %collective-permute-start.2 = (f32[384]{0:T(512)S(1)}, f32[384]{0:T(512)S(1)}, u32[]{:S(2)}, u32[]{:S(2)}) collective-permute-start(f32[384]{0:T(512)S(1)} %multiply_reduce_fusion), channel_id=1, source_target_pairs={{0,1},{1,0},{8,9},{9,8},{2,3},{3,2},{10,11},{11,10},{4,5},{5,4},{1... | collective-permute-start | bytes 4616 | tf_op jit(solution)/shard_map/ppermute | solution.py:46
  151.1 6.3 %collective-permute-start.3 = (f32[384]{0:T(512)S(1)}, f32[384]{0:T(512)S(1)}, u32[]{:S(2)}, u32[]{:S(2)}) collective-permute-start(f32[384]{0:T(512)S(1)} %multiply_reduce_fusion), channel_id=1, source_target_pairs={{0,8},{1,9},{8,0},{9,1},{2,10},{3,11},{10,2},{11,3},{4,12},{5,13},... | collective-permute-start | bytes 4616 | tf_op jit(solution)/shard_map/ppermute | solution.py:46
  155.0 8.8 %collective-permute-start.4 = (f32[384]{0:T(512)S(1)}, f32[384]{0:T(512)S(1)}, u32[]{:S(2)}, u32[]{:S(2)}) collective-permute-start(f32[384]{0:T(512)S(1)} %multiply_reduce_fusion), channel_id=1, source_target_pairs={{0,9},{1,8},{8,1},{9,0},{2,11},{3,10},{10,3},{11,2},{4,13},{5,12},... | collective-permute-start | bytes 4616 | tf_op jit(solution)/shard_map/ppermute | solution.py:46
  163.7 3.7 %collective-permute-start.5 = (f32[384]{0:T(512)S(1)}, f32[384]{0:T(512)S(1)}, u32[]{:S(2)}, u32[]{:S(2)}) collective-permute-start(f32[384]{0:T(512)S(1)} %add_add_fusion), channel_id=1, source_target_pairs={{0,2},{2,0},{4,6},{6,4},{1,3},{3,1},{5,7},{7,5},{8,10},{10,8},{12,... | collective-permute-start | bytes 4616 | tf_op jit(solution)/shard_map/ppermute | solution.py:46
  163.7 3.7 %collective-permute-start.6 = (f32[384]{0:T(512)S(1)}, f32[384]{0:T(512)S(1)}, u32[]{:S(2)}, u32[]{:S(2)}) collective-permute-start(f32[384]{0:T(512)S(1)} %add_add_fusion), channel_id=1, source_target_pairs={{0,4},{2,6},{4,0},{6,2},{1,5},{3,7},{5,1},{7,3},{8,12},{10,14},{12... | collective-permute-start | bytes 4616 | tf_op jit(solution)/shard_map/ppermute | solution.py:46
  165.3 4.2 %collective-permute-start.7 = (f32[384]{0:T(512)S(1)}, f32[384]{0:T(512)S(1)}, u32[]{:S(2)}, u32[]{:S(2)}) collective-permute-start(f32[384]{0:T(512)S(1)} %add_add_fusion), channel_id=1, source_target_pairs={{0,6},{2,4},{4,2},{6,0},{1,7},{3,5},{5,3},{7,1},{8,14},{10,12},{12... | collective-permute-start | bytes 4616 | tf_op jit(solution)/shard_map/ppermute | solution.py:46
  206.2 3.0 %copy-start.1 = (bf16[1536,512]{1,0:T(8,128)(2,1)S(1)}, bf16[1536,512]{1,0:T(8,128)(2,1)}, u32[]{:S(2)}) copy-start(bf16[1536,512]{1,0:T(8,128)(2,1)} %all-gather.4.cloned.1.call-done) | copy-start | bytes 4718596
Sparse Core Ops, SparseCore 0:
  20.7 78.7 all-gather.5
  170.6 35.5 all-gather.3

commit v17 on v14

--- a/solution.py
+++ b/solution.py
@@ -51,7 +51,16 @@
     ).astype(jnp.bfloat16)
     width = binned.shape[1]
     total_trs = responses.shape[0]
-    story = lax.all_gather(binned, GROUP, axis=0, tiled=True)
+    story = binned[None]
+    for axis in ("y", ("xlo", "core")):
+        size = lax.axis_size(axis)
+        by_xor = jnp.stack(
+            [story] + [lax.ppermute(story, axis, [(i, i ^ m) for i in range(size)]) for m in range(1, size)]
+        )
+        mine = lax.axis_index(axis)
+        story = jnp.stack([lax.dynamic_index_in_dim(by_xor, p ^ mine, 0, keepdims=False) for p in range(size)])
+    xlos, ys, cores = lax.axis_size("xlo"), lax.axis_size("y"), lax.axis_size("core")
+    story = story.reshape(xlos, cores, ys, -1, width).transpose(0, 2, 1, 3, 4).reshape(-1, width)
     extended = jnp.concatenate([jnp.zeros((LAGS, width), story.dtype), story], axis=0)
     contract = (((0,), (0,)), ((), ()))
     products = []

time: 209 us -> 206 us (0.986)
  waiting for transfers between devices: 90 us -> 75 us
  starting transfers between devices: 20.7 us -> 32.9 us
  matrix products: 15.2 us -> 13.1 us
    all_gather x1 -> x0, waiting for transfers between devices: 31.4 us -> none  [on_device(): story = lax.all_gather(binned, GROUP, axis=0, tiled=True)]
    ppermute x0 -> x6, waiting for transfers between devices: none -> 16.4 us  [on_device(): lax.ppermute(story, axis, [(i, i ^ m) for i in range(size)])]
    ppermute x0 -> x6, starting transfers between devices: none -> 12.2 us  [on_device(): lax.ppermute(story, axis, [(i, i ^ m) for i in range(size)])]
  transfers between devices with their start and end apart: 10 -> 15, of which waited for: 7 -> 10; matrix products, arithmetic and copies ran while one was open for 1% -> 1% of each run, Pallas kernels for 0% -> 0%
where the time goes in v17:
time: 206 us; the launch traced here: 205 us
  waiting for transfers between devices  75 us (36%)
  blocking collectives  57.2 us (28%)
  starting transfers between devices  32.9 us (16%)
  between operations  18.5 us (9%)
  matrix products  13.1 us (6%)
  other arithmetic  5.1 us (2%)
  local copies, waits for them, and re-layouts  3.71 us (2%)
    all_to_all x1, blocking collectives, on_device(): lax.all_to_all(partial.astype(jnp.bfloat16), 'zhi', 1, 1, tiled=True)  44.4 us
    all_gather x1, waiting for transfers between devices, on_device(): lax.all_gather(ring_block(out_weight), GROUP, axis=0)  23.7 us
    ppermute x1, waiting for transfers between devices, on_device(): other = lax.ppermute(pair, 'zlo', [(0, 1), (1, 0)])  17.9 us
    ppermute x6, waiting for transfers between devices, on_device(): lax.ppermute(story, axis, [(i, i ^ m) for i in range(size)])  16.4 us
    all_gather x1, blocking collectives, on_device(): pair = lax.all_gather(attention, 'xhi', axis=1, tiled=True)  12.8 us
    ppermute x6, starting transfers between devices, on_device(): lax.ppermute(story, axis, [(i, i ^ m) for i in range(size)])  12.2 us
    ppermute x1, waiting for transfers between devices, ring_block(): return lax.ppermute(block, GROUP + TENSOR, route)  10.8 us
    ppermute x6, starting transfers between devices, on_device(): lax.ppermute(squares, axis, [(i, i ^ m) for i in range(size)])  10.1 us
  transfers between devices with their start and end apart: 15, of which 10 were waited for; matrix products, arithmetic and copies ran while one was open for 1% of the time, Pallas kernels for 0%

profile of v17, /device:TPU:1, one launch (start us, length us, event | category | flops | bytes accessed | tf_op | source)
XLA Modules:
  0.0 205.5 jit_solution(1691738578515700596)
XLA Ops:
  6.5 6.1 %collective-permute-start.1 = (bf16[512,512]{1,0:T(8,128)(2,1)}, bf16[512,512]{1,0:T(8,128)(2,1)S(1)}, u32[]{:S(2)}, u32[]{:S(2)}) collective-permute-start(bf16[512,512]{1,0:T(8,128)(2,1)} %param.8), channel_id=1, source_target_pairs={{0,0},{16,1},{32,2},{48,3},{4,4},{20,5},{36,6},{52,7},{8,8},{24,9}... | collective-permute-start | bytes 1572872 | tf_op jit(solution)/shard_map/ppermute | solution.py:23
  12.7 10.8 %collective-permute-done.1 = bf16[512,512]{1,0:T(8,128)(2,1)S(1)} collective-permute-done((bf16[512,512]{1,0:T(8,128)(2,1)}, bf16[512,512]{1,0:T(8,128)(2,1)S(1)}, u32[]{:S(2)}, u32[]{:S(2)}) %collective-permute-start.1) | collective-permute-done | bytes 524320 | tf_op jit(solution)/shard_map/ppermute | solution.py:23
  25.6 12.8 %all_gather.9 = bf16[384,1024]{0,1:T(8,128)(2,1)S(1)} all-gather(bf16[384,512]{0,1:T(8,128)(2,1)S(1)} %copy.15), channel_id=1, replica_groups=mesh['xlo'=2,'y'=4,'core'=2,'zhi'=4,'zlo'=2,'xhi'=2] {'xhi'}, dimensions={1}, use_global_device_ids=true | all-gather | bytes 1179648 | tf_op jit(solution)/shard_map/all_gather | solution.py:30
  38.3 4.4 %collective-permute-start = (bf16[384,1024]{0,1:T(8,128)(2,1)S(1)}, bf16[384,1024]{0,1:T(8,128)(2,1)S(1)}, u32[]{:S(2)}, u32[]{:S(2)}) collective-permute-start(bf16[384,1024]{0,1:T(8,128)(2,1)S(1)} %all_gather.9), channel_id=1, source_target_pairs={{0,2},{2,0},{1,3},{3,1},{4,6},{6,4},{5,7},{7,5},{8,10},{10,8},{9,1... | collective-permute-start | bytes 2359304 | tf_op jit(solution)/shard_map/ppermute | solution.py:31
  42.7 17.9 %collective-permute-done = bf16[384,1024]{0,1:T(8,128)(2,1)S(1)} collective-permute-done((bf16[384,1024]{0,1:T(8,128)(2,1)S(1)}, bf16[384,1024]{0,1:T(8,128)(2,1)S(1)}, u32[]{:S(2)}, u32[]{:S(2)}) %collective-permute-start) | collective-permute-done | bytes 786464 | tf_op jit(solution)/shard_map/ppermute | solution.py:31
  60.9 23.7 %all-gather.3.cloned.1.call-done = bf16[8192,512]{1,0:T(8,128)(2,1)} async-done(((bf16[512,512]{1,0:T(8,128)(2,1)}), bf16[8192,512]{1,0:T(8,128)(2,1)}) %all-gather.3.cloned.1.call-update) | async-done | bytes 8388624 | tf_op jit(solution)/shard_map/all_gather | solution.py:34
  84.6 6.8 %bitcast_convert_fusion = bf16[384,4,512]{2,0,1:T(8,128)(2,1)S(1)} fusion(bf16[384,4,512,1]{0,2,1,3:T(8,128)(2,1)S(1)} %bitcast.51, bf16[4,4,512,512]{3,2,1,0:T(8,128)(2,1)} %bitcast.62), kind=kOutput, calls=%fused_computation.1 | convolution fusion | flops 3222011904 | bytes 11534336 | tf_op jit(solution)/shard_map/iqh,rqhf->irf/dot_general | solution.py:35
  91.4 44.4 %all_to_all.5 = bf16[384,4,512]{2,0,1:T(8,128)(2,1)S(1)} all-to-all(bf16[384,4,512]{2,0,1:T(8,128)(2,1)S(1)} %bitcast_convert_fusion), channel_id=1, replica_groups=mesh['xlo'=2,'y'=4,'core'=2,'zhi'=4,'zlo'=2,'xhi'=2] {'zhi'}, dimensions={1} | all-to-all | bytes 3145728 | tf_op jit(solution)/shard_map/all_to_all | solution.py:38
  137.1 2.8 %collective-permute-start.2 = (f32[384]{0:T(512)S(1)}, f32[384]{0:T(512)S(1)}, u32[]{:S(2)}, u32[]{:S(2)}) collective-permute-start(f32[384]{0:T(512)S(1)} %multiply_reduce_fusion), channel_id=1, source_target_pairs={{0,1},{1,0},{2,3},{3,2},{4,5},{5,4},{6,7},{7,6},{8,9},{9,8},{10,11... | collective-permute-start | bytes 4616 | tf_op jit(solution)/shard_map/ppermute | solution.py:44
  142.3 2.4 %collective-permute-done.4 = f32[384]{0:T(512)S(1)} collective-permute-done((f32[384]{0:T(512)S(1)}, f32[384]{0:T(512)S(1)}, u32[]{:S(2)}, u32[]{:S(2)}) %collective-permute-start.4) | collective-permute-done | bytes 1568 | tf_op jit(solution)/shard_map/ppermute | solution.py:44
  144.7 2.5 %collective-permute-start.5 = (f32[384]{0:T(512)S(1)}, f32[384]{0:T(512)S(1)}, u32[]{:S(2)}, u32[]{:S(2)}) collective-permute-start(f32[384]{0:T(512)S(1)} %add_add_fusion), channel_id=1, source_target_pairs={{0,4},{4,0},{8,12},{12,8},{1,5},{5,1},{9,13},{13,9},{2,6},{6,2},{1... | collective-permute-start | bytes 4616 | tf_op jit(solution)/shard_map/ppermute | solution.py:44
  148.0 2.5 %collective-permute-start.7 = (f32[384]{0:T(512)S(1)}, f32[384]{0:T(512)S(1)}, u32[]{:S(2)}, u32[]{:S(2)}) collective-permute-start(f32[384]{0:T(512)S(1)} %add_add_fusion), channel_id=1, source_target_pairs={{0,12},{4,8},{8,4},{12,0},{1,13},{5,9},{9,5},{13,1},{2,14},{6,10},... | collective-permute-start | bytes 4616 | tf_op jit(solution)/shard_map/ppermute | solution.py:44
  150.7 2.8 %collective-permute-done.6 = f32[384]{0:T(512)S(1)} collective-permute-done((f32[384]{0:T(512)S(1)}, f32[384]{0:T(512)S(1)}, u32[]{:S(2)}, u32[]{:S(2)}) %collective-permute-start.6) | collective-permute-done | bytes 1568 | tf_op jit(solution)/shard_map/ppermute | solution.py:44
  155.1 2.1 %collective-permute-start.9 = (bf16[1,96,512]{2,1,0:T(8,128)(2,1)S(1)}, bf16[1,96,512]{2,1,0:T(8,128)(2,1)S(1)}, u32[]{:S(2)}, u32[]{:S(2)}) collective-permute-start(bf16[1,96,512]{2,1,0:T(8,128)(2,1)S(1)} %bitcast.56), channel_id=1, source_target_pairs={{0,64},{32,96},{64,0},{96,32},{1,65},{33,97},{65,1},{97,33},{2,66}... | collective-permute-start | bytes 294920 | tf_op jit(solution)/shard_map/ppermute | solution.py:58
  157.8 2.5 %collective-permute-done.9 = bf16[1,96,512]{2,1,0:T(8,128)(2,1)S(1)} collective-permute-done((bf16[1,96,512]{2,1,0:T(8,128)(2,1)S(1)}, bf16[1,96,512]{2,1,0:T(8,128)(2,1)S(1)}, u32[]{:S(2)}, u32[]{:S(2)}) %collective-permute-start.9) | collective-permute-done | bytes 98336 | tf_op jit(solution)/shard_map/ppermute | solution.py:58
  160.3 1.6 collective-permute-done.10
  163.0 6.7 %collective-permute-start.11 = (bf16[4,1,96,512]{3,2,0,1:T(8,128)(2,1)}, bf16[4,1,96,512]{3,2,0,1:T(8,128)(2,1)S(1)}, u32[]{:S(2)}, u32[]{:S(2)}) collective-permute-start(bf16[4,1,96,512]{3,2,0,1:T(8,128)(2,1)} %get-tuple-element.12), channel_id=1, source_target_pairs={{0,16},{16,0},{128,144},{144,128},{1,17},{17,1},{129,145},{145,129... | collective-permute-start | bytes 1179656 | tf_op jit(solution)/shard_map/ppermute | solution.py:58
  169.7 1.6 collective-permute-start.13
  176.9 3.6 %collective-permute-done.12 = bf16[4,1,96,512]{3,2,0,1:T(8,128)(2,1)S(1)} collective-permute-done((bf16[4,1,96,512]{3,2,0,1:T(8,128)(2,1)}, bf16[4,1,96,512]{3,2,0,1:T(8,128)(2,1)S(1)}, u32[]{:S(2)}, u32[]{:S(2)}) %collective-permute-start.12) | collective-permute-done | bytes 393248 | tf_op jit(solution)/shard_map/ppermute | solution.py:58
  180.5 8.6 %collective-permute-done.13 = bf16[4,1,96,512]{3,2,1,0:T(8,128)(2,1)S(1)} collective-permute-done((bf16[4,1,96,512]{3,2,1,0:T(8,128)(2,1)}, bf16[4,1,96,512]{3,2,1,0:T(8,128)(2,1)S(1)}, u32[]{:S(2)}, u32[]{:S(2)}) %collective-permute-start.13) | collective-permute-done | bytes 393248 | tf_op jit(solution)/shard_map/ppermute | solution.py:58
  191.3 1.5 fusion.14
  192.8 1.5 fusion.8
  194.3 1.5 fusion.17
  195.8 2.8 %maximum_multiply_fusion = f32[4,512,640]{2,1,0:T(8,128)} fusion(f32[1,512,640]{2,1,0:T(8,128)S(1)} %fusion.17, f32[1,512,640]{2,1,0:T(8,128)S(1)} %fusion.14, f32[1,512,640]{2,1,0:T(8,128)S(1)} %fusion.11, f32[1,512,640]{2,1,0:T(8,128)S(1)} %fusion.8), kind=kLoop, calls=%fused_computation | loop fusion | flops 5242880 | bytes 10485760 | tf_op jit(solution)/shard_map/mul | solution.py:71
  (45 shorter events, 12.9 us)
Async XLA Ops:
  6.5 183.3 %copy-start = (bf16[1536,640]{1,0:T(8,128)(2,1)S(1)}, bf16[1536,640]{1,0:T(8,128)(2,1)}, u32[]{:S(2)}) copy-start(bf16[1536,640]{1,0:T(8,128)(2,1)} %param.13) | copy-start | bytes 5898244
  6.5 78.1 %all-gather.3.cloned.1.call-start = ((), (), s32[]{:S(2)}) async-start(), calls=%async_computation.1 | async-start | bytes 8912896 | tf_op jit(solution)/shard_map/all_gather | solution.py:34
  6.5 17.0 %collective-permute-start.1 = (bf16[512,512]{1,0:T(8,128)(2,1)}, bf16[512,512]{1,0:T(8,128)(2,1)S(1)}, u32[]{:S(2)}, u32[]{:S(2)}) collective-permute-start(bf16[512,512]{1,0:T(8,128)(2,1)} %param.8), channel_id=1, source_target_pairs={{0,0},{16,1},{32,2},{48,3},{4,4},{20,5},{36,6},{52,7},{8,8},{24,9}... | collective-permute-start | bytes 1572872 | tf_op jit(solution)/shard_map/ppermute | solution.py:23
  23.5 0.8 copy-start.1
  38.3 22.3 %collective-permute-start = (bf16[384,1024]{0,1:T(8,128)(2,1)S(1)}, bf16[384,1024]{0,1:T(8,128)(2,1)S(1)}, u32[]{:S(2)}, u32[]{:S(2)}) collective-permute-start(bf16[384,1024]{0,1:T(8,128)(2,1)S(1)} %all_gather.9), channel_id=1, source_target_pairs={{0,2},{2,0},{1,3},{3,1},{4,6},{6,4},{5,7},{7,5},{8,10},{10,8},{9,1... | collective-permute-start | bytes 2359304 | tf_op jit(solution)/shard_map/ppermute | solution.py:31
  135.9 1.0 copy-start.2
  135.9 5.4 %copy-start.4 = (s32[1,384]{1,0:T(1,128)S(1)}, s32[1,384]{1,0:T(1,128)}, u32[]{:S(2)}) copy-start(s32[1,384]{1,0:T(1,128)} %param.11) | copy-start | bytes 4612
  135.9 17.6 %copy-start.5 = (f32[512]{0:T(512)S(1)}, f32[512]{0:T(512)}, u32[]{:S(2)}) copy-start(f32[512]{0:T(512)} %param.10) | copy-start | bytes 6148
  137.1 4.3 %collective-permute-start.2 = (f32[384]{0:T(512)S(1)}, f32[384]{0:T(512)S(1)}, u32[]{:S(2)}, u32[]{:S(2)}) collective-permute-start(f32[384]{0:T(512)S(1)} %multiply_reduce_fusion), channel_id=1, source_target_pairs={{0,1},{1,0},{2,3},{3,2},{4,5},{5,4},{6,7},{7,6},{8,9},{9,8},{10,11... | collective-permute-start | bytes 4616 | tf_op jit(solution)/shard_map/ppermute | solution.py:44
  139.8 2.4 %collective-permute-start.3 = (f32[384]{0:T(512)S(1)}, f32[384]{0:T(512)S(1)}, u32[]{:S(2)}, u32[]{:S(2)}) collective-permute-start(f32[384]{0:T(512)S(1)} %multiply_reduce_fusion), channel_id=1, source_target_pairs={{0,2},{1,3},{2,0},{3,1},{4,6},{5,7},{6,4},{7,5},{8,10},{9,11},{10,... | collective-permute-start | bytes 4616 | tf_op jit(solution)/shard_map/ppermute | solution.py:44
  139.8 4.8 %collective-permute-start.4 = (f32[384]{0:T(512)S(1)}, f32[384]{0:T(512)S(1)}, u32[]{:S(2)}, u32[]{:S(2)}) collective-permute-start(f32[384]{0:T(512)S(1)} %multiply_reduce_fusion), channel_id=1, source_target_pairs={{0,3},{1,2},{2,1},{3,0},{4,7},{5,6},{6,5},{7,4},{8,11},{9,10},{10,... | collective-permute-start | bytes 4616 | tf_op jit(solution)/shard_map/ppermute | solution.py:44
  144.7 6.0 %collective-permute-start.5 = (f32[384]{0:T(512)S(1)}, f32[384]{0:T(512)S(1)}, u32[]{:S(2)}, u32[]{:S(2)}) collective-permute-start(f32[384]{0:T(512)S(1)} %add_add_fusion), channel_id=1, source_target_pairs={{0,4},{4,0},{8,12},{12,8},{1,5},{5,1},{9,13},{13,9},{2,6},{6,2},{1... | collective-permute-start | bytes 4616 | tf_op jit(solution)/shard_map/ppermute | solution.py:44
  147.2 6.3 %collective-permute-start.6 = (f32[384]{0:T(512)S(1)}, f32[384]{0:T(512)S(1)}, u32[]{:S(2)}, u32[]{:S(2)}) collective-permute-start(f32[384]{0:T(512)S(1)} %add_add_fusion), channel_id=1, source_target_pairs={{0,8},{4,12},{8,0},{12,4},{1,9},{5,13},{9,1},{13,5},{2,10},{6,14},... | collective-permute-start | bytes 4616 | tf_op jit(solution)/shard_map/ppermute | solution.py:44
  148.0 5.5 %collective-permute-start.7 = (f32[384]{0:T(512)S(1)}, f32[384]{0:T(512)S(1)}, u32[]{:S(2)}, u32[]{:S(2)}) collective-permute-start(f32[384]{0:T(512)S(1)} %add_add_fusion), channel_id=1, source_target_pairs={{0,12},{4,8},{8,4},{12,0},{1,13},{5,9},{9,5},{13,1},{2,14},{6,10},... | collective-permute-start | bytes 4616 | tf_op jit(solution)/shard_map/ppermute | solution.py:44
  153.9 3.9 %collective-permute-start.8 = (bf16[1,96,512]{2,1,0:T(8,128)(2,1)S(1)}, bf16[1,96,512]{2,1,0:T(8,128)(2,1)S(1)}, u32[]{:S(2)}, u32[]{:S(2)}) collective-permute-start(bf16[1,96,512]{2,1,0:T(8,128)(2,1)S(1)} %bitcast.55), channel_id=1, source_target_pairs={{0,32},{32,0},{64,96},{96,64},{1,33},{33,1},{65,97},{97,65},{2,34}... | collective-permute-start | bytes 294920 | tf_op jit(solution)/shard_map/ppermute | solution.py:58
  155.1 5.2 %collective-permute-start.9 = (bf16[1,96,512]{2,1,0:T(8,128)(2,1)S(1)}, bf16[1,96,512]{2,1,0:T(8,128)(2,1)S(1)}, u32[]{:S(2)}, u32[]{:S(2)}) collective-permute-start(bf16[1,96,512]{2,1,0:T(8,128)(2,1)S(1)} %bitcast.56), channel_id=1, source_target_pairs={{0,64},{32,96},{64,0},{96,32},{1,65},{33,97},{65,1},{97,33},{2,66}... | collective-permute-start | bytes 294920 | tf_op jit(solution)/shard_map/ppermute | solution.py:58
  157.3 4.7 %collective-permute-start.10 = (bf16[1,96,512]{2,1,0:T(8,128)(2,1)S(1)}, bf16[1,96,512]{2,1,0:T(8,128)(2,1)S(1)}, u32[]{:S(2)}, u32[]{:S(2)}) collective-permute-start(bf16[1,96,512]{2,1,0:T(8,128)(2,1)S(1)} %bitcast.57), channel_id=1, source_target_pairs={{0,96},{32,64},{64,32},{96,0},{1,97},{33,65},{65,33},{97,1},{2,98}... | collective-permute-start | bytes 294920 | tf_op jit(solution)/shard_map/ppermute | solution.py:58
  162.0 9.4 %copy-start.3 = (s32[4]{0:T(128)S(1)}, s32[4]{0:T(128)}, u32[]{:S(2)}) copy-start(s32[4]{0:T(128)} %param.12) | copy-start | bytes 52
  163.0 13.9 %collective-permute-start.11 = (bf16[4,1,96,512]{3,2,0,1:T(8,128)(2,1)}, bf16[4,1,96,512]{3,2,0,1:T(8,128)(2,1)S(1)}, u32[]{:S(2)}, u32[]{:S(2)}) collective-permute-start(bf16[4,1,96,512]{3,2,0,1:T(8,128)(2,1)} %get-tuple-element.12), channel_id=1, source_target_pairs={{0,16},{16,0},{128,144},{144,128},{1,17},{17,1},{129,145},{145,129... | collective-permute-start | bytes 1179656 | tf_op jit(solution)/shard_map/ppermute | solution.py:58
  169.7 10.9 %collective-permute-start.12 = (bf16[4,1,96,512]{3,2,0,1:T(8,128)(2,1)}, bf16[4,1,96,512]{3,2,0,1:T(8,128)(2,1)S(1)}, u32[]{:S(2)}, u32[]{:S(2)}) collective-permute-start(bf16[4,1,96,512]{3,2,0,1:T(8,128)(2,1)} %get-tuple-element.12), channel_id=1, source_target_pairs={{0,128},{16,144},{128,0},{144,16},{1,129},{17,145},{129,1},{145,17... | collective-permute-start | bytes 1179656 | tf_op jit(solution)/shard_map/ppermute | solution.py:58
  169.7 19.5 %collective-permute-start.13 = (bf16[4,1,96,512]{3,2,1,0:T(8,128)(2,1)}, bf16[4,1,96,512]{3,2,1,0:T(8,128)(2,1)S(1)}, u32[]{:S(2)}, u32[]{:S(2)}) collective-permute-start(bf16[4,1,96,512]{3,2,1,0:T(8,128)(2,1)} %get-tuple-element.13), channel_id=1, source_target_pairs={{0,144},{16,128},{128,16},{144,0},{1,145},{17,129},{129,17},{145,1... | collective-permute-start | bytes 1179656 | tf_op jit(solution)/shard_map/ppermute | solution.py:58
Sparse Core Ops, SparseCore 0:
  24.5 60.0 all-gather.2

commit v18 on v14

--- a/solution.py
+++ b/solution.py
@@ -23,6 +23,20 @@
     return lax.ppermute(block, GROUP + TENSOR, route)
 
 
+def gather_group(block):
+    gathered = block[None]
+    for axis in ("y", ("xlo", "core")):
+        size = lax.axis_size(axis)
+        by_xor = jnp.stack(
+            [gathered] + [lax.ppermute(gathered, axis, [(i, i ^ m) for i in range(size)]) for m in range(1, size)]
+        )
+        mine = lax.axis_index(axis)
+        gathered = jnp.stack([lax.dynamic_index_in_dim(by_xor, p ^ mine, 0, keepdims=False) for p in range(size)])
+    xlos, ys, cores = lax.axis_size("xlo"), lax.axis_size("y"), lax.axis_size("core")
+    shape = block.shape
+    return gathered.reshape((xlos, cores, ys) + shape).transpose((0, 2, 1) + tuple(range(3, 3 + len(shape)))).reshape((-1,) + shape)
+
+
 def on_device(attention, out_weight, residual, gain, token_tr, lag_offsets, responses):
     quad = lax.axis_size(("zlo", "xhi"))
     ring = lax.axis_size("zhi")
@@ -31,7 +45,7 @@
     other = lax.ppermute(pair, "zlo", [(0, 1), (1, 0)])
     low = lax.axis_index("zlo") == 0
     slab = jnp.concatenate([jnp.where(low, pair, other), jnp.where(low, other, pair)], axis=1)
-    blocks = lax.all_gather(ring_block(out_weight), GROUP, axis=0).reshape(ring, quad, heads, -1)
+    blocks = gather_group(ring_block(out_weight)).reshape(ring, quad, heads, -1)
     partial = jnp.einsum(
         "iqh,rqhf->irf", slab.reshape(-1, quad, heads), blocks, preferred_element_type=jnp.float32
     )
@@ -51,7 +65,7 @@
     ).astype(jnp.bfloat16)
     width = binned.shape[1]
     total_trs = responses.shape[0]
-    story = lax.all_gather(binned, GROUP, axis=0, tiled=True)
+    story = gather_group(binned).reshape(-1, width)
     extended = jnp.concatenate([jnp.zeros((LAGS, width), story.dtype), story], axis=0)
     contract = (((0,), (0,)), ((), ()))
     products = []

time: 209 us -> 302 us (1.44)
  blocking collectives: 57.2 us -> 135 us
  starting transfers between devices: 20.7 us -> 46.7 us
  waiting for transfers between devices: 90 us -> 73 us
  other arithmetic: 3.69 us -> 18.2 us
  between operations: 18.7 us -> 5.07 us
  local copies, waits for them, and re-layouts: 3.42 us -> 10.4 us
    all_gather x1, blocking collectives: 12.8 us -> 96.7 us  [on_device(): pair = lax.all_gather(attention, 'xhi', axis=1, tiled=True)]
    all_gather x2 -> x0, waiting for transfers between devices: 55 us -> none  [the longest x1 31.4 us: on_device(): story = lax.all_gather(binned, GROUP, axis=0, tiled=True)]
    ppermute x0 -> x12, waiting for transfers between devices: none -> 39.3 us  [gather_group(): lax.ppermute(gathered, axis, [(i, i ^ m) for i in range(size)])]
    ppermute x0 -> x12, starting transfers between devices: none -> 21 us  [gather_group(): lax.ppermute(gathered, axis, [(i, i ^ m) for i in range(size)])]
    another operation x0 -> x8, other arithmetic: none -> 13.3 us  [the longest x6 9.3 us: gather_group(): jnp.stack([gathered] + [lax.ppermute(gathered, axis, [(i, i ^ m) for i in...]
    ppermute x6, starting transfers between devices: 10.1 us -> 18.4 us  [on_device(): lax.ppermute(squares, axis, [(i, i ^ m) for i in range(size)])]
    reshape x0 -> x2, local copies, waits for them, and re-layouts: none -> 7.62 us  [gather_group(): gathered.reshape((xlos, cores, ys) + shape)]
    all_to_all x1, blocking collectives: 44.4 us -> 38.7 us  [on_device(): lax.all_to_all(partial.astype(jnp.bfloat16), 'zhi', 1, 1, tiled=True)]
  transfers between devices with their start and end apart: 10 -> 20, of which waited for: 7 -> 13; matrix products, arithmetic and copies ran while one was open for 1% -> 1% of each run, Pallas kernels for 0% -> 0%
where the time goes in v18:
time: 302 us
  blocking collectives  135 us (45%)
  waiting for transfers between devices  73 us (24%)
  starting transfers between devices  46.7 us (15%)
  other arithmetic  18.2 us (6%)
  matrix products  13.1 us (4%)
  local copies, waits for them, and re-layouts  10.4 us (3%)
  between operations  5.07 us (2%)
    all_gather x1, blocking collectives, on_device(): pair = lax.all_gather(attention, 'xhi', axis=1, tiled=True)  96.7 us
    ppermute x12, waiting for transfers between devices, gather_group(): lax.ppermute(gathered, axis, [(i, i ^ m) for i in range(size)])  39.3 us
    all_to_all x1, blocking collectives, on_device(): lax.all_to_all(partial.astype(jnp.bfloat16), 'zhi', 1, 1, tiled=True)  38.7 us
    ppermute x12, starting transfers between devices, gather_group(): lax.ppermute(gathered, axis, [(i, i ^ m) for i in range(size)])  21 us
    ppermute x6, starting transfers between devices, on_device(): lax.ppermute(squares, axis, [(i, i ^ m) for i in range(size)])  18.4 us
    ppermute x1, waiting for transfers between devices, on_device(): other = lax.ppermute(pair, 'zlo', [(0, 1), (1, 0)])  16.3 us
    ppermute x1, waiting for transfers between devices, ring_block(): return lax.ppermute(block, GROUP + TENSOR, route)  10.8 us
    another operation x6, other arithmetic, gather_group(): jnp.stack([gathered] + [lax.ppermute(gathered, axis, [(i, i ^ m) for i in...  9.3 us
  transfers between devices with their start and end apart: 20, of which 13 were waited for; matrix products, arithmetic and copies ran while one was open for 1% of the time, Pallas kernels for 0%

profile of v18, /device:TPU:1, one launch (start us, length us, event | category | flops | bytes accessed | tf_op | source)
XLA Modules:
  0.0 301.8 jit_solution(2437191266324871071)
XLA Ops:
  0.0 6.1 %collective-permute-start.1 = (bf16[512,512]{1,0:T(8,128)(2,1)}, bf16[512,512]{1,0:T(8,128)(2,1)S(1)}, u32[]{:S(2)}, u32[]{:S(2)}) collective-permute-start(bf16[512,512]{1,0:T(8,128)(2,1)} %param.8), channel_id=1, source_target_pairs={{0,0},{16,1},{32,2},{48,3},{4,4},{20,5},{36,6},{52,7},{8,8},{24,9}... | collective-permute-start | bytes 1572872 | tf_op jit(solution)/shard_map/ppermute | solution.py:23
  6.2 10.8 %collective-permute-done.1 = bf16[512,512]{1,0:T(8,128)(2,1)S(1)} collective-permute-done((bf16[512,512]{1,0:T(8,128)(2,1)}, bf16[512,512]{1,0:T(8,128)(2,1)S(1)}, u32[]{:S(2)}, u32[]{:S(2)}) %collective-permute-start.1) | collective-permute-done | bytes 524320 | tf_op jit(solution)/shard_map/ppermute | solution.py:23
  17.0 4.4 %collective-permute-start.2 = (bf16[1,512,512]{2,1,0:T(8,128)(2,1)S(1)}, bf16[1,512,512]{2,1,0:T(8,128)(2,1)S(1)}, u32[]{:S(2)}, u32[]{:S(2)}) collective-permute-start(bf16[1,512,512]{2,1,0:T(8,128)(2,1)S(1)} %bitcast.70), channel_id=1, source_target_pairs={{0,32},{32,0},{64,96},{96,64},{1,33},{33,1},{65,97},{97,65},{2,34}... | collective-permute-start | bytes 1572872 | tf_op jit(solution)/shard_map/ppermute | solution.py:31
  21.4 2.6 collective-permute-start.3
  24.0 10.0 %collective-permute-done.2 = bf16[1,512,512]{2,1,0:T(8,128)(2,1)S(1)} collective-permute-done((bf16[1,512,512]{2,1,0:T(8,128)(2,1)S(1)}, bf16[1,512,512]{2,1,0:T(8,128)(2,1)S(1)}, u32[]{:S(2)}, u32[]{:S(2)}) %collective-permute-start.2) | collective-permute-done | bytes 524320 | tf_op jit(solution)/shard_map/ppermute | solution.py:31
  33.9 11.5 %collective-permute-done.3 = bf16[1,512,512]{2,1,0:T(8,128)(2,1)S(1)} collective-permute-done((bf16[1,512,512]{2,1,0:T(8,128)(2,1)S(1)}, bf16[1,512,512]{2,1,0:T(8,128)(2,1)S(1)}, u32[]{:S(2)}, u32[]{:S(2)}) %collective-permute-start.3) | collective-permute-done | bytes 524320 | tf_op jit(solution)/shard_map/ppermute | solution.py:31
  45.4 3.2 %collective-permute-done.4 = bf16[1,512,512]{2,1,0:T(8,128)(2,1)} collective-permute-done((bf16[1,512,512]{2,1,0:T(8,128)(2,1)S(1)}, bf16[1,512,512]{2,1,0:T(8,128)(2,1)}, u32[]{:S(2)}, u32[]{:S(2)}) %collective-permute-start.4) | collective-permute-done | bytes 524320 | tf_op jit(solution)/shard_map/ppermute | solution.py:31
  50.2 2.9 fusion.39
  56.1 96.7 %all_gather.3 = bf16[384,1024]{0,1:T(8,128)(2,1)S(1)} all-gather(bf16[384,512]{0,1:T(8,128)(2,1)S(1)} %copy.21), channel_id=1, replica_groups=mesh['xlo'=2,'y'=4,'core'=2,'zhi'=4,'zlo'=2,'xhi'=2] {'xhi'}, dimensions={1}, use_global_device_ids=true | all-gather | bytes 1179648 | tf_op jit(solution)/shard_map/all_gather | solution.py:44
  154.0 16.3 %collective-permute-done = bf16[384,1024]{0,1:T(8,128)(2,1)S(1)} collective-permute-done((bf16[384,1024]{0,1:T(8,128)(2,1)S(1)}, bf16[384,1024]{0,1:T(8,128)(2,1)S(1)}, u32[]{:S(2)}, u32[]{:S(2)}) %collective-permute-start) | collective-permute-done | bytes 786464 | tf_op jit(solution)/shard_map/ppermute | solution.py:45
  172.6 3.9 %pad_maximum_fusion = bf16[4,4,1,512,512]{4,3,1,2,0:T(8,128)(2,1)S(1)} fusion(bf16[1,4,1,512,512]{4,3,1,2,0:T(8,128)(2,1)} %bitcast.12, bf16[1,4,1,512,512]{4,3,1,2,0:T(8,128)(2,1)} %bitcast.11, bf16[1,4,1,512,512]{4,3,1,2,0:T(8,128)(2,1)} %bitcast.9, bf16[1,4,1,512,512]{4,3,1,2,0:T(8,128)(2,1)S(1)} %copy-done.1), kind=kLoop, calls=%fused_computation | loop fusion | flops 12582912 | bytes 16777216 | tf_op jit(solution)/shard_map/stack | solution.py:30
  177.3 3.9 %pad_maximum_fusion.1 = bf16[4,4,1,512,512]{4,3,1,2,0:T(8,128)(2,1)} fusion(bf16[1,4,1,512,512]{4,3,1,2,0:T(8,128)(2,1)S(1)} %get-tuple-element.6, bf16[1,4,1,512,512]{4,3,1,2,0:T(8,128)(2,1)S(1)} %get-tuple-element.7, bf16[1,4,1,512,512]{4,3,1,2,0:T(8,128)(2,1)S(1)} %get-tuple-element.8, bf16[1,4,1,512,512]{4,3,1,2,0:T(8,128)(2,1)S(1)} %get-tuple-element.5), kind=kLoop, calls=%fused_computation.1 | loop fusion | flops 12582912 | bytes 16777216 | tf_op jit(solution)/shard_map/stack | solution.py:34
  181.1 7.5 %copy.24 = bf16[2,2,4,512,512]{4,3,1,2,0:T(8,128)(2,1)} copy(bf16[2,2,4,512,512]{4,3,2,1,0:T(8,128)(2,1)} %bitcast.66) | data formatting | bytes 16777216 | tf_op jit(solution)/shard_map/reshape | solution.py:37
  188.6 6.9 %bitcast_convert_fusion = bf16[384,4,512]{2,0,1:T(8,128)(2,1)S(1)} fusion(bf16[384,4,512,1]{0,2,1,3:T(8,128)(2,1)S(1)} %bitcast.69, bf16[4,4,512,512]{3,2,1,0:T(8,128)(2,1)} %bitcast.67), kind=kOutput, calls=%fused_computation.3 | convolution fusion | flops 3222011904 | bytes 11534336 | tf_op jit(solution)/shard_map/iqh,rqhf->irf/dot_general | solution.py:49
  195.5 38.7 %all_to_all.5 = bf16[384,4,512]{2,0,1:T(8,128)(2,1)S(1)} all-to-all(bf16[384,4,512]{2,0,1:T(8,128)(2,1)S(1)} %bitcast_convert_fusion), channel_id=1, replica_groups=mesh['xlo'=2,'y'=4,'core'=2,'zhi'=4,'zlo'=2,'xhi'=2] {'zhi'}, dimensions={1} | all-to-all | bytes 3145728 | tf_op jit(solution)/shard_map/all_to_all | solution.py:52
  234.6 12.0 %collective-permute-start.10 = (f32[384]{0:T(512)S(1)}, f32[384]{0:T(512)S(1)}, u32[]{:S(2)}, u32[]{:S(2)}) collective-permute-start(f32[384]{0:T(512)S(1)} %multiply_reduce_fusion), channel_id=1, source_target_pairs={{0,3},{1,2},{2,1},{3,0},{4,7},{5,6},{6,5},{7,4},{8,11},{9,10},{10,... | collective-permute-start | bytes 4616 | tf_op jit(solution)/shard_map/ppermute | solution.py:58
  247.6 3.0 collective-permute-done.8
  250.9 4.2 %collective-permute-start.12 = (f32[384]{0:T(512)S(1)}, f32[384]{0:T(512)S(1)}, u32[]{:S(2)}, u32[]{:S(2)}) collective-permute-start(f32[384]{0:T(512)S(1)} %add_add_fusion), channel_id=1, source_target_pairs={{0,8},{4,12},{8,0},{12,4},{1,9},{5,13},{9,1},{13,5},{2,10},{6,14},... | collective-permute-start | bytes 4616 | tf_op jit(solution)/shard_map/ppermute | solution.py:58
  257.3 2.3 collective-permute-done.13
  260.2 3.7 %collective-permute-start.16 = (bf16[1,96,512]{2,1,0:T(8,128)(2,1)S(1)}, bf16[1,96,512]{2,1,0:T(8,128)(2,1)S(1)}, u32[]{:S(2)}, u32[]{:S(2)}) collective-permute-start(bf16[1,96,512]{2,1,0:T(8,128)(2,1)S(1)} %bitcast.81), channel_id=1, source_target_pairs={{0,96},{32,64},{64,32},{96,0},{1,97},{33,65},{65,33},{97,1},{2,98}... | collective-permute-start | bytes 294920 | tf_op jit(solution)/shard_map/ppermute | solution.py:31
  267.2 5.6 %collective-permute-start.17 = (bf16[4,1,96,512]{3,2,0,1:T(8,128)(2,1)}, bf16[4,1,96,512]{3,2,0,1:T(8,128)(2,1)S(1)}, u32[]{:S(2)}, u32[]{:S(2)}) collective-permute-start(bf16[4,1,96,512]{3,2,0,1:T(8,128)(2,1)} %get-tuple-element.23), channel_id=1, source_target_pairs={{0,16},{16,0},{128,144},{144,128},{1,17},{17,1},{129,145},{145,129... | collective-permute-start | bytes 1179656 | tf_op jit(solution)/shard_map/ppermute | solution.py:31
  280.0 3.7 %collective-permute-done.18 = bf16[4,1,96,512]{3,2,0,1:T(8,128)(2,1)S(1)} collective-permute-done((bf16[4,1,96,512]{3,2,0,1:T(8,128)(2,1)}, bf16[4,1,96,512]{3,2,0,1:T(8,128)(2,1)S(1)}, u32[]{:S(2)}, u32[]{:S(2)}) %collective-permute-start.18) | collective-permute-done | bytes 393248 | tf_op jit(solution)/shard_map/ppermute | solution.py:31
  283.8 8.6 %collective-permute-done.19 = bf16[4,1,96,512]{3,2,1,0:T(8,128)(2,1)S(1)} collective-permute-done((bf16[4,1,96,512]{3,2,1,0:T(8,128)(2,1)}, bf16[4,1,96,512]{3,2,1,0:T(8,128)(2,1)S(1)}, u32[]{:S(2)}, u32[]{:S(2)}) %collective-permute-start.19) | collective-permute-done | bytes 393248 | tf_op jit(solution)/shard_map/ppermute | solution.py:31
  299.0 2.8 maximum_multiply_fusion
  (65 shorter events, 25.4 us)
Async XLA Ops:
  0.0 293.1 %copy-start = (bf16[1536,640]{1,0:T(8,128)(2,1)S(1)}, bf16[1536,640]{1,0:T(8,128)(2,1)}, u32[]{:S(2)}) copy-start(bf16[1536,640]{1,0:T(8,128)(2,1)} %param.13) | copy-start | bytes 5898244
  0.0 17.0 %collective-permute-start.1 = (bf16[512,512]{1,0:T(8,128)(2,1)}, bf16[512,512]{1,0:T(8,128)(2,1)S(1)}, u32[]{:S(2)}, u32[]{:S(2)}) collective-permute-start(bf16[512,512]{1,0:T(8,128)(2,1)} %param.8), channel_id=1, source_target_pairs={{0,0},{16,1},{32,2},{48,3},{4,4},{20,5},{36,6},{52,7},{8,8},{24,9}... | collective-permute-start | bytes 1572872 | tf_op jit(solution)/shard_map/ppermute | solution.py:23
  17.0 16.9 %collective-permute-start.2 = (bf16[1,512,512]{2,1,0:T(8,128)(2,1)S(1)}, bf16[1,512,512]{2,1,0:T(8,128)(2,1)S(1)}, u32[]{:S(2)}, u32[]{:S(2)}) collective-permute-start(bf16[1,512,512]{2,1,0:T(8,128)(2,1)S(1)} %bitcast.70), channel_id=1, source_target_pairs={{0,32},{32,0},{64,96},{96,64},{1,33},{33,1},{65,97},{97,65},{2,34}... | collective-permute-start | bytes 1572872 | tf_op jit(solution)/shard_map/ppermute | solution.py:31
  21.4 24.1 %collective-permute-start.3 = (bf16[1,512,512]{2,1,0:T(8,128)(2,1)S(1)}, bf16[1,512,512]{2,1,0:T(8,128)(2,1)S(1)}, u32[]{:S(2)}, u32[]{:S(2)}) collective-permute-start(bf16[1,512,512]{2,1,0:T(8,128)(2,1)S(1)} %bitcast.71), channel_id=1, source_target_pairs={{0,64},{32,96},{64,0},{96,32},{1,65},{33,97},{65,1},{97,33},{2,66}... | collective-permute-start | bytes 1572872 | tf_op jit(solution)/shard_map/ppermute | solution.py:31
  24.0 24.7 %collective-permute-start.4 = (bf16[1,512,512]{2,1,0:T(8,128)(2,1)S(1)}, bf16[1,512,512]{2,1,0:T(8,128)(2,1)}, u32[]{:S(2)}, u32[]{:S(2)}) collective-permute-start(bf16[1,512,512]{2,1,0:T(8,128)(2,1)S(1)} %bitcast.72), channel_id=1, source_target_pairs={{0,96},{32,64},{64,32},{96,0},{1,97},{33,65},{65,33},{97,1},{2,98}... | collective-permute-start | bytes 1572872 | tf_op jit(solution)/shard_map/ppermute | solution.py:31
  53.1 118.7 %collective-permute-start.6 = (bf16[4,1,512,512]{3,2,0,1:T(8,128)(2,1)}, bf16[4,1,512,512]{3,2,0,1:T(8,128)(2,1)}, u32[]{:S(2)}, u32[]{:S(2)}) collective-permute-start(bf16[4,1,512,512]{3,2,0,1:T(8,128)(2,1)} %get-tuple-element.10), channel_id=1, source_target_pairs={{0,128},{16,144},{128,0},{144,16},{1,129},{17,145},{129,1},{145,17... | collective-permute-start | bytes 6291464 | tf_op jit(solution)/shard_map/ppermute | solution.py:31
  54.9 116.9 %collective-permute-start.7 = (bf16[4,1,512,512]{3,2,1,0:T(8,128)(2,1)}, bf16[4,1,512,512]{3,2,1,0:T(8,128)(2,1)}, u32[]{:S(2)}, u32[]{:S(2)}) collective-permute-start(bf16[4,1,512,512]{3,2,1,0:T(8,128)(2,1)} %get-tuple-element.11), channel_id=1, source_target_pairs={{0,144},{16,128},{128,16},{144,0},{1,145},{17,129},{129,17},{145,1... | collective-permute-start | bytes 6291464 | tf_op jit(solution)/shard_map/ppermute | solution.py:31
  55.5 116.3 %collective-permute-start.5 = (bf16[4,1,512,512]{3,2,0,1:T(8,128)(2,1)}, bf16[4,1,512,512]{3,2,0,1:T(8,128)(2,1)}, u32[]{:S(2)}, u32[]{:S(2)}) collective-permute-start(bf16[4,1,512,512]{3,2,0,1:T(8,128)(2,1)} %get-tuple-element.10), channel_id=1, source_target_pairs={{0,16},{16,0},{128,144},{144,128},{1,17},{17,1},{129,145},{145,129... | collective-permute-start | bytes 6291464 | tf_op jit(solution)/shard_map/ppermute | solution.py:31
  152.8 17.6 %collective-permute-start = (bf16[384,1024]{0,1:T(8,128)(2,1)S(1)}, bf16[384,1024]{0,1:T(8,128)(2,1)S(1)}, u32[]{:S(2)}, u32[]{:S(2)}) collective-permute-start(bf16[384,1024]{0,1:T(8,128)(2,1)S(1)} %all_gather.3), channel_id=1, source_target_pairs={{0,2},{2,0},{1,3},{3,1},{4,6},{6,4},{5,7},{7,5},{8,10},{10,8},{9,1... | collective-permute-start | bytes 2359304 | tf_op jit(solution)/shard_map/ppermute | solution.py:45
  195.5 38.9 %copy-start.4 = (bf16[384,512]{1,0:T(8,128)(2,1)S(1)}, bf16[384,512]{1,0:T(8,128)(2,1)}, u32[]{:S(2)}) copy-start(bf16[384,512]{1,0:T(8,128)(2,1)} %param.9) | copy-start | bytes 1179652
  234.1 25.5 %copy-start.7 = (f32[512]{0:T(512)S(1)}, f32[512]{0:T(512)}, u32[]{:S(2)}) copy-start(f32[512]{0:T(512)} %param.10) | copy-start | bytes 6148
  234.6 13.0 %collective-permute-start.10 = (f32[384]{0:T(512)S(1)}, f32[384]{0:T(512)S(1)}, u32[]{:S(2)}, u32[]{:S(2)}) collective-permute-start(f32[384]{0:T(512)S(1)} %multiply_reduce_fusion), channel_id=1, source_target_pairs={{0,3},{1,2},{2,1},{3,0},{4,7},{5,6},{6,5},{7,4},{8,11},{9,10},{10,... | collective-permute-start | bytes 4616 | tf_op jit(solution)/shard_map/ppermute | solution.py:58
  246.6 3.9 %collective-permute-start.8 = (f32[384]{0:T(512)S(1)}, f32[384]{0:T(512)S(1)}, u32[]{:S(2)}, u32[]{:S(2)}) collective-permute-start(f32[384]{0:T(512)S(1)} %multiply_reduce_fusion), channel_id=1, source_target_pairs={{0,1},{1,0},{2,3},{3,2},{4,5},{5,4},{6,7},{7,6},{8,9},{9,8},{10,11... | collective-permute-start | bytes 4616 | tf_op jit(solution)/shard_map/ppermute | solution.py:58
  246.6 3.9 %collective-permute-start.9 = (f32[384]{0:T(512)S(1)}, f32[384]{0:T(512)S(1)}, u32[]{:S(2)}, u32[]{:S(2)}) collective-permute-start(f32[384]{0:T(512)S(1)} %multiply_reduce_fusion), channel_id=1, source_target_pairs={{0,2},{1,3},{2,0},{3,1},{4,6},{5,7},{6,4},{7,5},{8,10},{9,11},{10,... | collective-permute-start | bytes 4616 | tf_op jit(solution)/shard_map/ppermute | solution.py:58
  250.6 6.0 %collective-permute-start.11 = (f32[384]{0:T(512)S(1)}, f32[384]{0:T(512)S(1)}, u32[]{:S(2)}, u32[]{:S(2)}) collective-permute-start(f32[384]{0:T(512)S(1)} %add_add_fusion), channel_id=1, source_target_pairs={{0,4},{4,0},{8,12},{12,8},{1,5},{5,1},{9,13},{13,9},{2,6},{6,2},{1... | collective-permute-start | bytes 4616 | tf_op jit(solution)/shard_map/ppermute | solution.py:58
  250.9 6.4 %collective-permute-start.12 = (f32[384]{0:T(512)S(1)}, f32[384]{0:T(512)S(1)}, u32[]{:S(2)}, u32[]{:S(2)}) collective-permute-start(f32[384]{0:T(512)S(1)} %add_add_fusion), channel_id=1, source_target_pairs={{0,8},{4,12},{8,0},{12,4},{1,9},{5,13},{9,1},{13,5},{2,10},{6,14},... | collective-permute-start | bytes 4616 | tf_op jit(solution)/shard_map/ppermute | solution.py:58
  255.1 4.5 %collective-permute-start.13 = (f32[384]{0:T(512)S(1)}, f32[384]{0:T(512)S(1)}, u32[]{:S(2)}, u32[]{:S(2)}) collective-permute-start(f32[384]{0:T(512)S(1)} %add_add_fusion), channel_id=1, source_target_pairs={{0,12},{4,8},{8,4},{12,0},{1,13},{5,9},{9,5},{13,1},{2,14},{6,10},... | collective-permute-start | bytes 4616 | tf_op jit(solution)/shard_map/ppermute | solution.py:58
  259.6 14.9 %copy-start.5 = (s32[4]{0:T(128)S(1)}, s32[4]{0:T(128)}, u32[]{:S(2)}) copy-start(s32[4]{0:T(128)} %param.12) | copy-start | bytes 52
  260.0 3.9 %collective-permute-start.14 = (bf16[1,96,512]{2,1,0:T(8,128)(2,1)S(1)}, bf16[1,96,512]{2,1,0:T(8,128)(2,1)S(1)}, u32[]{:S(2)}, u32[]{:S(2)}) collective-permute-start(bf16[1,96,512]{2,1,0:T(8,128)(2,1)S(1)} %bitcast.79), channel_id=1, source_target_pairs={{0,32},{32,0},{64,96},{96,64},{1,33},{33,1},{65,97},{97,65},{2,34}... | collective-permute-start | bytes 294920 | tf_op jit(solution)/shard_map/ppermute | solution.py:31
  260.1 5.1 %collective-permute-start.15 = (bf16[1,96,512]{2,1,0:T(8,128)(2,1)S(1)}, bf16[1,96,512]{2,1,0:T(8,128)(2,1)S(1)}, u32[]{:S(2)}, u32[]{:S(2)}) collective-permute-start(bf16[1,96,512]{2,1,0:T(8,128)(2,1)S(1)} %bitcast.80), channel_id=1, source_target_pairs={{0,64},{32,96},{64,0},{96,32},{1,65},{33,97},{65,1},{97,33},{2,66}... | collective-permute-start | bytes 294920 | tf_op jit(solution)/shard_map/ppermute | solution.py:31
  260.2 6.0 %collective-permute-start.16 = (bf16[1,96,512]{2,1,0:T(8,128)(2,1)S(1)}, bf16[1,96,512]{2,1,0:T(8,128)(2,1)S(1)}, u32[]{:S(2)}, u32[]{:S(2)}) collective-permute-start(bf16[1,96,512]{2,1,0:T(8,128)(2,1)S(1)} %bitcast.81), channel_id=1, source_target_pairs={{0,96},{32,64},{64,32},{96,0},{1,97},{33,65},{65,33},{97,1},{2,98}... | collective-permute-start | bytes 294920 | tf_op jit(solution)/shard_map/ppermute | solution.py:31
  267.2 12.8 %collective-permute-start.17 = (bf16[4,1,96,512]{3,2,0,1:T(8,128)(2,1)}, bf16[4,1,96,512]{3,2,0,1:T(8,128)(2,1)S(1)}, u32[]{:S(2)}, u32[]{:S(2)}) collective-permute-start(bf16[4,1,96,512]{3,2,0,1:T(8,128)(2,1)} %get-tuple-element.23), channel_id=1, source_target_pairs={{0,16},{16,0},{128,144},{144,128},{1,17},{17,1},{129,145},{145,129... | collective-permute-start | bytes 1179656 | tf_op jit(solution)/shard_map/ppermute | solution.py:31
  272.9 10.9 %collective-permute-start.18 = (bf16[4,1,96,512]{3,2,0,1:T(8,128)(2,1)}, bf16[4,1,96,512]{3,2,0,1:T(8,128)(2,1)S(1)}, u32[]{:S(2)}, u32[]{:S(2)}) collective-permute-start(bf16[4,1,96,512]{3,2,0,1:T(8,128)(2,1)} %get-tuple-element.23), channel_id=1, source_target_pairs={{0,128},{16,144},{128,0},{144,16},{1,129},{17,145},{129,1},{145,17... | collective-permute-start | bytes 1179656 | tf_op jit(solution)/shard_map/ppermute | solution.py:31
  273.4 18.9 %collective-permute-start.19 = (bf16[4,1,96,512]{3,2,1,0:T(8,128)(2,1)}, bf16[4,1,96,512]{3,2,1,0:T(8,128)(2,1)S(1)}, u32[]{:S(2)}, u32[]{:S(2)}) collective-permute-start(bf16[4,1,96,512]{3,2,1,0:T(8,128)(2,1)} %get-tuple-element.24), channel_id=1, source_target_pairs={{0,144},{16,128},{128,16},{144,0},{1,145},{17,129},{129,17},{145,1... | collective-permute-start | bytes 1179656 | tf_op jit(solution)/shard_map/ppermute | solution.py:31
  (4 other events, 28.3 us)

commit v19 on v17

--- a/solution.py
+++ b/solution.py
@@ -27,7 +27,9 @@
     quad = lax.axis_size(("zlo", "xhi"))
     ring = lax.axis_size("zhi")
     heads = attention.shape[1]
-    pair = lax.all_gather(attention, "xhi", axis=1, tiled=True)
+    partner = lax.ppermute(attention, "xhi", [(0, 1), (1, 0)])
+    first = lax.axis_index("xhi") == 0
+    pair = jnp.concatenate([jnp.where(first, attention, partner), jnp.where(first, partner, attention)], axis=1)
     other = lax.ppermute(pair, "zlo", [(0, 1), (1, 0)])
     low = lax.axis_index("zlo") == 0
     slab = jnp.concatenate([jnp.where(low, pair, other), jnp.where(low, other, pair)], axis=1)

time: 206 us -> 206 us (level)
  blocking collectives: 57.2 us -> 44.4 us
  waiting for transfers between devices: 75 us -> 86.3 us
    all_gather x1 -> x0, blocking collectives: 12.8 us -> none  [on_device(): pair = lax.all_gather(attention, 'xhi', axis=1, tiled=True)]
    ppermute x0 -> x1, waiting for transfers between devices: none -> 12.1 us  [on_device(): partner = lax.ppermute(attention, 'xhi', [(0, 1), (1, 0)])]
  transfers between devices with their start and end apart: 15 -> 16, of which waited for: 10 -> 11; matrix products, arithmetic and copies ran while one was open for 1% -> 2% of each run, Pallas kernels for 0% -> 0%
where the time goes in v19:
time: 206 us; the launch traced here: 205 us
  waiting for transfers between devices  86.3 us (42%)
  blocking collectives  44.4 us (22%)
  starting transfers between devices  33 us (16%)
  between operations  18.5 us (9%)
  matrix products  13.1 us (6%)
  other arithmetic  6.57 us (3%)
  local copies, waits for them, and re-layouts  3.71 us (2%)
    all_to_all x1, blocking collectives, on_device(): lax.all_to_all(partial.astype(jnp.bfloat16), 'zhi', 1, 1, tiled=True)  44.4 us
    all_gather x1, waiting for transfers between devices, on_device(): lax.all_gather(ring_block(out_weight), GROUP, axis=0)  22.8 us
    ppermute x1, waiting for transfers between devices, on_device(): other = lax.ppermute(pair, 'zlo', [(0, 1), (1, 0)])  17.9 us
    ppermute x6, waiting for transfers between devices, on_device(): lax.ppermute(story, axis, [(i, i ^ m) for i in range(size)])  16.4 us
    ppermute x6, starting transfers between devices, on_device(): lax.ppermute(story, axis, [(i, i ^ m) for i in range(size)])  12.2 us
    ppermute x1, waiting for transfers between devices, on_device(): partner = lax.ppermute(attention, 'xhi', [(0, 1), (1, 0)])  12.1 us
    ppermute x1, waiting for transfers between devices, ring_block(): return lax.ppermute(block, GROUP + TENSOR, route)  10.8 us
    ppermute x6, starting transfers between devices, on_device(): lax.ppermute(squares, axis, [(i, i ^ m) for i in range(size)])  10.1 us
  transfers between devices with their start and end apart: 16, of which 11 were waited for; matrix products, arithmetic and copies ran while one was open for 2% of the time, Pallas kernels for 0%

profile of v19, /device:TPU:1, one launch (start us, length us, event | category | flops | bytes accessed | tf_op | source)
XLA Modules:
  0.0 205.5 jit_solution(10011582262800430114)
XLA Ops:
  6.5 6.1 %collective-permute-start.2 = (bf16[512,512]{1,0:T(8,128)(2,1)}, bf16[512,512]{1,0:T(8,128)(2,1)S(1)}, u32[]{:S(2)}, u32[]{:S(2)}) collective-permute-start(bf16[512,512]{1,0:T(8,128)(2,1)} %param.8), channel_id=1, source_target_pairs={{0,0},{16,1},{32,2},{48,3},{4,4},{20,5},{36,6},{52,7},{8,8},{24,9}... | collective-permute-start | bytes 1572872 | tf_op jit(solution)/shard_map/ppermute | solution.py:23
  12.7 10.8 %collective-permute-done.2 = bf16[512,512]{1,0:T(8,128)(2,1)S(1)} collective-permute-done((bf16[512,512]{1,0:T(8,128)(2,1)}, bf16[512,512]{1,0:T(8,128)(2,1)S(1)}, u32[]{:S(2)}, u32[]{:S(2)}) %collective-permute-start.2) | collective-permute-done | bytes 524320 | tf_op jit(solution)/shard_map/ppermute | solution.py:23
  25.7 12.1 %collective-permute-done = bf16[384,512]{0,1:T(8,128)(2,1)S(1)} collective-permute-done((bf16[384,512]{0,1:T(8,128)(2,1)S(1)}, bf16[384,512]{0,1:T(8,128)(2,1)S(1)}, u32[]{:S(2)}, u32[]{:S(2)}) %collective-permute-start) | collective-permute-done | bytes 393248 | tf_op jit(solution)/shard_map/ppermute | solution.py:30
  38.0 4.5 %collective-permute-start.1 = (bf16[384,1024]{0,1:T(8,128)(2,1)S(1)}, bf16[384,1024]{0,1:T(8,128)(2,1)}, u32[]{:S(2)}, u32[]{:S(2)}) collective-permute-start(bf16[384,1024]{0,1:T(8,128)(2,1)S(1)} %pad_maximum_fusion.3), channel_id=1, source_target_pairs={{0,2},{2,0},{1,3},{3,1},{4,6},{6,4},{5,7},{7,5},{8,10},{10,8},{9,1... | collective-permute-start | bytes 2359304 | tf_op jit(solution)/shard_map/ppermute | solution.py:33
  42.4 17.9 %collective-permute-done.1 = bf16[384,1024]{0,1:T(8,128)(2,1)} collective-permute-done((bf16[384,1024]{0,1:T(8,128)(2,1)S(1)}, bf16[384,1024]{0,1:T(8,128)(2,1)}, u32[]{:S(2)}, u32[]{:S(2)}) %collective-permute-start.1) | collective-permute-done | bytes 786464 | tf_op jit(solution)/shard_map/ppermute | solution.py:33
  61.9 22.8 %all-gather.3.cloned.1.call-done = bf16[8192,512]{1,0:T(8,128)(2,1)} async-done(((bf16[512,512]{1,0:T(8,128)(2,1)}), bf16[8192,512]{1,0:T(8,128)(2,1)}) %all-gather.3.cloned.1.call-update) | async-done | bytes 8388624 | tf_op jit(solution)/shard_map/all_gather | solution.py:36
  84.7 6.8 %bitcast_convert_fusion = bf16[384,4,512]{2,0,1:T(8,128)(2,1)S(1)} fusion(bf16[384,4,512,1]{0,2,1,3:T(8,128)(2,1)S(1)} %bitcast.51, bf16[4,4,512,512]{3,2,1,0:T(8,128)(2,1)} %bitcast.62), kind=kOutput, calls=%fused_computation.1 | convolution fusion | flops 3222011904 | bytes 11534336 | tf_op jit(solution)/shard_map/iqh,rqhf->irf/dot_general | solution.py:37
  91.5 44.4 %all_to_all.5 = bf16[384,4,512]{2,0,1:T(8,128)(2,1)S(1)} all-to-all(bf16[384,4,512]{2,0,1:T(8,128)(2,1)S(1)} %bitcast_convert_fusion), channel_id=1, replica_groups=mesh['xlo'=2,'y'=4,'core'=2,'zhi'=4,'zlo'=2,'xhi'=2] {'zhi'}, dimensions={1} | all-to-all | bytes 3145728 | tf_op jit(solution)/shard_map/all_to_all | solution.py:40
  137.1 2.8 %collective-permute-start.3 = (f32[384]{0:T(512)S(1)}, f32[384]{0:T(512)S(1)}, u32[]{:S(2)}, u32[]{:S(2)}) collective-permute-start(f32[384]{0:T(512)S(1)} %multiply_reduce_fusion), channel_id=1, source_target_pairs={{0,1},{1,0},{2,3},{3,2},{4,5},{5,4},{6,7},{7,6},{8,9},{9,8},{10,11... | collective-permute-start | bytes 4616 | tf_op jit(solution)/shard_map/ppermute | solution.py:46
  142.3 2.4 %collective-permute-done.5 = f32[384]{0:T(512)S(1)} collective-permute-done((f32[384]{0:T(512)S(1)}, f32[384]{0:T(512)S(1)}, u32[]{:S(2)}, u32[]{:S(2)}) %collective-permute-start.5) | collective-permute-done | bytes 1568 | tf_op jit(solution)/shard_map/ppermute | solution.py:46
  144.7 2.5 %collective-permute-start.6 = (f32[384]{0:T(512)S(1)}, f32[384]{0:T(512)S(1)}, u32[]{:S(2)}, u32[]{:S(2)}) collective-permute-start(f32[384]{0:T(512)S(1)} %add_add_fusion), channel_id=1, source_target_pairs={{0,4},{4,0},{8,12},{12,8},{1,5},{5,1},{9,13},{13,9},{2,6},{6,2},{1... | collective-permute-start | bytes 4616 | tf_op jit(solution)/shard_map/ppermute | solution.py:46
  148.0 2.5 %collective-permute-start.8 = (f32[384]{0:T(512)S(1)}, f32[384]{0:T(512)S(1)}, u32[]{:S(2)}, u32[]{:S(2)}) collective-permute-start(f32[384]{0:T(512)S(1)} %add_add_fusion), channel_id=1, source_target_pairs={{0,12},{4,8},{8,4},{12,0},{1,13},{5,9},{9,5},{13,1},{2,14},{6,10},... | collective-permute-start | bytes 4616 | tf_op jit(solution)/shard_map/ppermute | solution.py:46
  150.7 2.8 %collective-permute-done.7 = f32[384]{0:T(512)S(1)} collective-permute-done((f32[384]{0:T(512)S(1)}, f32[384]{0:T(512)S(1)}, u32[]{:S(2)}, u32[]{:S(2)}) %collective-permute-start.7) | collective-permute-done | bytes 1568 | tf_op jit(solution)/shard_map/ppermute | solution.py:46
  155.1 2.1 %collective-permute-start.10 = (bf16[1,96,512]{2,1,0:T(8,128)(2,1)S(1)}, bf16[1,96,512]{2,1,0:T(8,128)(2,1)S(1)}, u32[]{:S(2)}, u32[]{:S(2)}) collective-permute-start(bf16[1,96,512]{2,1,0:T(8,128)(2,1)S(1)} %bitcast.56), channel_id=1, source_target_pairs={{0,64},{32,96},{64,0},{96,32},{1,65},{33,97},{65,1},{97,33},{2,66}... | collective-permute-start | bytes 294920 | tf_op jit(solution)/shard_map/ppermute | solution.py:60
  157.8 2.5 %collective-permute-done.10 = bf16[1,96,512]{2,1,0:T(8,128)(2,1)S(1)} collective-permute-done((bf16[1,96,512]{2,1,0:T(8,128)(2,1)S(1)}, bf16[1,96,512]{2,1,0:T(8,128)(2,1)S(1)}, u32[]{:S(2)}, u32[]{:S(2)}) %collective-permute-start.10) | collective-permute-done | bytes 98336 | tf_op jit(solution)/shard_map/ppermute | solution.py:60
  160.3 1.6 collective-permute-done.11
  163.0 6.7 %collective-permute-start.12 = (bf16[4,1,96,512]{3,2,0,1:T(8,128)(2,1)}, bf16[4,1,96,512]{3,2,0,1:T(8,128)(2,1)S(1)}, u32[]{:S(2)}, u32[]{:S(2)}) collective-permute-start(bf16[4,1,96,512]{3,2,0,1:T(8,128)(2,1)} %get-tuple-element.14), channel_id=1, source_target_pairs={{0,16},{16,0},{128,144},{144,128},{1,17},{17,1},{129,145},{145,129... | collective-permute-start | bytes 1179656 | tf_op jit(solution)/shard_map/ppermute | solution.py:60
  169.7 1.6 collective-permute-start.14
  176.9 3.7 %collective-permute-done.13 = bf16[4,1,96,512]{3,2,0,1:T(8,128)(2,1)S(1)} collective-permute-done((bf16[4,1,96,512]{3,2,0,1:T(8,128)(2,1)}, bf16[4,1,96,512]{3,2,0,1:T(8,128)(2,1)S(1)}, u32[]{:S(2)}, u32[]{:S(2)}) %collective-permute-start.13) | collective-permute-done | bytes 393248 | tf_op jit(solution)/shard_map/ppermute | solution.py:60
  180.5 8.6 %collective-permute-done.14 = bf16[4,1,96,512]{3,2,1,0:T(8,128)(2,1)S(1)} collective-permute-done((bf16[4,1,96,512]{3,2,1,0:T(8,128)(2,1)}, bf16[4,1,96,512]{3,2,1,0:T(8,128)(2,1)S(1)}, u32[]{:S(2)}, u32[]{:S(2)}) %collective-permute-start.14) | collective-permute-done | bytes 393248 | tf_op jit(solution)/shard_map/ppermute | solution.py:60
  191.3 1.5 fusion.14
  192.8 1.5 fusion.8
  194.3 1.5 fusion.17
  195.8 2.8 %maximum_multiply_fusion = f32[4,512,640]{2,1,0:T(8,128)} fusion(f32[1,512,640]{2,1,0:T(8,128)S(1)} %fusion.17, f32[1,512,640]{2,1,0:T(8,128)S(1)} %fusion.14, f32[1,512,640]{2,1,0:T(8,128)S(1)} %fusion.11, f32[1,512,640]{2,1,0:T(8,128)S(1)} %fusion.8), kind=kLoop, calls=%fused_computation | loop fusion | flops 5242880 | bytes 10485760 | tf_op jit(solution)/shard_map/mul | solution.py:73
  (48 shorter events, 14.5 us)
Async XLA Ops:
  6.5 183.3 %copy-start = (bf16[1536,640]{1,0:T(8,128)(2,1)S(1)}, bf16[1536,640]{1,0:T(8,128)(2,1)}, u32[]{:S(2)}) copy-start(bf16[1536,640]{1,0:T(8,128)(2,1)} %param.13) | copy-start | bytes 5898244
  6.5 78.2 %all-gather.3.cloned.1.call-start = ((), (), s32[]{:S(2)}) async-start(), calls=%async_computation.1 | async-start | bytes 8912896 | tf_op jit(solution)/shard_map/all_gather | solution.py:36
  6.5 17.0 %collective-permute-start.2 = (bf16[512,512]{1,0:T(8,128)(2,1)}, bf16[512,512]{1,0:T(8,128)(2,1)S(1)}, u32[]{:S(2)}, u32[]{:S(2)}) collective-permute-start(bf16[512,512]{1,0:T(8,128)(2,1)} %param.8), channel_id=1, source_target_pairs={{0,0},{16,1},{32,2},{48,3},{4,4},{20,5},{36,6},{52,7},{8,8},{24,9}... | collective-permute-start | bytes 1572872 | tf_op jit(solution)/shard_map/ppermute | solution.py:23
  23.5 0.8 copy-start.1
  25.6 12.2 %collective-permute-start = (bf16[384,512]{0,1:T(8,128)(2,1)S(1)}, bf16[384,512]{0,1:T(8,128)(2,1)S(1)}, u32[]{:S(2)}, u32[]{:S(2)}) collective-permute-start(bf16[384,512]{0,1:T(8,128)(2,1)S(1)} %copy.18), channel_id=1, source_target_pairs={{0,1},{1,0},{2,3},{3,2},{4,5},{5,4},{6,7},{7,6},{8,9},{9,8},{10,11... | collective-permute-start | bytes 1179656 | tf_op jit(solution)/shard_map/ppermute | solution.py:30
  38.0 22.3 %collective-permute-start.1 = (bf16[384,1024]{0,1:T(8,128)(2,1)S(1)}, bf16[384,1024]{0,1:T(8,128)(2,1)}, u32[]{:S(2)}, u32[]{:S(2)}) collective-permute-start(bf16[384,1024]{0,1:T(8,128)(2,1)S(1)} %pad_maximum_fusion.3), channel_id=1, source_target_pairs={{0,2},{2,0},{1,3},{3,1},{4,6},{6,4},{5,7},{7,5},{8,10},{10,8},{9,1... | collective-permute-start | bytes 2359304 | tf_op jit(solution)/shard_map/ppermute | solution.py:33
  135.9 1.0 copy-start.2
  135.9 5.4 %copy-start.4 = (s32[1,384]{1,0:T(1,128)S(1)}, s32[1,384]{1,0:T(1,128)}, u32[]{:S(2)}) copy-start(s32[1,384]{1,0:T(1,128)} %param.11) | copy-start | bytes 4612
  135.9 17.6 %copy-start.5 = (f32[512]{0:T(512)S(1)}, f32[512]{0:T(512)}, u32[]{:S(2)}) copy-start(f32[512]{0:T(512)} %param.10) | copy-start | bytes 6148
  137.1 4.3 %collective-permute-start.3 = (f32[384]{0:T(512)S(1)}, f32[384]{0:T(512)S(1)}, u32[]{:S(2)}, u32[]{:S(2)}) collective-permute-start(f32[384]{0:T(512)S(1)} %multiply_reduce_fusion), channel_id=1, source_target_pairs={{0,1},{1,0},{2,3},{3,2},{4,5},{5,4},{6,7},{7,6},{8,9},{9,8},{10,11... | collective-permute-start | bytes 4616 | tf_op jit(solution)/shard_map/ppermute | solution.py:46
  139.8 2.4 %collective-permute-start.4 = (f32[384]{0:T(512)S(1)}, f32[384]{0:T(512)S(1)}, u32[]{:S(2)}, u32[]{:S(2)}) collective-permute-start(f32[384]{0:T(512)S(1)} %multiply_reduce_fusion), channel_id=1, source_target_pairs={{0,2},{1,3},{2,0},{3,1},{4,6},{5,7},{6,4},{7,5},{8,10},{9,11},{10,... | collective-permute-start | bytes 4616 | tf_op jit(solution)/shard_map/ppermute | solution.py:46
  139.8 4.8 %collective-permute-start.5 = (f32[384]{0:T(512)S(1)}, f32[384]{0:T(512)S(1)}, u32[]{:S(2)}, u32[]{:S(2)}) collective-permute-start(f32[384]{0:T(512)S(1)} %multiply_reduce_fusion), channel_id=1, source_target_pairs={{0,3},{1,2},{2,1},{3,0},{4,7},{5,6},{6,5},{7,4},{8,11},{9,10},{10,... | collective-permute-start | bytes 4616 | tf_op jit(solution)/shard_map/ppermute | solution.py:46
  144.7 6.0 %collective-permute-start.6 = (f32[384]{0:T(512)S(1)}, f32[384]{0:T(512)S(1)}, u32[]{:S(2)}, u32[]{:S(2)}) collective-permute-start(f32[384]{0:T(512)S(1)} %add_add_fusion), channel_id=1, source_target_pairs={{0,4},{4,0},{8,12},{12,8},{1,5},{5,1},{9,13},{13,9},{2,6},{6,2},{1... | collective-permute-start | bytes 4616 | tf_op jit(solution)/shard_map/ppermute | solution.py:46
  147.2 6.3 %collective-permute-start.7 = (f32[384]{0:T(512)S(1)}, f32[384]{0:T(512)S(1)}, u32[]{:S(2)}, u32[]{:S(2)}) collective-permute-start(f32[384]{0:T(512)S(1)} %add_add_fusion), channel_id=1, source_target_pairs={{0,8},{4,12},{8,0},{12,4},{1,9},{5,13},{9,1},{13,5},{2,10},{6,14},... | collective-permute-start | bytes 4616 | tf_op jit(solution)/shard_map/ppermute | solution.py:46
  148.0 5.5 %collective-permute-start.8 = (f32[384]{0:T(512)S(1)}, f32[384]{0:T(512)S(1)}, u32[]{:S(2)}, u32[]{:S(2)}) collective-permute-start(f32[384]{0:T(512)S(1)} %add_add_fusion), channel_id=1, source_target_pairs={{0,12},{4,8},{8,4},{12,0},{1,13},{5,9},{9,5},{13,1},{2,14},{6,10},... | collective-permute-start | bytes 4616 | tf_op jit(solution)/shard_map/ppermute | solution.py:46
  153.9 3.9 %collective-permute-start.9 = (bf16[1,96,512]{2,1,0:T(8,128)(2,1)S(1)}, bf16[1,96,512]{2,1,0:T(8,128)(2,1)S(1)}, u32[]{:S(2)}, u32[]{:S(2)}) collective-permute-start(bf16[1,96,512]{2,1,0:T(8,128)(2,1)S(1)} %bitcast.55), channel_id=1, source_target_pairs={{0,32},{32,0},{64,96},{96,64},{1,33},{33,1},{65,97},{97,65},{2,34}... | collective-permute-start | bytes 294920 | tf_op jit(solution)/shard_map/ppermute | solution.py:60
  155.1 5.2 %collective-permute-start.10 = (bf16[1,96,512]{2,1,0:T(8,128)(2,1)S(1)}, bf16[1,96,512]{2,1,0:T(8,128)(2,1)S(1)}, u32[]{:S(2)}, u32[]{:S(2)}) collective-permute-start(bf16[1,96,512]{2,1,0:T(8,128)(2,1)S(1)} %bitcast.56), channel_id=1, source_target_pairs={{0,64},{32,96},{64,0},{96,32},{1,65},{33,97},{65,1},{97,33},{2,66}... | collective-permute-start | bytes 294920 | tf_op jit(solution)/shard_map/ppermute | solution.py:60
  157.3 4.7 %collective-permute-start.11 = (bf16[1,96,512]{2,1,0:T(8,128)(2,1)S(1)}, bf16[1,96,512]{2,1,0:T(8,128)(2,1)S(1)}, u32[]{:S(2)}, u32[]{:S(2)}) collective-permute-start(bf16[1,96,512]{2,1,0:T(8,128)(2,1)S(1)} %bitcast.57), channel_id=1, source_target_pairs={{0,96},{32,64},{64,32},{96,0},{1,97},{33,65},{65,33},{97,1},{2,98}... | collective-permute-start | bytes 294920 | tf_op jit(solution)/shard_map/ppermute | solution.py:60
  162.0 9.4 %copy-start.3 = (s32[4]{0:T(128)S(1)}, s32[4]{0:T(128)}, u32[]{:S(2)}) copy-start(s32[4]{0:T(128)} %param.12) | copy-start | bytes 52
  163.0 13.8 %collective-permute-start.12 = (bf16[4,1,96,512]{3,2,0,1:T(8,128)(2,1)}, bf16[4,1,96,512]{3,2,0,1:T(8,128)(2,1)S(1)}, u32[]{:S(2)}, u32[]{:S(2)}) collective-permute-start(bf16[4,1,96,512]{3,2,0,1:T(8,128)(2,1)} %get-tuple-element.14), channel_id=1, source_target_pairs={{0,16},{16,0},{128,144},{144,128},{1,17},{17,1},{129,145},{145,129... | collective-permute-start | bytes 1179656 | tf_op jit(solution)/shard_map/ppermute | solution.py:60
  169.7 10.9 %collective-permute-start.13 = (bf16[4,1,96,512]{3,2,0,1:T(8,128)(2,1)}, bf16[4,1,96,512]{3,2,0,1:T(8,128)(2,1)S(1)}, u32[]{:S(2)}, u32[]{:S(2)}) collective-permute-start(bf16[4,1,96,512]{3,2,0,1:T(8,128)(2,1)} %get-tuple-element.14), channel_id=1, source_target_pairs={{0,128},{16,144},{128,0},{144,16},{1,129},{17,145},{129,1},{145,17... | collective-permute-start | bytes 1179656 | tf_op jit(solution)/shard_map/ppermute | solution.py:60
  169.7 19.5 %collective-permute-start.14 = (bf16[4,1,96,512]{3,2,1,0:T(8,128)(2,1)}, bf16[4,1,96,512]{3,2,1,0:T(8,128)(2,1)S(1)}, u32[]{:S(2)}, u32[]{:S(2)}) collective-permute-start(bf16[4,1,96,512]{3,2,1,0:T(8,128)(2,1)} %get-tuple-element.15), channel_id=1, source_target_pairs={{0,144},{16,128},{128,16},{144,0},{1,145},{17,129},{129,17},{145,1... | collective-permute-start | bytes 1179656 | tf_op jit(solution)/shard_map/ppermute | solution.py:60
Sparse Core Ops, SparseCore 0:
  24.5 60.1 all-gather.2
